TPU v7x, 32 devices: a whole 2x2x4 slice. The times are simulated.
32 devices in a mesh: parts: 2 (over x), seq: 16 (over z, y, core).
Axes of the slice: x: 2, y: 2, z: 4, core: 2. Of those that a mesh axis runs over, the one named last changes fastest.
Arguments:
- queries: bfloat16 [8192, 4096], P(('parts', 'seq')), parts along dimension 0, may hold values from -6 to 6
- keys: bfloat16 [8192, 256], P(('parts', 'seq')), parts along dimension 0, may hold values from -6 to 6
- values: bfloat16 [8192, 256], P(('parts', 'seq')), parts along dimension 0, may hold values from -6 to 6
- outputs: bfloat16 [8192, 4096], P(('parts', 'seq')), parts along dimension 0, may hold values from -0.59765625 to 0.59765625
- out_grad: bfloat16 [8192, 4096], P(('parts', 'seq')), parts along dimension 0, may hold values from -6 to 6
- logsumexp: float32 [32, 8192], P(None, ('parts', 'seq')), parts along dimension 1, may hold values from 4 to 7
- doc_lengths: int32 [32], P('parts'), parts along dimension 0, may hold values from 1 to 512, 4096 in all
Outputs:
- query_grad: bfloat16 [8192, 4096], P(('parts', 'seq')), parts along dimension 0
- key_grad: bfloat16 [8192, 256], P(('parts', 'seq')), parts along dimension 0
- value_grad: bfloat16 [8192, 256], P(('parts', 'seq')), parts along dimension 0
There are 2 independent parts, one for each index of `parts`. A program takes and returns all parts, laid end to end along the dimension named above; each array names one. Nothing has to cross between parts.
Inputs may be any that keep to these rules, and one draw needn't show every extreme that they name: `doc_lengths`: lengths of whole documents that fill the pack: they sum to 4096, and the longest has exactly 512 tokens.
All inputs are finite; a program needn't handle non-finite values.
Results may differ from a plain program's by a relative error of at most 0.0057.
Values may be sent and summed in bfloat16 or wider, within the bound.
No kernel may reach another device: no remote copies, remote signals or barrier semaphores. Data moves between devices by JAX's collectives and lax.ppermute only.
A program may use at most 64 MiB of HBM per device.

v0:
```python
import math

import jax
import jax.numpy as jnp
from jax import lax
from jax.sharding import PartitionSpec as P

H = 32
KVH = 2
HD = 128
REACH = 2


def shifted(block, axis, distance):
    devices = range(lax.axis_size(axis))
    route = [(i - distance, i) for i in devices if i - distance in devices]
    return lax.ppermute(block, axis, route)


def tile_grads(
    query_groups,
    grad_groups,
    delta_groups,
    lse_groups,
    key_tile,
    value_tile,
    query_ids,
    query_places,
    key_ids,
    key_places,
):
    kv_heads, tok_rows, group_size, head_dim = query_groups.shape
    key_rows = key_tile.shape[0]
    scaling = 1.0 / math.sqrt(head_dim)
    key_groups = jnp.moveaxis(key_tile.reshape(key_rows, kv_heads, head_dim), 1, 0)
    value_groups = jnp.moveaxis(value_tile.reshape(key_rows, kv_heads, head_dim), 1, 0)
    visible = (
        (query_ids[:, None] == key_ids[None, :])
        & (key_places[None, :] <= query_places[:, None])
        & (key_places[None, :] >= 0)
    )

    def one_group(pieces):
        query_one, key_one, value_one, grad_one, delta_one, lse_one = pieces
        scores = (
            jnp.einsum("qrd,kd->rqk", query_one, key_one, preferred_element_type=jnp.float32)
            * scaling
        )
        probs = jnp.where(visible[None], jnp.exp(scores - lse_one[:, :, None]), 0.0)
        probs_low = probs.astype(jnp.bfloat16)
        value_term = jnp.einsum(
            "rqk,qrd->kd", probs_low, grad_one, preferred_element_type=jnp.float32
        )
        prob_grad = jnp.einsum(
            "qrd,kd->rqk", grad_one, value_one, preferred_element_type=jnp.float32
        )
        score_low = (probs * (prob_grad - delta_one[:, :, None])).astype(jnp.bfloat16)
        query_term = (
            jnp.einsum("rqk,kd->qrd", score_low, key_one, preferred_element_type=jnp.float32)
            * scaling
        )
        key_term = (
            jnp.einsum("rqk,qrd->kd", score_low, query_one, preferred_element_type=jnp.float32)
            * scaling
        )
        return (query_term, key_term, value_term)

    query_part, key_part, value_part = lax.map(
        one_group, (query_groups, key_groups, value_groups, grad_groups, delta_groups, lse_groups)
    )
    return (
        jnp.moveaxis(query_part, 0, 1).reshape(tok_rows, -1),
        jnp.moveaxis(key_part, 0, 1).reshape(key_rows, -1),
        jnp.moveaxis(value_part, 0, 1).reshape(key_rows, -1),
    )


def per_device(queries, keys, values, outputs, out_grad, logsumexp, doc_lengths):
    tok_rows = queries.shape[0]
    group_size = H // KVH
    position = lax.axis_index("seq")
    doc_ends = jnp.cumsum(doc_lengths)

    def doc_of(places):
        return jnp.sum((doc_ends[None, :] <= places[:, None]).astype(jnp.int32), axis=1)

    query_places = position * tok_rows + jnp.arange(tok_rows, dtype=jnp.int32)
    query_ids = doc_of(query_places)
    query_groups = jnp.moveaxis(queries.reshape(tok_rows, KVH, group_size, HD), 1, 0)
    grad_groups = jnp.moveaxis(out_grad.reshape(tok_rows, KVH, group_size, HD), 1, 0)
    delta = jnp.sum(
        out_grad.astype(jnp.float32).reshape(tok_rows, KVH, group_size, HD)
        * outputs.astype(jnp.float32).reshape(tok_rows, KVH, group_size, HD),
        axis=3,
    )
    delta_groups = jnp.transpose(delta, (1, 2, 0))
    lse_groups = logsumexp.reshape(KVH, group_size, tok_rows)
    shared = (query_groups, grad_groups, delta_groups, lse_groups)
    key_tiles = [keys]
    value_tiles = [values]
    for hop in range(1, REACH + 1):
        moved = shifted((keys, values), "seq", hop)
        key_tiles.append(moved[0])
        value_tiles.append(moved[1])
    key_window = jnp.concatenate([key_tiles[hop] for hop in range(REACH, -1, -1)], axis=0)
    value_window = jnp.concatenate([value_tiles[hop] for hop in range(REACH, -1, -1)], axis=0)
    window_places = (position - REACH) * tok_rows + jnp.arange(
        (REACH + 1) * tok_rows, dtype=jnp.int32
    )
    query_total, key_window_grad, value_window_grad = tile_grads(
        *shared,
        key_window,
        value_window,
        query_ids,
        query_places,
        doc_of(window_places),
        window_places
    )
    key_grads = [
        key_window_grad[(REACH - hop) * tok_rows : (REACH - hop + 1) * tok_rows]
        for hop in range(REACH + 1)
    ]
    value_grads = [
        value_window_grad[(REACH - hop) * tok_rows : (REACH - hop + 1) * tok_rows]
        for hop in range(REACH + 1)
    ]
    key_total = key_grads[0]
    value_total = value_grads[0]
    for hop in range(1, REACH + 1):
        returned = shifted((key_grads[hop], value_grads[hop]), "seq", -hop)
        key_total = key_total + returned[0]
        value_total = value_total + returned[1]
    return (
        query_total.astype(jnp.bfloat16),
        key_total.astype(jnp.bfloat16),
        value_total.astype(jnp.bfloat16),
    )


def solution(mesh):
    in_specs = (
        P(("parts", "seq"), None),
        P(("parts", "seq"), None),
        P(("parts", "seq"), None),
        P(("parts", "seq"), None),
        P(("parts", "seq"), None),
        P(None, ("parts", "seq")),
        P("parts"),
    )
    out_specs = (P(("parts", "seq"), None), P(("parts", "seq"), None), P(("parts", "seq"), None))
    return jax.shard_map(
        per_device, mesh=mesh, in_specs=in_specs, out_specs=out_specs, check_vma=False
    )
```

profile of v0, /device:TPU:12, one launch (start us, length us, event | category | flops | bytes accessed | tf_op | source)
XLA Modules:
  0.0 109.0 jit_solution(16392103275962634925)
XLA Ops:
  0.6 1.8 %copy.71 = bf16[256,256]{0,1:T(8,128)(2,1)} copy(bf16[256,256]{1,0:T(8,128)(2,1)} %param.11) | data formatting | bytes 262144 | tf_op args[2]
  2.5 1.9 %collective-permute-start.3 = (bf16[256,256]{0,1:T(8,128)(2,1)}, bf16[256,256]{0,1:T(8,128)(2,1)}, u32[]{:S(2)}, u32[]{:S(2)}) collective-permute-start(bf16[256,256]{0,1:T(8,128)(2,1)} %copy.71), channel_id=1, source_target_pairs={{0,1},{1,2},{2,3},{3,4},{4,5},{5,6},{6,7},{7,8},{8,9},{9,10},{10,1... | collective-permute-start | bytes 393224 | tf_op jit(solution)/shard_map/ppermute | solution.py:17
  4.4 3.4 %collective-permute-start.2 = (bf16[256,256]{0,1:T(8,128)(2,1)}, bf16[256,256]{0,1:T(8,128)(2,1)}, u32[]{:S(2)}, u32[]{:S(2)}) collective-permute-start(bf16[256,256]{0,1:T(8,128)(2,1)} %copy.71), channel_id=1, source_target_pairs={{0,2},{1,3},{2,4},{3,5},{4,6},{5,7},{6,8},{7,9},{8,10},{9,11},{10,... | collective-permute-start | bytes 393224 | tf_op jit(solution)/shard_map/ppermute | solution.py:17
  7.8 1.7 %copy.67 = bf16[256,256]{0,1:T(8,128)(2,1)} copy(bf16[256,256]{1,0:T(8,128)(2,1)} %param.10) | data formatting | bytes 262144 | tf_op args[1]
  9.5 3.2 %collective-permute-start.1 = (bf16[256,256]{0,1:T(8,128)(2,1)}, bf16[256,256]{0,1:T(8,128)(2,1)}, u32[]{:S(2)}, u32[]{:S(2)}) collective-permute-start(bf16[256,256]{0,1:T(8,128)(2,1)} %copy.67), channel_id=1, source_target_pairs={{0,1},{1,2},{2,3},{3,4},{4,5},{5,6},{6,7},{7,8},{8,9},{9,10},{10,1... | collective-permute-start | bytes 393224 | tf_op jit(solution)/shard_map/ppermute | solution.py:17
  12.7 3.4 %collective-permute-start = (bf16[256,256]{0,1:T(8,128)(2,1)}, bf16[256,256]{0,1:T(8,128)(2,1)}, u32[]{:S(2)}, u32[]{:S(2)}) collective-permute-start(bf16[256,256]{0,1:T(8,128)(2,1)} %copy.67), channel_id=1, source_target_pairs={{0,2},{1,3},{2,4},{3,5},{4,6},{5,7},{6,8},{7,9},{8,10},{9,11},{10,... | collective-permute-start | bytes 393224 | tf_op jit(solution)/shard_map/ppermute | solution.py:17
  17.7 4.9 %multiply_bitcast_fusion = f32[32,8,32,128]{3,1,2,0:T(8,128)} fusion(bf16[256,4096]{1,0:T(8,128)(2,1)} %param.12, bf16[256,4096]{1,0:T(8,128)(2,1)} %param.13), kind=kLoop, calls=%fused_computation.42 | loop fusion | flops 3145728 | bytes 8388608
  24.5 2.5 %copy.74 = bf16[256,4096]{0,1:T(8,128)(2,1)} copy(bf16[256,4096]{1,0:T(8,128)(2,1)S(1)} %copy-done) | data formatting | bytes 4194304 | tf_op args[4]
  26.9 3.3 %copy.70 = bf16[256,4096]{0,1:T(8,128)(2,1)S(1)} copy(bf16[256,4096]{1,0:T(8,128)(2,1)} %param.9) | data formatting | bytes 4194304 | tf_op args[0]
  30.2 4.9 %copy.102 = f32[32,8,32,128]{3,2,1,0:T(8,128)} copy(f32[32,8,32,128]{3,1,2,0:T(8,128)} %multiply_bitcast_fusion) | data formatting | bytes 8388608
  35.1 3.5 %reduce_sum.29 = f32[256,2,16]{2,1,0:T(2,128)S(1)} reduce(f32[256,2,16,128]{3,2,1,0:T(8,128)} %bitcast.172, f32[]{:T(128)} %constant.24.clone.1), dimensions={3}, to_apply=%region_0.0 | reduce | flops 1040384 | bytes 4227076 | tf_op jit(solution)/shard_map/reduce_sum | solution.py:91
  39.3 1.8 %pad_maximum_fusion.1 = bf16[768,256]{0,1:T(8,128)(2,1)} fusion(bf16[256,256]{0,1:T(8,128)(2,1)} %copy.71, bf16[256,256]{0,1:T(8,128)(2,1)} %collective-permute-done.3, bf16[256,256]{0,1:T(8,128)(2,1)} %collective-permute-done.2), kind=kLoop, calls=%fused_computation.44 | loop fusion | flops 1179648 | bytes 786432 | tf_op jit(solution)/shard_map/concatenate | solution.py:106
  41.1 1.8 %pad_maximum_fusion = bf16[768,256]{0,1:T(8,128)(2,1)} fusion(bf16[256,256]{0,1:T(8,128)(2,1)} %copy.67, bf16[256,256]{0,1:T(8,128)(2,1)} %collective-permute-done.1, bf16[256,256]{0,1:T(8,128)(2,1)} %collective-permute-done), kind=kLoop, calls=%fused_computation.43 | loop fusion | flops 1179648 | bytes 786432 | tf_op jit(solution)/shard_map/concatenate | solution.py:105
  42.9 38.5 %while.15 = (s32[]{:T(128)}, bf16[2,256,16,128]{1,3,2,0:T(8,128)(2,1)}, f32[2,768,128]{2,1,0:T(8,128)}, f32[2,768,128]{2,1,0:T(8,128)}, bf16[2,768,128]{1,2,0:T(...) while((s32[]{:T(128)}, ...), condition=%wide.region_5.6_spmd.clone, body=%wide.region_4.5_spmd.clone.sunk | while | flops 4059398144 | bytes 90961936 | solution.py:68
  43.7 1.6 %and_and_fusion.2 = pred[256,768]{0,1:T(8,128)(4,1)S(1)} fusion(s32[256]{0:T(256)} %get-tuple-element.324, s32[256]{0:T(256)} %get-tuple-element.323, s32[768]{0:T(1024)S(1)} %get-tuple-element.325, s32[768]{0:T(1024)S(1)} %get-tuple-element.322, pred[768]{0:T(1024)(128)(4,1)} %get-tuple-element.326), kind=kLoop, calls=%fused_computation.26.clone.1 | loop fusion | flops 786432 | bytes 205568 | tf_op jit(solution)/shard_map/and | solution.py:38
  45.3 2.9 %fusion.71 = f32[768,256,16]{1,0,2:T(8,128)S(1)} fusion(bf16[2,256,16,128]{1,3,2,0:T(8,128)(2,1)S(1)} %get-tuple-element.317, s32[]{:T(128)S(6)} %copy.120, bf16[2,768,128]{1,2,0:T(8,128)(2,1)} %get-tuple-element.316), kind=kOutput, calls=%fused_computation.20.clone.1 | convolution fusion | flops 805306368 | bytes 13829120 | tf_op jit(solution)/shard_map/while/body/eval_jaxpr/qrd,kd->rqk/dot_general | solution.py:46
  48.2 2.9 %fusion.74 = f32[2,768,128]{2,1,0:T(8,128)} fusion(f32[2,768,128]{2,1,0:T(8,128)} %get-tuple-element.299, s32[]{:T(128)S(6)} %copy.120, f32[768,256,16]{1,0,2:T(8,128)S(1)} %fusion.71, f32[16,256]{1,0:T(8,128)S(1)} %get-tuple-element.279, pred[256,768]{0,1:T(8,128)(4,1)S(1)} %and_and_fusion.2, bf16[2,256,16,128]{1,3,2,0:T(8,128)(2,1)S(1)} %copy-done.2), kind=kOutput, calls=%fused_computation.12.clone.1 | convolution fusion | flops 817889280 | bytes 14238720 | tf_op jit(solution)/shard_map/while/body/eval_jaxpr/rqk,qrd->kd/dot_general | solution.py:51
  51.1 5.3 %fusion.72 = bf16[16,256,768]{1,2,0:T(8,128)(2,1)S(1)} fusion(f32[768,256,16]{1,0,2:T(8,128)S(1)} %fusion.71, f32[16,256]{1,0:T(8,128)S(1)} %get-tuple-element.278, f32[16,256]{1,0:T(8,128)S(1)} %get-tuple-element.279, pred[256,768]{0,1:T(8,128)(4,1)} %copy-done.1, bf16[2,256,16,128]{1,3,2,0:T(8,128)(2,1)} %get-tuple-element.320, s32[]{:T(128)S(6)} %copy.120, ...), kind=kOutput, calls=%fused_computation.3.clone.1 | convolution fusion | flops 824180736 | bytes 20349952 | tf_op jit(solution)/shard_map/while/body/eval_jaxpr/qrd,kd->rqk/dot_general | solution.py:54
  56.4 2.6 %fusion.73 = f32[2,768,128]{2,1,0:T(8,128)} fusion(f32[2,768,128]{2,1,0:T(8,128)} %get-tuple-element.298, s32[]{:T(128)S(6)} %copy.120, bf16[16,256,768]{1,2,0:T(8,128)(2,1)S(1)} %fusion.72, bf16[2,256,16,128]{1,3,2,0:T(8,128)(2,1)S(1)} %get-tuple-element.317), kind=kOutput, calls=%fused_computation.16.clone.1 | convolution fusion | flops 805404672 | bytes 7734272 | tf_op jit(solution)/shard_map/while/body/eval_jaxpr/rqk,qrd->kd/dot_general | solution.py:63
  58.9 1.9 %bitcast_dynamic-update-slice_fusion.2 = bf16[2,256,16,128]{1,3,2,0:T(8,128)(2,1)S(1)} fusion(bf16[2,256,16,128]{1,3,2,0:T(8,128)(2,1)S(1)} %copy-done.3, s32[]{:T(128)S(6)} %copy.120, bf16[16,256,768]{1,2,0:T(8,128)(2,1)S(1)} %fusion.72, bf16[2,768,128]{1,2,0:T(8,128)(2,1)} %get-tuple-element.316), kind=kOutput, calls=%fused_computation.10.clone.1 | convolution fusion | flops 805830656 | bytes 8586240 | tf_op jit(solution)/shard_map/while/body/eval_jaxpr/rqk,kd->qrd/dot_general | solution.py:59
  64.5 2.9 %fusion.71 = f32[768,256,16]{1,0,2:T(8,128)S(1)} fusion(bf16[2,256,16,128]{1,3,2,0:T(8,128)(2,1)S(1)} %get-tuple-element.317, s32[]{:T(128)S(6)} %copy.120, bf16[2,768,128]{1,2,0:T(8,128)(2,1)} %get-tuple-element.316), kind=kOutput, calls=%fused_computation.20.clone.1 | convolution fusion | flops 805306368 | bytes 13829120 | tf_op jit(solution)/shard_map/while/body/eval_jaxpr/qrd,kd->rqk/dot_general | solution.py:46
  67.4 2.9 %fusion.74 = f32[2,768,128]{2,1,0:T(8,128)} fusion(f32[2,768,128]{2,1,0:T(8,128)} %get-tuple-element.299, s32[]{:T(128)S(6)} %copy.120, f32[768,256,16]{1,0,2:T(8,128)S(1)} %fusion.71, f32[16,256]{1,0:T(8,128)S(1)} %get-tuple-element.279, pred[256,768]{0,1:T(8,128)(4,1)S(1)} %and_and_fusion.2, bf16[2,256,16,128]{1,3,2,0:T(8,128)(2,1)S(1)} %copy-done.2), kind=kOutput, calls=%fused_computation.12.clone.1 | convolution fusion | flops 817889280 | bytes 14238720 | tf_op jit(solution)/shard_map/while/body/eval_jaxpr/rqk,qrd->kd/dot_general | solution.py:51
  70.3 5.3 %fusion.72 = bf16[16,256,768]{1,2,0:T(8,128)(2,1)S(1)} fusion(f32[768,256,16]{1,0,2:T(8,128)S(1)} %fusion.71, f32[16,256]{1,0:T(8,128)S(1)} %get-tuple-element.278, f32[16,256]{1,0:T(8,128)S(1)} %get-tuple-element.279, pred[256,768]{0,1:T(8,128)(4,1)} %copy-done.1, bf16[2,256,16,128]{1,3,2,0:T(8,128)(2,1)} %get-tuple-element.320, s32[]{:T(128)S(6)} %copy.120, ...), kind=kOutput, calls=%fused_computation.3.clone.1 | convolution fusion | flops 824180736 | bytes 20349952 | tf_op jit(solution)/shard_map/while/body/eval_jaxpr/qrd,kd->rqk/dot_general | solution.py:54
  75.6 2.5 %fusion.73 = f32[2,768,128]{2,1,0:T(8,128)} fusion(f32[2,768,128]{2,1,0:T(8,128)} %get-tuple-element.298, s32[]{:T(128)S(6)} %copy.120, bf16[16,256,768]{1,2,0:T(8,128)(2,1)S(1)} %fusion.72, bf16[2,256,16,128]{1,3,2,0:T(8,128)(2,1)S(1)} %get-tuple-element.317), kind=kOutput, calls=%fused_computation.16.clone.1 | convolution fusion | flops 805404672 | bytes 7734272 | tf_op jit(solution)/shard_map/while/body/eval_jaxpr/rqk,qrd->kd/dot_general | solution.py:63
  78.2 1.9 %bitcast_dynamic-update-slice_fusion.2 = bf16[2,256,16,128]{1,3,2,0:T(8,128)(2,1)S(1)} fusion(bf16[2,256,16,128]{1,3,2,0:T(8,128)(2,1)S(1)} %copy-done.3, s32[]{:T(128)S(6)} %copy.120, bf16[16,256,768]{1,2,0:T(8,128)(2,1)S(1)} %fusion.72, bf16[2,768,128]{1,2,0:T(8,128)(2,1)} %get-tuple-element.316), kind=kOutput, calls=%fused_computation.10.clone.1 | convolution fusion | flops 805830656 | bytes 8586240 | tf_op jit(solution)/shard_map/while/body/eval_jaxpr/rqk,kd->qrd/dot_general | solution.py:59
  84.2 2.0 %collective-permute-start.6 = (f32[256,256]{1,0:T(8,128)}, f32[256,256]{1,0:T(8,128)S(1)}, u32[]{:S(2)}, u32[]{:S(2)}) collective-permute-start(f32[256,256]{1,0:T(8,128)} %bitcast.134), channel_id=1, source_target_pairs={{1,0},{2,1},{3,2},{4,3},{5,4},{6,5},{7,6},{8,7},{9,8},{10,9},{11,1... | collective-permute-start | bytes 786440 | tf_op jit(solution)/shard_map/ppermute | solution.py:17
  86.2 3.3 %collective-permute-start.7 = (f32[256,256]{1,0:T(8,128)}, f32[256,256]{1,0:T(8,128)S(1)}, u32[]{:S(2)}, u32[]{:S(2)}) collective-permute-start(f32[256,256]{1,0:T(8,128)} %bitcast.133), channel_id=1, source_target_pairs={{2,0},{3,1},{4,2},{5,3},{6,4},{7,5},{8,6},{9,7},{10,8},{11,9},{12,... | collective-permute-start | bytes 786440 | tf_op jit(solution)/shard_map/ppermute | solution.py:17
  92.1 2.1 %collective-permute-start.4 = (f32[256,256]{1,0:T(8,128)}, f32[256,256]{1,0:T(8,128)S(1)}, u32[]{:S(2)}, u32[]{:S(2)}) collective-permute-start(f32[256,256]{1,0:T(8,128)} %bitcast.136), channel_id=1, source_target_pairs={{1,0},{2,1},{3,2},{4,3},{5,4},{6,5},{7,6},{8,7},{9,8},{10,9},{11,1... | collective-permute-start | bytes 786440 | tf_op jit(solution)/shard_map/ppermute | solution.py:17
  94.3 3.1 %collective-permute-start.5 = (f32[256,256]{1,0:T(8,128)}, f32[256,256]{1,0:T(8,128)}, u32[]{:S(2)}, u32[]{:S(2)}) collective-permute-start(f32[256,256]{1,0:T(8,128)} %bitcast.135), channel_id=1, source_target_pairs={{2,0},{3,1},{4,2},{5,3},{6,4},{7,5},{8,6},{9,7},{10,8},{11,9},{12,... | collective-permute-start | bytes 786440 | tf_op jit(solution)/shard_map/ppermute | solution.py:17
  97.3 2.9 %copy.90 = bf16[256,4096]{1,0:T(8,128)(2,1)} copy(bf16[256,4096]{0,1:T(8,128)(2,1)S(1)} %bitcast.174) | data formatting | bytes 4194304 | tf_op jit(solution)/shard_map/convert_element_type | solution.py:134
  100.9 6.4 %collective-permute-done.5 = f32[256,256]{1,0:T(8,128)} collective-permute-done((f32[256,256]{1,0:T(8,128)}, f32[256,256]{1,0:T(8,128)}, u32[]{:S(2)}, u32[]{:S(2)}) %collective-permute-start.5) | collective-permute-done | bytes 262176 | tf_op jit(solution)/shard_map/ppermute | solution.py:17
  107.3 1.6 %fusion.44 = bf16[256,256]{1,0:T(8,128)(2,1)} fusion(f32[256,256]{1,0:T(8,128)} %collective-permute-done.5, f32[256,256]{1,0:T(8,128)S(1)} %collective-permute-done.4, f32[2,32,8,128]{3,2,1,0:T(8,128)S(1)} %get-tuple-element.182), kind=kLoop, calls=%fused_computation.54 | loop fusion | flops 196608 | bytes 917504 | tf_op jit(solution)/shard_map/convert_element_type | solution.py:135
  (49 shorter events, 15.8 us)
Async XLA Ops:
  0.6 23.8 %copy-start = (bf16[256,4096]{1,0:T(8,128)(2,1)S(1)}, bf16[256,4096]{1,0:T(8,128)(2,1)}, u32[]{:S(2)}) copy-start(bf16[256,4096]{1,0:T(8,128)(2,1)} %param.13) | copy-start | bytes 6291460
  2.5 36.9 %collective-permute-start.3 = (bf16[256,256]{0,1:T(8,128)(2,1)}, bf16[256,256]{0,1:T(8,128)(2,1)}, u32[]{:S(2)}, u32[]{:S(2)}) collective-permute-start(bf16[256,256]{0,1:T(8,128)(2,1)} %copy.71), channel_id=1, source_target_pairs={{0,1},{1,2},{2,3},{3,4},{4,5},{5,6},{6,7},{7,8},{8,9},{9,10},{10,1... | collective-permute-start | bytes 393224 | tf_op jit(solution)/shard_map/ppermute | solution.py:17
  4.4 35.0 %collective-permute-start.2 = (bf16[256,256]{0,1:T(8,128)(2,1)}, bf16[256,256]{0,1:T(8,128)(2,1)}, u32[]{:S(2)}, u32[]{:S(2)}) collective-permute-start(bf16[256,256]{0,1:T(8,128)(2,1)} %copy.71), channel_id=1, source_target_pairs={{0,2},{1,3},{2,4},{3,5},{4,6},{5,7},{6,8},{7,9},{8,10},{9,11},{10,... | collective-permute-start | bytes 393224 | tf_op jit(solution)/shard_map/ppermute | solution.py:17
  9.5 31.7 %collective-permute-start.1 = (bf16[256,256]{0,1:T(8,128)(2,1)}, bf16[256,256]{0,1:T(8,128)(2,1)}, u32[]{:S(2)}, u32[]{:S(2)}) collective-permute-start(bf16[256,256]{0,1:T(8,128)(2,1)} %copy.67), channel_id=1, source_target_pairs={{0,1},{1,2},{2,3},{3,4},{4,5},{5,6},{6,7},{7,8},{8,9},{9,10},{10,1... | collective-permute-start | bytes 393224 | tf_op jit(solution)/shard_map/ppermute | solution.py:17
  12.7 28.4 %collective-permute-start = (bf16[256,256]{0,1:T(8,128)(2,1)}, bf16[256,256]{0,1:T(8,128)(2,1)}, u32[]{:S(2)}, u32[]{:S(2)}) collective-permute-start(bf16[256,256]{0,1:T(8,128)(2,1)} %copy.67), channel_id=1, source_target_pairs={{0,2},{1,3},{2,4},{3,5},{4,6},{5,7},{6,8},{7,9},{8,10},{9,11},{10,... | collective-permute-start | bytes 393224 | tf_op jit(solution)/shard_map/ppermute | solution.py:17
  45.3 2.9 %copy-start.1 = (pred[256,768]{0,1:T(8,128)(4,1)}, pred[256,768]{0,1:T(8,128)(4,1)S(1)}, u32[]{:S(2)}) copy-start(pred[256,768]{0,1:T(8,128)(4,1)S(1)} %and_and_fusion.2) | copy-start | bytes 589828 | tf_op jit(solution)/shard_map/while
  45.3 2.9 %copy-start.2 = (bf16[2,256,16,128]{1,3,2,0:T(8,128)(2,1)S(1)}, bf16[2,256,16,128]{1,3,2,0:T(8,128)(2,1)}, u32[]{:S(2)}) copy-start(bf16[2,256,16,128]{1,3,2,0:T(8,128)(2,1)} %get-tuple-element.320) | copy-start | bytes 6291460 | tf_op jit(solution)/shard_map/while
  56.4 2.6 %copy-start.3 = (bf16[2,256,16,128]{1,3,2,0:T(8,128)(2,1)S(1)}, bf16[2,256,16,128]{1,3,2,0:T(8,128)(2,1)}, u32[]{:S(2)}) copy-start(bf16[2,256,16,128]{1,3,2,0:T(8,128)(2,1)} %get-tuple-element.297) | copy-start | bytes 6291460 | tf_op jit(solution)/shard_map/while
  60.9 1.3 %copy-start.4 = (bf16[2,256,16,128]{1,3,2,0:T(8,128)(2,1)}, bf16[2,256,16,128]{1,3,2,0:T(8,128)(2,1)S(1)}, u32[]{:S(2)}) copy-start(bf16[2,256,16,128]{1,3,2,0:T(8,128)(2,1)S(1)} %bitcast_dynamic-update-slice_fusion.2) | copy-start | bytes 6291460 | tf_op jit(solution)/shard_map/while
  64.5 2.9 %copy-start.1 = (pred[256,768]{0,1:T(8,128)(4,1)}, pred[256,768]{0,1:T(8,128)(4,1)S(1)}, u32[]{:S(2)}) copy-start(pred[256,768]{0,1:T(8,128)(4,1)S(1)} %and_and_fusion.2) | copy-start | bytes 589828 | tf_op jit(solution)/shard_map/while
  64.5 2.9 %copy-start.2 = (bf16[2,256,16,128]{1,3,2,0:T(8,128)(2,1)S(1)}, bf16[2,256,16,128]{1,3,2,0:T(8,128)(2,1)}, u32[]{:S(2)}) copy-start(bf16[2,256,16,128]{1,3,2,0:T(8,128)(2,1)} %get-tuple-element.320) | copy-start | bytes 6291460 | tf_op jit(solution)/shard_map/while
  75.6 2.6 %copy-start.3 = (bf16[2,256,16,128]{1,3,2,0:T(8,128)(2,1)S(1)}, bf16[2,256,16,128]{1,3,2,0:T(8,128)(2,1)}, u32[]{:S(2)}) copy-start(bf16[2,256,16,128]{1,3,2,0:T(8,128)(2,1)} %get-tuple-element.297) | copy-start | bytes 6291460 | tf_op jit(solution)/shard_map/while
  80.1 1.3 %copy-start.4 = (bf16[2,256,16,128]{1,3,2,0:T(8,128)(2,1)}, bf16[2,256,16,128]{1,3,2,0:T(8,128)(2,1)S(1)}, u32[]{:S(2)}) copy-start(bf16[2,256,16,128]{1,3,2,0:T(8,128)(2,1)S(1)} %bitcast_dynamic-update-slice_fusion.2) | copy-start | bytes 6291460 | tf_op jit(solution)/shard_map/while
  81.5 15.9 %copy-start.5 = (bf16[2,256,16,128]{1,3,2,0:T(8,128)(2,1)S(1)}, bf16[2,256,16,128]{1,3,2,0:T(8,128)(2,1)}, u32[]{:S(2)}) copy-start(bf16[2,256,16,128]{1,3,2,0:T(8,128)(2,1)} %get-tuple-element.62) | copy-start | bytes 6291460
  84.2 16.0 %collective-permute-start.6 = (f32[256,256]{1,0:T(8,128)}, f32[256,256]{1,0:T(8,128)S(1)}, u32[]{:S(2)}, u32[]{:S(2)}) collective-permute-start(f32[256,256]{1,0:T(8,128)} %bitcast.134), channel_id=1, source_target_pairs={{1,0},{2,1},{3,2},{4,3},{5,4},{6,5},{7,6},{8,7},{9,8},{10,9},{11,1... | collective-permute-start | bytes 786440 | tf_op jit(solution)/shard_map/ppermute | solution.py:17
  86.2 14.0 %collective-permute-start.7 = (f32[256,256]{1,0:T(8,128)}, f32[256,256]{1,0:T(8,128)S(1)}, u32[]{:S(2)}, u32[]{:S(2)}) collective-permute-start(f32[256,256]{1,0:T(8,128)} %bitcast.133), channel_id=1, source_target_pairs={{2,0},{3,1},{4,2},{5,3},{6,4},{7,5},{8,6},{9,7},{10,8},{11,9},{12,... | collective-permute-start | bytes 786440 | tf_op jit(solution)/shard_map/ppermute | solution.py:17
  92.1 8.8 %collective-permute-start.4 = (f32[256,256]{1,0:T(8,128)}, f32[256,256]{1,0:T(8,128)S(1)}, u32[]{:S(2)}, u32[]{:S(2)}) collective-permute-start(f32[256,256]{1,0:T(8,128)} %bitcast.136), channel_id=1, source_target_pairs={{1,0},{2,1},{3,2},{4,3},{5,4},{6,5},{7,6},{8,7},{9,8},{10,9},{11,1... | collective-permute-start | bytes 786440 | tf_op jit(solution)/shard_map/ppermute | solution.py:17
  94.3 13.1 %collective-permute-start.5 = (f32[256,256]{1,0:T(8,128)}, f32[256,256]{1,0:T(8,128)}, u32[]{:S(2)}, u32[]{:S(2)}) collective-permute-start(f32[256,256]{1,0:T(8,128)} %bitcast.135), channel_id=1, source_target_pairs={{2,0},{3,1},{4,2},{5,3},{6,4},{7,5},{8,6},{9,7},{10,8},{11,9},{12,... | collective-permute-start | bytes 786440 | tf_op jit(solution)/shard_map/ppermute | solution.py:17
where the time goes:
time: 111 us; the launch traced here: 109 us
  matrix products  31.1 us (28%)
  local copies, waits for them, and re-layouts  27.9 us (25%)
  starting transfers between devices  22.5 us (20%)
  other arithmetic  20.1 us (18%)
  waiting for transfers between devices  6.44 us (6%)
    ppermute x8, starting transfers between devices, shifted(): return lax.ppermute(block, axis, route)  22.5 us
    unnamed x12, local copies, waits for them, and re-layouts  17.3 us
    dot_general x2, matrix products, one_group(): jnp.einsum('qrd,kd->rqk', grad_one, value_one, preferred_element_type=jnp...  10.5 us
    ppermute x8, waiting for transfers between devices, shifted(): return lax.ppermute(block, axis, route)  6.44 us
    dot_general x2, matrix products, one_group(): jnp.einsum('rqk,qrd->kd', probs_low, grad_one, preferred_element_type=jnp...  5.8 us
    dot_general x2, matrix products, one_group(): jnp.einsum('qrd,kd->rqk', query_one, key_one, preferred_element_type=jnp....  5.79 us
    dot_general x2, matrix products, one_group(): jnp.einsum('rqk,qrd->kd', score_low, query_one, preferred_element_type=jn...  5.1 us
    unnamed x1, other arithmetic  4.89 us
  transfers between devices with their start and end apart: 8, of which 1 were waited for; matrix products, arithmetic and copies ran while one was open for 30% of the time, Pallas kernels for 0%

commit v1 on v0

v1 whole, which is shorter than its diff:
```python
import math

import jax
import jax.numpy as jnp
from jax import lax
from jax.experimental import pallas as pl
from jax.experimental.pallas import tpu as pltpu
from jax.sharding import PartitionSpec as P

HD = 128
MOST = 512
KEY_TILE = 128
HEADS_PER_STEP = 4
NT_DIMS = (((1,), (1,)), ((), ()))


def shifted(block, axis, distance):
    devices = range(lax.axis_size(axis))
    route = [(i - distance, i) for i in devices if i - distance in devices]
    return lax.ppermute(block, axis, route)


def make_kernel(heads_per_group, tok, win, diag_tile):
    blocks_per_group = heads_per_group // HEADS_PER_STEP
    n_tiles = win // KEY_TILE
    scale = 1.0 / math.sqrt(HD)

    def kernel(flags_ref, q_ref, do_ref, lse_ref, delta_ref, k_ref, v_ref, kt_ref, bias_ref,
               dq_ref, dk_ref, dv_ref, dqt_scr):
        g = pl.program_id(0)
        b = pl.program_id(1)

        @pl.when(b == 0)
        def _():
            dk_ref[...] = jnp.zeros_like(dk_ref)
            dv_ref[...] = jnp.zeros_like(dv_ref)

        for i in range(HEADS_PER_STEP):
            h = (g * blocks_per_group + b) * HEADS_PER_STEP + i
            cols = slice(i * HD, (i + 1) * HD)
            q = q_ref[:, cols]
            do = do_ref[:, cols]
            lse = lse_ref[pl.ds(h, 1), :]
            dl = delta_ref[pl.ds(h, 1), :]
            dqt_scr[...] = jnp.zeros_like(dqt_scr)

            for j in range(n_tiles):
                def tile(j=j, q=q, do=do, lse=lse, dl=dl):
                    rows = slice(j * KEY_TILE, (j + 1) * KEY_TILE)
                    k = k_ref[rows, :]
                    v = v_ref[rows, :]
                    st = lax.dot_general(k, q, NT_DIMS, preferred_element_type=jnp.float32)
                    p = jnp.exp(st * scale - lse + bias_ref[rows, :])
                    dv_ref[rows, :] += jnp.dot(
                        p.astype(jnp.bfloat16), do, preferred_element_type=jnp.float32)
                    dpt = lax.dot_general(v, do, NT_DIMS, preferred_element_type=jnp.float32)
                    ds = (p * (dpt - dl)).astype(jnp.bfloat16)
                    dk_ref[rows, :] += jnp.dot(ds, q, preferred_element_type=jnp.float32)
                    dqt_scr[...] += jnp.dot(
                        kt_ref[:, rows], ds, preferred_element_type=jnp.float32)

                if j >= diag_tile:
                    tile()
                else:
                    pl.when(flags_ref[j] != 0)(tile)

            dq_ref[:, cols] = (dqt_scr[...] * scale).T.astype(dq_ref.dtype)

    return kernel


def grads_kernel(flags, queries, out_grad, lse, delta, key_win, value_win, key_win_t, bias):
    tok, width = queries.shape
    win, kv_width = key_win.shape
    n_heads = width // HD
    kvh = kv_width // HD
    heads_per_group = n_heads // kvh
    blocks_per_group = heads_per_group // HEADS_PER_STEP
    diag_tile = (win - tok) // KEY_TILE
    kernel = make_kernel(heads_per_group, tok, win, diag_tile)
    hb = HEADS_PER_STEP * HD

    def head_block(g, b, flags_ref):
        return (0, g * blocks_per_group + b)

    def full(g, b, flags_ref):
        return (0, 0)

    def group_cols(g, b, flags_ref):
        return (0, g)

    def group_rows(g, b, flags_ref):
        return (g, 0)

    grid_spec = pltpu.PrefetchScalarGridSpec(
        num_scalar_prefetch=1,
        grid=(kvh, blocks_per_group),
        in_specs=[
            pl.BlockSpec((tok, hb), head_block),
            pl.BlockSpec((tok, hb), head_block),
            pl.BlockSpec((n_heads, tok), full),
            pl.BlockSpec((n_heads, tok), full),
            pl.BlockSpec((win, HD), group_cols),
            pl.BlockSpec((win, HD), group_cols),
            pl.BlockSpec((HD, win), group_rows),
            pl.BlockSpec((win, tok), full),
        ],
        out_specs=[
            pl.BlockSpec((tok, hb), head_block),
            pl.BlockSpec((win, HD), group_cols),
            pl.BlockSpec((win, HD), group_cols),
        ],
        scratch_shapes=[pltpu.VMEM((HD, tok), jnp.float32)],
    )
    return pl.pallas_call(
        kernel,
        grid_spec=grid_spec,
        out_shape=[
            jax.ShapeDtypeStruct((tok, width), jnp.bfloat16),
            jax.ShapeDtypeStruct((win, kv_width), jnp.float32),
            jax.ShapeDtypeStruct((win, kv_width), jnp.float32),
        ],
        compiler_params=pltpu.CompilerParams(
            dimension_semantics=("arbitrary", "arbitrary")),
    )(flags, queries, out_grad, lse, delta, key_win, value_win, key_win_t, bias)


def per_device(queries, keys, values, outputs, out_grad, logsumexp, doc_lengths):
    tok, width = queries.shape
    n_heads = width // HD
    reach = -(-(MOST - 1) // tok)
    win = (reach + 1) * tok
    scale = 1.0 / math.sqrt(HD)
    position = lax.axis_index("seq")
    doc_ends = jnp.cumsum(doc_lengths)

    def doc_of(places):
        return jnp.sum((doc_ends[None, :] <= places[:, None]).astype(jnp.int32), axis=1)

    query_places = position * tok + jnp.arange(tok, dtype=jnp.int32)
    query_ids = doc_of(query_places)
    key_places = (position - reach) * tok + jnp.arange(win, dtype=jnp.int32)
    key_ids = jnp.where(key_places >= 0, doc_of(key_places), -1)
    visible = (key_ids[:, None] == query_ids[None, :]) & (
        key_places[:, None] <= query_places[None, :])
    bias = jnp.where(visible, 0.0, -jnp.inf).astype(jnp.float32)
    n_tiles = win // KEY_TILE
    last_ids = key_ids[KEY_TILE - 1::KEY_TILE]
    diag_tile = (win - tok) // KEY_TILE
    flags = ((last_ids == query_ids[0])
             | (jnp.arange(n_tiles) >= diag_tile)).astype(jnp.int32)

    delta = jnp.sum(
        (out_grad.astype(jnp.float32) * outputs.astype(jnp.float32)).reshape(tok, n_heads, HD),
        axis=2,
    ).T

    key_tiles = [keys]
    value_tiles = [values]
    for hop in range(1, reach + 1):
        moved = shifted((keys, values), "seq", hop)
        key_tiles.append(moved[0])
        value_tiles.append(moved[1])
    key_win = jnp.concatenate(key_tiles[::-1], axis=0)
    value_win = jnp.concatenate(value_tiles[::-1], axis=0)
    key_win_t = key_win.T

    dq, dk_win, dv_win = grads_kernel(
        flags, queries, out_grad, logsumexp, delta, key_win, value_win, key_win_t, bias)

    def piece(arr, hop):
        return arr[(reach - hop) * tok:(reach - hop + 1) * tok]

    key_total = piece(dk_win, 0)
    value_total = piece(dv_win, 0)
    for hop in range(1, reach + 1):
        returned = shifted((piece(dk_win, hop), piece(dv_win, hop)), "seq", -hop)
        key_total = key_total + returned[0]
        value_total = value_total + returned[1]
    return (
        dq,
        (key_total * scale).astype(jnp.bfloat16),
        value_total.astype(jnp.bfloat16),
    )


def solution(mesh):
    in_specs = (
        P(("parts", "seq"), None),
        P(("parts", "seq"), None),
        P(("parts", "seq"), None),
        P(("parts", "seq"), None),
        P(("parts", "seq"), None),
        P(None, ("parts", "seq")),
        P("parts"),
    )
    out_specs = (P(("parts", "seq"), None), P(("parts", "seq"), None), P(("parts", "seq"), None))
    return jax.shard_map(
        per_device, mesh=mesh, in_specs=in_specs, out_specs=out_specs, check_vma=False
    )
```

time: 111 us -> 144 us (1.30)
  the two profiles are of different devices: /device:TPU:12 before, /device:TPU:13 now
where the time goes in v1:
time: 144 us
  starting transfers between devices  67.4 us (47%)
  Pallas kernels  44.7 us (31%)
  other arithmetic  13.9 us (10%)
  local copies, waits for them, and re-layouts  8.78 us (6%)
  waiting for transfers between devices  8.11 us (6%)
    ppermute x8, starting transfers between devices, shifted(): return lax.ppermute(block, axis, route)  67.4 us
    pallas_call x1, Pallas kernels, grads_kernel(): pl.pallas_call(kernel, grid_spec=grid_spec, out_shape=[jax.ShapeDtypeStru...  44.7 us
    ppermute x8, waiting for transfers between devices, shifted(): return lax.ppermute(block, axis, route)  8.11 us
    unnamed x4, local copies, waits for them, and re-layouts  3.67 us
    reduce_sum x1, other arithmetic, per_device(): jnp.sum((out_grad.astype(jnp.float32) * outputs.astype(jnp.float32)).resh...  3.34 us
    unnamed x1, other arithmetic  2.94 us
  transfers between devices with their start and end apart: 8, of which 2 were waited for; matrix products, arithmetic and copies ran while one was open for 13% of the time, Pallas kernels for 0%

profile of v1, /device:TPU:13, one launch (start us, length us, event | category | flops | bytes accessed | tf_op | source)
XLA Modules:
  0.0 143.6 jit_solution(15281677917480702013)
XLA Ops:
  0.6 1.0 copy.28
  1.6 3.7 %collective-permute-start.1 = (bf16[256,256]{0,1:T(8,128)(2,1)S(1)}, bf16[256,256]{0,1:T(8,128)(2,1)S(1)}, u32[]{:S(2)}, u32[]{:S(2)}) collective-permute-start(bf16[256,256]{0,1:T(8,128)(2,1)S(1)} %copy.28), channel_id=1, source_target_pairs={{0,1},{1,2},{2,3},{3,4},{4,5},{5,6},{6,7},{7,8},{8,9},{9,10},{10,1... | collective-permute-start | bytes 393224 | tf_op jit(solution)/shard_map/ppermute | solution.py:20
  5.4 3.1 %collective-permute-start = (bf16[256,256]{0,1:T(8,128)(2,1)S(1)}, bf16[256,256]{0,1:T(8,128)(2,1)S(1)}, u32[]{:S(2)}, u32[]{:S(2)}) collective-permute-start(bf16[256,256]{0,1:T(8,128)(2,1)S(1)} %copy.28), channel_id=1, source_target_pairs={{0,2},{1,3},{2,4},{3,5},{4,6},{5,7},{6,8},{7,9},{8,10},{9,11},{10,... | collective-permute-start | bytes 393224 | tf_op jit(solution)/shard_map/ppermute | solution.py:20
  8.5 2.2 %collective-permute-start.3 = (bf16[256,256]{1,0:T(8,128)(2,1)}, bf16[256,256]{1,0:T(8,128)(2,1)S(1)}, u32[]{:S(2)}, u32[]{:S(2)}) collective-permute-start(bf16[256,256]{1,0:T(8,128)(2,1)} %param.9), channel_id=1, source_target_pairs={{0,1},{1,2},{2,3},{3,4},{4,5},{5,6},{6,7},{7,8},{8,9},{9,10},{10,1... | collective-permute-start | bytes 393224 | tf_op jit(solution)/shard_map/ppermute | solution.py:20
  10.7 3.1 %collective-permute-start.2 = (bf16[256,256]{1,0:T(8,128)(2,1)}, bf16[256,256]{1,0:T(8,128)(2,1)S(1)}, u32[]{:S(2)}, u32[]{:S(2)}) collective-permute-start(bf16[256,256]{1,0:T(8,128)(2,1)} %param.9), channel_id=1, source_target_pairs={{0,2},{1,3},{2,4},{3,5},{4,6},{5,7},{6,8},{7,9},{8,10},{9,11},{10,... | collective-permute-start | bytes 393224 | tf_op jit(solution)/shard_map/ppermute | solution.py:20
  13.9 0.7 copy.26
  14.7 0.1 reduce
  14.8 0.1 convert_reduce_fusion
  14.9 0.1 slice.24
  15.0 0.1 convert_reduce_fusion.1
  15.1 0.5 slice.25
  15.6 1.1 and_select_fusion.bias_ref
  16.7 2.9 %multiply_bitcast_fusion = f32[32,8,32,128]{3,1,2,0:T(8,128)S(1)} fusion(bf16[256,4096]{1,0:T(8,128)(2,1)} %param.10, bf16[256,4096]{1,0:T(8,128)(2,1)} %do_ref.1), kind=kLoop, calls=%fused_computation | loop fusion | flops 3145728 | bytes 8388608
  19.7 2.7 %copy.32 = f32[32,8,32,128]{3,2,1,0:T(8,128)} copy(f32[32,8,32,128]{3,1,2,0:T(8,128)S(1)} %multiply_bitcast_fusion) | data formatting | bytes 8388608
  22.4 3.3 %reduce_sum.29 = f32[256,32]{1,0:T(8,128)S(1)} reduce(f32[256,32,128]{2,1,0:T(8,128)} %bitcast.8, f32[]{:T(128)} %constant.7.clone.1), dimensions={2}, to_apply=%region_3.4 | reduce | flops 1040384 | bytes 4227076 | tf_op jit(solution)/shard_map/reduce_sum | solution.py:153
  25.7 0.0 copy-start
  25.7 0.7 copy.27
  26.4 1.2 or_convert_fusion.flags_ref
  27.6 0.8 fusion
  28.4 0.9 copy.31.k_ref
  29.4 0.8 pad_maximum_fusion.1.v_ref
  30.2 44.7 %shard_map.94 = (bf16[256,4096]{1,0:T(8,128)(2,1)}, f32[768,256]{1,0:T(8,128)}, f32[768,256]{1,0:T(8,128)}) custom-call(s32[6]{0:T(128)} %or_convert_fusion.flags_ref, bf16[256,4096]{1,0:T(8,128)(2,1)} %q_ref.1, bf16[256,4096]{1,0:T(8,128)(2,1)} %do_ref.1, f32[32,256]{1,0:T(8,128)} %lse_ref.1, f32[32,256]{1,0:T(8,128)} %bitcast.9, ...), custom_call_target="tpu_custom_call" | custom-call | tf_op jit(solution)/shard_map/pallas_call | solution.py:115
  74.8 1.1 fusion.2
  75.9 2.1 %collective-permute-start.5 = (f32[256,256]{1,0:T(8,128)S(1)}, f32[256,256]{1,0:T(8,128)S(1)}, u32[]{:S(2)}, u32[]{:S(2)}) collective-permute-start(f32[256,256]{1,0:T(8,128)S(1)} %get-tuple-element.12), channel_id=1, source_target_pairs={{2,0},{3,1},{4,2},{5,3},{6,4},{7,5},{8,6},{9,7},{10,8},{11,9},{12,... | collective-permute-start | bytes 786440 | tf_op jit(solution)/shard_map/ppermute | solution.py:20
  78.1 49.2 %collective-permute-start.4 = (f32[256,256]{1,0:T(8,128)S(1)}, f32[256,256]{1,0:T(8,128)S(1)}, u32[]{:S(2)}, u32[]{:S(2)}) collective-permute-start(f32[256,256]{1,0:T(8,128)S(1)} %get-tuple-element.11), channel_id=1, source_target_pairs={{1,0},{2,1},{3,2},{4,3},{5,4},{6,5},{7,6},{8,7},{9,8},{10,9},{11,1... | collective-permute-start | bytes 786440 | tf_op jit(solution)/shard_map/ppermute | solution.py:20
  127.2 1.1 fusion.1
  128.3 1.9 %collective-permute-start.7 = (f32[256,256]{1,0:T(8,128)S(1)}, f32[256,256]{1,0:T(8,128)S(1)}, u32[]{:S(2)}, u32[]{:S(2)}) collective-permute-start(f32[256,256]{1,0:T(8,128)S(1)} %get-tuple-element.10), channel_id=1, source_target_pairs={{2,0},{3,1},{4,2},{5,3},{6,4},{7,5},{8,6},{9,7},{10,8},{11,9},{12,... | collective-permute-start | bytes 786440 | tf_op jit(solution)/shard_map/ppermute | solution.py:20
  130.2 1.9 %collective-permute-start.6 = (f32[256,256]{1,0:T(8,128)S(1)}, f32[256,256]{1,0:T(8,128)S(1)}, u32[]{:S(2)}, u32[]{:S(2)}) collective-permute-start(f32[256,256]{1,0:T(8,128)S(1)} %get-tuple-element.9), channel_id=1, source_target_pairs={{1,0},{2,1},{3,2},{4,3},{5,4},{6,5},{7,6},{8,7},{9,8},{10,9},{11,1... | collective-permute-start | bytes 786440 | tf_op jit(solution)/shard_map/ppermute | solution.py:20
  132.2 1.7 %multiply_convert_fusion = bf16[256,256]{1,0:T(8,128)(2,1)} fusion(f32[256,256]{1,0:T(8,128)S(1)} %collective-permute-done.5, f32[256,256]{1,0:T(8,128)S(1)} %collective-permute-done.4, f32[768,256]{1,0:T(8,128)} %get-tuple-element.7), kind=kLoop, calls=%fused_computation.5 | loop fusion | flops 262144 | bytes 917504 | tf_op jit(solution)/shard_map/convert_element_type | solution.py:182
  133.8 5.2 %collective-permute-done.7 = f32[256,256]{1,0:T(8,128)S(1)} collective-permute-done((f32[256,256]{1,0:T(8,128)S(1)}, f32[256,256]{1,0:T(8,128)S(1)}, u32[]{:S(2)}, u32[]{:S(2)}) %collective-permute-start.7) | collective-permute-done | bytes 262176 | tf_op jit(solution)/shard_map/ppermute | solution.py:20
  139.0 2.9 %collective-permute-done.6 = f32[256,256]{1,0:T(8,128)S(1)} collective-permute-done((f32[256,256]{1,0:T(8,128)S(1)}, f32[256,256]{1,0:T(8,128)S(1)}, u32[]{:S(2)}, u32[]{:S(2)}) %collective-permute-start.6) | collective-permute-done | bytes 262176 | tf_op jit(solution)/shard_map/ppermute | solution.py:20
  141.9 1.7 %add_convert_fusion = bf16[256,256]{1,0:T(8,128)(2,1)} fusion(f32[256,256]{1,0:T(8,128)S(1)} %collective-permute-done.7, f32[256,256]{1,0:T(8,128)S(1)} %collective-permute-done.6, f32[768,256]{1,0:T(8,128)} %get-tuple-element.8), kind=kLoop, calls=%fused_computation.4 | loop fusion | flops 196608 | bytes 917504 | tf_op jit(solution)/shard_map/convert_element_type | solution.py:183
  (11 shorter events, 0.1 us)
Async XLA Ops:
  1.6 26.0 %collective-permute-start.1 = (bf16[256,256]{0,1:T(8,128)(2,1)S(1)}, bf16[256,256]{0,1:T(8,128)(2,1)S(1)}, u32[]{:S(2)}, u32[]{:S(2)}) collective-permute-start(bf16[256,256]{0,1:T(8,128)(2,1)S(1)} %copy.28), channel_id=1, source_target_pairs={{0,1},{1,2},{2,3},{3,4},{4,5},{5,6},{6,7},{7,8},{8,9},{9,10},{10,1... | collective-permute-start | bytes 393224 | tf_op jit(solution)/shard_map/ppermute | solution.py:20
  5.4 22.3 %collective-permute-start = (bf16[256,256]{0,1:T(8,128)(2,1)S(1)}, bf16[256,256]{0,1:T(8,128)(2,1)S(1)}, u32[]{:S(2)}, u32[]{:S(2)}) collective-permute-start(bf16[256,256]{0,1:T(8,128)(2,1)S(1)} %copy.28), channel_id=1, source_target_pairs={{0,2},{1,3},{2,4},{3,5},{4,6},{5,7},{6,8},{7,9},{8,10},{9,11},{10,... | collective-permute-start | bytes 393224 | tf_op jit(solution)/shard_map/ppermute | solution.py:20
  8.5 20.9 %collective-permute-start.3 = (bf16[256,256]{1,0:T(8,128)(2,1)}, bf16[256,256]{1,0:T(8,128)(2,1)S(1)}, u32[]{:S(2)}, u32[]{:S(2)}) collective-permute-start(bf16[256,256]{1,0:T(8,128)(2,1)} %param.9), channel_id=1, source_target_pairs={{0,1},{1,2},{2,3},{3,4},{4,5},{5,6},{6,7},{7,8},{8,9},{9,10},{10,1... | collective-permute-start | bytes 393224 | tf_op jit(solution)/shard_map/ppermute | solution.py:20
  10.7 18.7 %collective-permute-start.2 = (bf16[256,256]{1,0:T(8,128)(2,1)}, bf16[256,256]{1,0:T(8,128)(2,1)S(1)}, u32[]{:S(2)}, u32[]{:S(2)}) collective-permute-start(bf16[256,256]{1,0:T(8,128)(2,1)} %param.9), channel_id=1, source_target_pairs={{0,2},{1,3},{2,4},{3,5},{4,6},{5,7},{6,8},{7,9},{8,10},{9,11},{10,... | collective-permute-start | bytes 393224 | tf_op jit(solution)/shard_map/ppermute | solution.py:20
  25.7 3.7 %copy-start = (bf16[256,256]{1,0:T(8,128)(2,1)S(1)}, bf16[256,256]{1,0:T(8,128)(2,1)}, u32[]{:S(2)}) copy-start(bf16[256,256]{1,0:T(8,128)(2,1)} %param.9) | copy-start | bytes 393220
  75.9 56.3 %collective-permute-start.5 = (f32[256,256]{1,0:T(8,128)S(1)}, f32[256,256]{1,0:T(8,128)S(1)}, u32[]{:S(2)}, u32[]{:S(2)}) collective-permute-start(f32[256,256]{1,0:T(8,128)S(1)} %get-tuple-element.12), channel_id=1, source_target_pairs={{2,0},{3,1},{4,2},{5,3},{6,4},{7,5},{8,6},{9,7},{10,8},{11,9},{12,... | collective-permute-start | bytes 786440 | tf_op jit(solution)/shard_map/ppermute | solution.py:20
  78.1 54.1 %collective-permute-start.4 = (f32[256,256]{1,0:T(8,128)S(1)}, f32[256,256]{1,0:T(8,128)S(1)}, u32[]{:S(2)}, u32[]{:S(2)}) collective-permute-start(f32[256,256]{1,0:T(8,128)S(1)} %get-tuple-element.11), channel_id=1, source_target_pairs={{1,0},{2,1},{3,2},{4,3},{5,4},{6,5},{7,6},{8,7},{9,8},{10,9},{11,1... | collective-permute-start | bytes 786440 | tf_op jit(solution)/shard_map/ppermute | solution.py:20
  128.3 10.7 %collective-permute-start.7 = (f32[256,256]{1,0:T(8,128)S(1)}, f32[256,256]{1,0:T(8,128)S(1)}, u32[]{:S(2)}, u32[]{:S(2)}) collective-permute-start(f32[256,256]{1,0:T(8,128)S(1)} %get-tuple-element.10), channel_id=1, source_target_pairs={{2,0},{3,1},{4,2},{5,3},{6,4},{7,5},{8,6},{9,7},{10,8},{11,9},{12,... | collective-permute-start | bytes 786440 | tf_op jit(solution)/shard_map/ppermute | solution.py:20
  130.2 11.7 %collective-permute-start.6 = (f32[256,256]{1,0:T(8,128)S(1)}, f32[256,256]{1,0:T(8,128)S(1)}, u32[]{:S(2)}, u32[]{:S(2)}) collective-permute-start(f32[256,256]{1,0:T(8,128)S(1)} %get-tuple-element.9), channel_id=1, source_target_pairs={{1,0},{2,1},{3,2},{4,3},{5,4},{6,5},{7,6},{8,7},{9,8},{10,9},{11,1... | collective-permute-start | bytes 786440 | tf_op jit(solution)/shard_map/ppermute | solution.py:20

commit v2 on v1

v2 whole, which is shorter than its diff:
```python
import math

import jax
import jax.numpy as jnp
from jax import lax
from jax.experimental import pallas as pl
from jax.experimental.pallas import tpu as pltpu
from jax.sharding import PartitionSpec as P

HD = 128
MOST = 512
KEY_TILE = 128
HEADS_PER_STEP = 8
NT_DIMS = (((1,), (1,)), ((), ()))


def shifted(block, axis, distance):
    devices = range(lax.axis_size(axis))
    route = [(i - distance, i) for i in devices if i - distance in devices]
    return lax.ppermute(block, axis, route)


def make_kernel(tok, reach, blocks_per_group):
    hb = HEADS_PER_STEP
    win = (reach + 1) * tok
    n_tiles = win // KEY_TILE
    tiles_per_piece = tok // KEY_TILE
    diag_tile = reach * tiles_per_piece
    scale = 1.0 / math.sqrt(HD)

    def kernel(flags_ref, q_ref, do_ref, o_ref, lse_ref, kid_ref, qid_ref, *rest):
        kv_refs = rest[:reach + 1]
        dq_ref, dkv_ref = rest[reach + 1:reach + 3]
        qs_scr, dos_scr, dqt_scr, kt_scr, bias_scr = rest[reach + 3:]
        g = pl.program_id(0)
        b = pl.program_id(1)

        @pl.when(b == 0)
        def _():
            dkv_ref[...] = jnp.zeros_like(dkv_ref)
            for piece in range(reach + 1):
                kv = kv_refs[reach - piece]
                kt_scr[:, piece * tok:(piece + 1) * tok] = (
                    kv[:, :HD].astype(jnp.float32).T.astype(jnp.bfloat16))

        @pl.when((b == 0) & (g == 0))
        def _():
            key_index = lax.broadcasted_iota(jnp.int32, (win, tok), 0) - reach * tok
            query_index = lax.broadcasted_iota(jnp.int32, (win, tok), 1)
            visible = (kid_ref[...] == qid_ref[...]) & (key_index <= query_index)
            bias_scr[...] = jnp.where(visible, 0.0, -jnp.inf).astype(jnp.float32)

        delta_rows = []
        for i in range(hb):
            cols = slice(i * HD, (i + 1) * HD)
            qs_scr[i * tok:(i + 1) * tok, :] = q_ref[:, cols]
            dos_scr[i * tok:(i + 1) * tok, :] = do_ref[:, cols]
            prod = do_ref[:, cols].astype(jnp.float32) * o_ref[:, cols].astype(jnp.float32)
            delta_rows.append(jnp.sum(prod.T, axis=0, keepdims=True))
        dl_row = jnp.concatenate(delta_rows, axis=1)
        lse_row = jnp.concatenate([lse_ref[i:i + 1, :] for i in range(hb)], axis=1)
        dqt_scr[...] = jnp.zeros_like(dqt_scr)

        for j in range(n_tiles):
            piece = j // tiles_per_piece
            kv = kv_refs[reach - piece]
            r0 = (j % tiles_per_piece) * KEY_TILE
            rows = slice(r0, r0 + KEY_TILE)
            win_rows = slice(j * KEY_TILE, (j + 1) * KEY_TILE)

            def tile(kv=kv, rows=rows, win_rows=win_rows, piece=piece):
                k = kv[rows, :HD]
                v = kv[rows, HD:]
                qs = qs_scr[...]
                dos = dos_scr[...]
                st = lax.dot_general(k, qs, NT_DIMS, preferred_element_type=jnp.float32)
                bias = bias_scr[win_rows, :]
                p = jnp.exp(st * scale - lse_row + jnp.concatenate([bias] * hb, axis=1))
                dv = jnp.dot(p.astype(jnp.bfloat16), dos, preferred_element_type=jnp.float32)
                dpt = lax.dot_general(v, dos, NT_DIMS, preferred_element_type=jnp.float32)
                ds = (p * (dpt - dl_row)).astype(jnp.bfloat16)
                dk = jnp.dot(ds, qs, preferred_element_type=jnp.float32)
                dkv_ref[piece, rows, :HD] += dk
                dkv_ref[piece, rows, HD:] += dv
                dqt_scr[...] += jnp.dot(
                    kt_scr[:, win_rows], ds, preferred_element_type=jnp.float32)

            if j >= diag_tile:
                tile()
            else:
                pl.when(flags_ref[j] != 0)(tile)

        for i in range(hb):
            dq_ref[:, i * HD:(i + 1) * HD] = (
                dqt_scr[:, i * tok:(i + 1) * tok] * scale).T.astype(dq_ref.dtype)

    return kernel


def grads_kernel(flags, queries, out_grad, outputs, lse, kid, qid, kv_pieces, reach):
    tok, width = queries.shape
    n_heads = width // HD
    kvh = kv_pieces[0].shape[1] // (2 * HD)
    heads_per_group = n_heads // kvh
    blocks_per_group = heads_per_group // HEADS_PER_STEP
    win = (reach + 1) * tok
    kernel = make_kernel(tok, reach, blocks_per_group)
    hb = HEADS_PER_STEP

    def head_block(g, b, flags_ref):
        return (0, g * blocks_per_group + b)

    def lse_block(g, b, flags_ref):
        return (g * blocks_per_group + b, 0)

    def full(g, b, flags_ref):
        return (0, 0)

    def group_cols(g, b, flags_ref):
        return (0, g)

    def group_cols3(g, b, flags_ref):
        return (0, 0, g)

    grid_spec = pltpu.PrefetchScalarGridSpec(
        num_scalar_prefetch=1,
        grid=(kvh, blocks_per_group),
        in_specs=[
            pl.BlockSpec((tok, hb * HD), head_block),
            pl.BlockSpec((tok, hb * HD), head_block),
            pl.BlockSpec((tok, hb * HD), head_block),
            pl.BlockSpec((hb, tok), lse_block),
            pl.BlockSpec((win, 1), full),
            pl.BlockSpec((1, tok), full),
        ] + [pl.BlockSpec((tok, 2 * HD), group_cols) for _ in kv_pieces],
        out_specs=[
            pl.BlockSpec((tok, hb * HD), head_block),
            pl.BlockSpec((reach + 1, tok, 2 * HD), group_cols3),
        ],
        scratch_shapes=[
            pltpu.VMEM((hb * tok, HD), jnp.bfloat16),
            pltpu.VMEM((hb * tok, HD), jnp.bfloat16),
            pltpu.VMEM((HD, hb * tok), jnp.float32),
            pltpu.VMEM((HD, win), jnp.bfloat16),
            pltpu.VMEM((win, tok), jnp.float32),
        ],
    )
    return pl.pallas_call(
        kernel,
        grid_spec=grid_spec,
        out_shape=[
            jax.ShapeDtypeStruct((tok, width), jnp.bfloat16),
            jax.ShapeDtypeStruct((reach + 1, tok, kvh * 2 * HD), jnp.float32),
        ],
        compiler_params=pltpu.CompilerParams(
            dimension_semantics=("arbitrary", "arbitrary")),
    )(flags, queries, out_grad, outputs, lse, kid, qid, *kv_pieces)


def per_device(queries, keys, values, outputs, out_grad, logsumexp, doc_lengths):
    tok, width = queries.shape
    kvh = keys.shape[1] // HD
    reach = -(-(MOST - 1) // tok)
    win = (reach + 1) * tok
    scale = 1.0 / math.sqrt(HD)
    position = lax.axis_index("seq")
    doc_ends = jnp.cumsum(doc_lengths)

    def doc_of(places):
        return jnp.sum((doc_ends[None, :] <= places[:, None]).astype(jnp.int32), axis=1)

    query_places = position * tok + jnp.arange(tok, dtype=jnp.int32)
    query_ids = doc_of(query_places)
    key_places = (position - reach) * tok + jnp.arange(win, dtype=jnp.int32)
    key_ids = jnp.where(key_places >= 0, doc_of(key_places), -1)
    n_tiles = win // KEY_TILE
    last_ids = key_ids[KEY_TILE - 1::KEY_TILE]
    diag_tile = reach * tok // KEY_TILE
    flags = ((last_ids == query_ids[0])
             | (jnp.arange(n_tiles) >= diag_tile)).astype(jnp.int32)

    kv = jnp.concatenate(
        [keys.reshape(tok, kvh, 1, HD), values.reshape(tok, kvh, 1, HD)], axis=2
    ).reshape(tok, kvh * 2 * HD)
    kv_pieces = [kv] + [shifted(kv, "seq", hop) for hop in range(1, reach + 1)]

    dq, dkv = grads_kernel(
        flags, queries, out_grad, outputs, logsumexp, key_ids[:, None], query_ids[None, :],
        kv_pieces, reach)

    total = dkv[reach]
    for hop in range(1, reach + 1):
        total = total + shifted(dkv[reach - hop], "seq", -hop)
    total = total.reshape(tok, kvh, 2, HD)
    key_total = total[:, :, 0, :].reshape(tok, kvh * HD)
    value_total = total[:, :, 1, :].reshape(tok, kvh * HD)
    return (
        dq,
        (key_total * scale).astype(jnp.bfloat16),
        value_total.astype(jnp.bfloat16),
    )


def solution(mesh):
    in_specs = (
        P(("parts", "seq"), None),
        P(("parts", "seq"), None),
        P(("parts", "seq"), None),
        P(("parts", "seq"), None),
        P(("parts", "seq"), None),
        P(None, ("parts", "seq")),
        P("parts"),
    )
    out_specs = (P(("parts", "seq"), None), P(("parts", "seq"), None), P(("parts", "seq"), None))
    return jax.shard_map(
        per_device, mesh=mesh, in_specs=in_specs, out_specs=out_specs, check_vma=False
    )
```

time: 144 us -> 72.6 us (0.50)
  the two profiles are of different devices: /device:TPU:13 before, /device:TPU:10 now
where the time goes in v2:
time: 72.6 us; the launch traced here: 72.1 us
  waiting for transfers between devices  25.8 us (36%)
  Pallas kernels  24.2 us (33%)
  starting transfers between devices  9.19 us (13%)
  local copies, waits for them, and re-layouts  7.84 us (11%)
  other arithmetic  4.29 us (6%)
  between operations  0.81 us (1%)
    ppermute x4, waiting for transfers between devices, shifted(): return lax.ppermute(block, axis, route)  25.8 us
    pallas_call x1, Pallas kernels, grads_kernel(): pl.pallas_call(kernel, grid_spec=grid_spec, out_shape=[jax.ShapeDtypeStru...  24.2 us
    ppermute x4, starting transfers between devices, shifted(): return lax.ppermute(block, axis, route)  9.19 us
    unnamed x14, local copies, waits for them, and re-layouts  2.48 us
  transfers between devices with their start and end apart: 4, of which 4 were waited for; matrix products, arithmetic and copies ran while one was open for 4% of the time, Pallas kernels for 0%

profile of v2, /device:TPU:10, one launch (start us, length us, event | category | flops | bytes accessed | tf_op | source)
XLA Modules:
  0.0 72.1 jit_solution(18136196638704786494)
XLA Ops:
  0.6 0.0 copy-start.4
  0.6 1.3 %reshape.75 = bf16[256,2,1,128]{3,2,1,0:T(2,128)(2,1)S(1)} reshape(bf16[256,256]{1,0:T(8,128)(2,1)} %param.8) | data formatting | bytes 262144 | tf_op jit(solution)/shard_map/reshape | solution.py:183
  1.9 1.3 %reshape.76 = bf16[256,2,1,128]{3,2,1,0:T(2,128)(2,1)S(1)} reshape(bf16[256,256]{1,0:T(8,128)(2,1)} %param.9) | data formatting | bytes 262144 | tf_op jit(solution)/shard_map/reshape | solution.py:183
  3.2 0.6 pad_maximum_fusion
  3.8 0.1 reshape.73.rest_0_
  3.9 3.4 %collective-permute-start.1 = (bf16[256,512]{1,0:T(8,128)(2,1)S(1)}, bf16[256,512]{1,0:T(8,128)(2,1)S(1)}, u32[]{:S(2)}, u32[]{:S(2)}) collective-permute-start(bf16[256,512]{1,0:T(8,128)(2,1)S(1)} %reshape.73.rest_0_), channel_id=1, source_target_pairs={{0,2},{1,3},{2,4},{3,5},{4,6},{5,7},{6,8},{7,9},{8,10},{9,11},{10,... | collective-permute-start | bytes 786440 | tf_op jit(solution)/shard_map/ppermute | solution.py:20
  7.3 1.9 %collective-permute-start = (bf16[256,512]{1,0:T(8,128)(2,1)S(1)}, bf16[256,512]{1,0:T(8,128)(2,1)S(1)}, u32[]{:S(2)}, u32[]{:S(2)}) collective-permute-start(bf16[256,512]{1,0:T(8,128)(2,1)S(1)} %reshape.73.rest_0_), channel_id=1, source_target_pairs={{0,1},{1,2},{2,3},{3,4},{4,5},{5,6},{6,7},{7,8},{8,9},{9,10},{10,1... | collective-permute-start | bytes 786440 | tf_op jit(solution)/shard_map/ppermute | solution.py:20
  9.3 0.1 copy.21
  9.4 0.1 reduce
  9.5 0.1 convert_reduce_fusion
  9.6 0.9 %reshape_select_fusion.kid_ref = s32[768,1]{1,0:T(8,128)} fusion(s32[768]{0:T(1024)S(1)} %convert_reduce_fusion, s32[]{:T(128)S(6)} %mul.13), kind=kLoop, calls=%fused_computation.4 | loop fusion | flops 2304 | bytes 6148 | tf_op jit(solution)/shard_map/jit(_where)/select_n | solution.py:175
  10.5 0.1 convert_reduce_fusion.1
  10.6 0.5 slice.23
  11.1 0.1 slice.22
  11.2 1.2 %or_convert_fusion.flags_ref = s32[6]{0:T(128)} fusion(s32[6]{0:T(128)S(1)} %slice.22, s32[]{:T(128)} %bitcast.1), kind=kLoop, calls=%fused_computation.12 | loop fusion | flops 24 | bytes 52 | tf_op jit(solution)/shard_map/convert_element_type | solution.py:180
  12.5 3.4 %collective-permute-done.1.rest_2_ = bf16[256,512]{1,0:T(8,128)(2,1)S(1)} collective-permute-done((bf16[256,512]{1,0:T(8,128)(2,1)S(1)}, bf16[256,512]{1,0:T(8,128)(2,1)S(1)}, u32[]{:S(2)}, u32[]{:S(2)}) %collective-permute-start.1) | collective-permute-done | bytes 262176 | tf_op jit(solution)/shard_map/ppermute | solution.py:20
  15.9 1.7 %collective-permute-done.rest_1_ = bf16[256,512]{1,0:T(8,128)(2,1)S(1)} collective-permute-done((bf16[256,512]{1,0:T(8,128)(2,1)S(1)}, bf16[256,512]{1,0:T(8,128)(2,1)S(1)}, u32[]{:S(2)}, u32[]{:S(2)}) %collective-permute-start) | collective-permute-done | bytes 262176 | tf_op jit(solution)/shard_map/ppermute | solution.py:20
  17.6 0.7 copy-done.2
  18.2 24.2 %shard_map.94 = (bf16[256,4096]{1,0:T(8,128)(2,1)}, f32[3,256,512]{2,1,0:T(8,128)}) custom-call(s32[6]{0:T(128)} %or_convert_fusion.flags_ref, bf16[256,4096]{1,0:T(8,128)(2,1)} %q_ref.1, bf16[256,4096]{1,0:T(8,128)(2,1)} %do_ref.1, bf16[256,4096]{1,0:T(8,128)(2,1)} %o_ref.1, f32[32,256]{1,0:T(8,128)} %lse_ref.1, s32[768,1]{1,0:T(8,128)} %reshape_select_fusion.kid_ref, ...), custom_call_target="tpu_custom_call" | custom-call | tf_op jit(solution)/shard_map/pallas_call | solution.py:148
  42.5 1.3 %slice_bitcast_fusion.1 = (f32[256,512]{1,0:T(8,128)S(1)}, f32[256,512]{1,0:T(8,128)S(1)}) fusion(f32[3,256,512]{2,1,0:T(8,128)} %get-tuple-element.6), kind=kLoop, calls=%fused_computation.3 | loop fusion | bytes 2097152 | tf_op jit(solution)/shard_map/squeeze | solution.py:193
  43.7 1.9 %collective-permute-start.2 = (f32[256,512]{1,0:T(8,128)S(1)}, f32[256,512]{1,0:T(8,128)S(1)}, u32[]{:S(2)}, u32[]{:S(2)}) collective-permute-start(f32[256,512]{1,0:T(8,128)S(1)} %get-tuple-element.13), channel_id=1, source_target_pairs={{1,0},{2,1},{3,2},{4,3},{5,4},{6,5},{7,6},{8,7},{9,8},{10,9},{11,1... | collective-permute-start | bytes 1572872 | tf_op jit(solution)/shard_map/ppermute | solution.py:20
  45.7 1.9 %collective-permute-start.3 = (f32[256,512]{1,0:T(8,128)S(1)}, f32[256,512]{1,0:T(8,128)S(1)}, u32[]{:S(2)}, u32[]{:S(2)}) collective-permute-start(f32[256,512]{1,0:T(8,128)S(1)} %get-tuple-element.14), channel_id=1, source_target_pairs={{2,0},{3,1},{4,2},{5,3},{6,4},{7,5},{8,6},{9,7},{10,8},{11,9},{12,... | collective-permute-start | bytes 1572872 | tf_op jit(solution)/shard_map/ppermute | solution.py:20
  47.6 8.6 %collective-permute-done.2 = f32[256,512]{1,0:T(8,128)S(1)} collective-permute-done((f32[256,512]{1,0:T(8,128)S(1)}, f32[256,512]{1,0:T(8,128)S(1)}, u32[]{:S(2)}, u32[]{:S(2)}) %collective-permute-start.2) | collective-permute-done | bytes 524320 | tf_op jit(solution)/shard_map/ppermute | solution.py:20
  56.2 12.1 %collective-permute-done.3 = f32[256,512]{1,0:T(8,128)S(1)} collective-permute-done((f32[256,512]{1,0:T(8,128)S(1)}, f32[256,512]{1,0:T(8,128)S(1)}, u32[]{:S(2)}, u32[]{:S(2)}) %collective-permute-start.3) | collective-permute-done | bytes 524320 | tf_op jit(solution)/shard_map/ppermute | solution.py:20
  68.3 1.2 %fusion = f32[256,512]{1,0:T(8,128)S(1)} fusion(f32[256,512]{1,0:T(8,128)S(1)} %collective-permute-done.3, f32[256,512]{1,0:T(8,128)S(1)} %collective-permute-done.2, f32[3,256,512]{2,1,0:T(8,128)} %get-tuple-element.6), kind=kLoop, calls=%fused_computation.1 | loop fusion | flops 262144 | bytes 2097152 | tf_op jit(solution)/shard_map/add | solution.py:193
  69.5 0.3 reshape.74
  69.8 0.2 slice.29
  70.0 0.3 slice.30
  70.3 0.1 copy.30
  70.4 0.8 %copy.28 = bf16[256,256]{1,0:T(8,128)(2,1)} copy(bf16[256,256]{0,1:T(8,128)(2,1)S(1)} %bitcast.13) | data formatting | bytes 262144
  71.2 0.1 copy.29
  71.4 0.8 %copy.27 = bf16[256,256]{1,0:T(8,128)(2,1)} copy(bf16[256,256]{0,1:T(8,128)(2,1)S(1)} %bitcast.14) | data formatting | bytes 262144
  (13 shorter events, 0.1 us)
Async XLA Ops:
  0.6 8.6 %copy-start.4 = (s32[16]{0:T(128)S(1)}, s32[16]{0:T(128)}, u32[]{:S(2)}) copy-start(s32[16]{0:T(128)} %param.13) | copy-start | bytes 196
  3.9 13.7 %copy-start = (bf16[256,512]{1,0:T(8,128)(2,1)}, bf16[256,512]{1,0:T(8,128)(2,1)S(1)}, u32[]{:S(2)}) copy-start(bf16[256,512]{1,0:T(8,128)(2,1)S(1)} %reshape.73.rest_0_) | copy-start | bytes 786436
  3.9 12.0 %collective-permute-start.1 = (bf16[256,512]{1,0:T(8,128)(2,1)S(1)}, bf16[256,512]{1,0:T(8,128)(2,1)S(1)}, u32[]{:S(2)}, u32[]{:S(2)}) collective-permute-start(bf16[256,512]{1,0:T(8,128)(2,1)S(1)} %reshape.73.rest_0_), channel_id=1, source_target_pairs={{0,2},{1,3},{2,4},{3,5},{4,6},{5,7},{6,8},{7,9},{8,10},{9,11},{10,... | collective-permute-start | bytes 786440 | tf_op jit(solution)/shard_map/ppermute | solution.py:20
  7.3 10.2 %collective-permute-start = (bf16[256,512]{1,0:T(8,128)(2,1)S(1)}, bf16[256,512]{1,0:T(8,128)(2,1)S(1)}, u32[]{:S(2)}, u32[]{:S(2)}) collective-permute-start(bf16[256,512]{1,0:T(8,128)(2,1)S(1)} %reshape.73.rest_0_), channel_id=1, source_target_pairs={{0,1},{1,2},{2,3},{3,4},{4,5},{5,6},{6,7},{7,8},{8,9},{9,10},{10,1... | collective-permute-start | bytes 786440 | tf_op jit(solution)/shard_map/ppermute | solution.py:20
  10.6 6.9 %copy-start.3 = (s32[256]{0:T(256)}, s32[256]{0:T(256)S(1)}, u32[]{:S(2)}) copy-start(s32[256]{0:T(256)S(1)} %convert_reduce_fusion.1) | copy-start | bytes 3076
  15.9 1.7 %copy-start.1 = (bf16[256,512]{1,0:T(8,128)(2,1)}, bf16[256,512]{1,0:T(8,128)(2,1)S(1)}, u32[]{:S(2)}) copy-start(bf16[256,512]{1,0:T(8,128)(2,1)S(1)} %collective-permute-done.1.rest_2_) | copy-start | bytes 786436
  17.5 0.7 copy-start.2
  43.7 12.4 %collective-permute-start.2 = (f32[256,512]{1,0:T(8,128)S(1)}, f32[256,512]{1,0:T(8,128)S(1)}, u32[]{:S(2)}, u32[]{:S(2)}) collective-permute-start(f32[256,512]{1,0:T(8,128)S(1)} %get-tuple-element.13), channel_id=1, source_target_pairs={{1,0},{2,1},{3,2},{4,3},{5,4},{6,5},{7,6},{8,7},{9,8},{10,9},{11,1... | collective-permute-start | bytes 1572872 | tf_op jit(solution)/shard_map/ppermute | solution.py:20
  45.7 22.6 %collective-permute-start.3 = (f32[256,512]{1,0:T(8,128)S(1)}, f32[256,512]{1,0:T(8,128)S(1)}, u32[]{:S(2)}, u32[]{:S(2)}) collective-permute-start(f32[256,512]{1,0:T(8,128)S(1)} %get-tuple-element.14), channel_id=1, source_target_pairs={{2,0},{3,1},{4,2},{5,3},{6,4},{7,5},{8,6},{9,7},{10,8},{11,9},{12,... | collective-permute-start | bytes 1572872 | tf_op jit(solution)/shard_map/ppermute | solution.py:20

commit v3 on v2

v3 whole, which is shorter than its diff:
```python
import math

import jax
import jax.numpy as jnp
from jax import lax
from jax.experimental import pallas as pl
from jax.experimental.pallas import tpu as pltpu
from jax.sharding import PartitionSpec as P

HD = 128
MOST = 512
KEY_TILE = 128
HEADS_PER_STEP = 8
NT_DIMS = (((1,), (1,)), ((), ()))


def shifted(block, axis, distance):
    devices = range(lax.axis_size(axis))
    route = [(i - distance, i) for i in devices if i - distance in devices]
    return lax.ppermute(block, axis, route)


def make_kernel(tok, reach, remote, dq_in, dq_final, n_alias):
    hb = HEADS_PER_STEP
    pieces = list(range(reach)) if remote else [reach]
    tiles_per_piece = tok // KEY_TILE
    n_rows = len(pieces) * tok
    scale = 1.0 / math.sqrt(HD)

    def kernel(flags_ref, q_ref, do_ref, o_ref, lse_ref, bias_ref, *rest):
        rest = list(rest)
        kv_refs = [rest.pop(0) for _ in pieces]
        dqp_ref = rest.pop(0) if dq_in else None
        rest = rest[n_alias:]
        dq_ref = rest.pop(0)
        dkv_ref = rest.pop(0)
        qs_scr, dos_scr, dqt_scr, kt_scr, acc_scr = rest[-5:]
        b = pl.program_id(0)
        nb = pl.num_programs(0)

        @pl.when(b == 0)
        def _():
            acc_scr[...] = jnp.zeros_like(acc_scr)
            for n, kv in enumerate(kv_refs):
                kt_scr[:, n * tok:(n + 1) * tok] = (
                    kv[:, :HD].astype(jnp.float32).T.astype(jnp.bfloat16))

        delta_rows = []
        for i in range(hb):
            cols = slice(i * HD, (i + 1) * HD)
            qs_scr[i * tok:(i + 1) * tok, :] = q_ref[:, cols]
            dos_scr[i * tok:(i + 1) * tok, :] = do_ref[:, cols]
            prod = do_ref[:, cols].astype(jnp.float32) * o_ref[:, cols].astype(jnp.float32)
            delta_rows.append(jnp.sum(prod.T, axis=0, keepdims=True))
        dl_row = jnp.concatenate(delta_rows, axis=1)
        lse_row = jnp.concatenate([lse_ref[i:i + 1, :] for i in range(hb)], axis=1)
        dqt_scr[...] = jnp.zeros_like(dqt_scr)

        for n, piece in enumerate(pieces):
            kv = kv_refs[n]
            for t in range(tiles_per_piece):
                j = piece * tiles_per_piece + t
                rows = slice(t * KEY_TILE, (t + 1) * KEY_TILE)
                loc_rows = slice(n * tok + t * KEY_TILE, n * tok + (t + 1) * KEY_TILE)

                def tile(kv=kv, rows=rows, loc_rows=loc_rows, n=n):
                    k = kv[rows, :HD]
                    v = kv[rows, HD:]
                    qs = qs_scr[...]
                    dos = dos_scr[...]
                    st = lax.dot_general(k, qs, NT_DIMS, preferred_element_type=jnp.float32)
                    bias = bias_ref[loc_rows, :]
                    p = jnp.exp(st * scale - lse_row + jnp.concatenate([bias] * hb, axis=1))
                    dv = jnp.dot(p.astype(jnp.bfloat16), dos, preferred_element_type=jnp.float32)
                    dpt = lax.dot_general(v, dos, NT_DIMS, preferred_element_type=jnp.float32)
                    ds = (p * (dpt - dl_row)).astype(jnp.bfloat16)
                    dk = jnp.dot(ds, qs, preferred_element_type=jnp.float32)
                    acc_scr[n, rows, :HD] += dk
                    acc_scr[n, rows, HD:] += dv
                    dqt_scr[...] += jnp.dot(
                        kt_scr[:, loc_rows], ds, preferred_element_type=jnp.float32)

                if remote:
                    pl.when(flags_ref[j] != 0)(tile)
                else:
                    tile()

        for i in range(hb):
            cols = slice(i * HD, (i + 1) * HD)
            part = dqt_scr[:, i * tok:(i + 1) * tok].T
            if dq_in:
                part = part + dqp_ref[:, cols]
            if dq_final:
                dq_ref[:, cols] = (part * scale).astype(dq_ref.dtype)
            else:
                dq_ref[:, cols] = part

        @pl.when(b == nb - 1)
        def _():
            dkv_ref[...] = acc_scr[...].astype(dkv_ref.dtype)

    return kernel


def grads_call(group, remote, flags, queries, out_grad, outputs, lse, bias, kv_pieces,
               reach, dq_part=None, dq_alias=None, dkv_alias=None):
    tok, width = queries.shape
    n_heads = width // HD
    kvh = kv_pieces[0].shape[1] // (2 * HD)
    heads_per_group = n_heads // kvh
    hb = HEADS_PER_STEP
    nb = heads_per_group // hb
    dq_final = dq_part is not None
    pieces = list(range(reach)) if remote else [reach]
    n_pieces = len(pieces)

    def head_block(b, f):
        return (0, group * nb + b)

    def lse_block(b, f):
        return (group * nb + b, 0)

    def local_block(b, f):
        return (0, b)

    def bias_block(b, f):
        return (0, 0) if remote else (reach, 0)

    def kv_block(b, f):
        return (0, group)

    in_specs = [
        pl.BlockSpec((tok, hb * HD), head_block),
        pl.BlockSpec((tok, hb * HD), head_block),
        pl.BlockSpec((tok, hb * HD), head_block),
        pl.BlockSpec((hb, tok), lse_block),
        pl.BlockSpec((n_pieces * tok, tok), bias_block),
    ] + [pl.BlockSpec((tok, 2 * HD), kv_block) for _ in pieces]
    args = [queries, out_grad, outputs, lse, bias] + [kv_pieces[reach - p] for p in pieces]
    if dq_part is not None:
        in_specs.append(pl.BlockSpec((tok, hb * HD), local_block))
        args.append(dq_part)
    aliases = {}
    if dq_alias is not None:
        aliases[len(args) + 1] = 0
        in_specs.append(pl.BlockSpec(memory_space=pl.ANY))
        args.append(dq_alias)
    if dkv_alias is not None:
        aliases[len(args) + 1] = 1
        in_specs.append(pl.BlockSpec(memory_space=pl.ANY))
        args.append(dkv_alias)

    kernel = make_kernel(tok, reach, remote, dq_part is not None, dq_final, len(aliases))
    if dq_final:
        dq_shape = jax.ShapeDtypeStruct((tok, width), jnp.bfloat16)
        dq_spec = pl.BlockSpec((tok, hb * HD), head_block)
    else:
        dq_shape = jax.ShapeDtypeStruct((tok, heads_per_group * HD), jnp.float32)
        dq_spec = pl.BlockSpec((tok, hb * HD), local_block)
    if remote:
        dkv_shape = jax.ShapeDtypeStruct((n_pieces, tok, kvh * 2 * HD), jnp.bfloat16)
        dkv_spec = pl.BlockSpec((n_pieces, tok, 2 * HD), lambda b, f: (0, 0, group))
    else:
        dkv_shape = jax.ShapeDtypeStruct((n_pieces, tok, 2 * HD), jnp.float32)
        dkv_spec = pl.BlockSpec((n_pieces, tok, 2 * HD), lambda b, f: (0, 0, 0))

    grid_spec = pltpu.PrefetchScalarGridSpec(
        num_scalar_prefetch=1,
        grid=(nb,),
        in_specs=in_specs,
        out_specs=[dq_spec, dkv_spec],
        scratch_shapes=[
            pltpu.VMEM((hb * tok, HD), jnp.bfloat16),
            pltpu.VMEM((hb * tok, HD), jnp.bfloat16),
            pltpu.VMEM((HD, hb * tok), jnp.float32),
            pltpu.VMEM((HD, n_pieces * tok), jnp.bfloat16),
            pltpu.VMEM((n_pieces, tok, 2 * HD), jnp.float32),
        ],
    )
    return pl.pallas_call(
        kernel,
        grid_spec=grid_spec,
        out_shape=[dq_shape, dkv_shape],
        input_output_aliases=aliases,
        compiler_params=pltpu.CompilerParams(dimension_semantics=("arbitrary",)),
    )(flags, *args)


def per_device(queries, keys, values, outputs, out_grad, logsumexp, doc_lengths):
    tok, width = queries.shape
    kvh = keys.shape[1] // HD
    reach = -(-(MOST - 1) // tok)
    win = (reach + 1) * tok
    scale = 1.0 / math.sqrt(HD)
    position = lax.axis_index("seq")
    doc_ends = jnp.cumsum(doc_lengths)

    def doc_of(places):
        return jnp.sum((doc_ends[None, :] <= places[:, None]).astype(jnp.int32), axis=1)

    query_places = position * tok + jnp.arange(tok, dtype=jnp.int32)
    query_ids = doc_of(query_places)
    key_places = (position - reach) * tok + jnp.arange(win, dtype=jnp.int32)
    key_ids = jnp.where(key_places >= 0, doc_of(key_places), -1)
    visible = (key_ids[:, None] == query_ids[None, :]) & (
        key_places[:, None] <= query_places[None, :])
    bias = jnp.where(visible, 0.0, -jnp.inf).astype(jnp.float32)
    n_tiles = win // KEY_TILE
    last_places = (position - reach) * tok + KEY_TILE * jnp.arange(
        1, n_tiles + 1, dtype=jnp.int32) - 1
    first_doc = doc_of(position[None] * tok)
    flags = ((doc_of(last_places) == first_doc) & (last_places >= 0)).astype(jnp.int32)

    kv = jnp.concatenate(
        [keys.reshape(tok, kvh, 1, HD), values.reshape(tok, kvh, 1, HD)], axis=2
    ).reshape(tok, kvh * 2 * HD)
    kv_pieces = [kv] + [shifted(kv, "seq", hop) for hop in range(1, reach + 1)]
    common = (flags, queries, out_grad, outputs, logsumexp, bias, kv_pieces, reach)

    dq_part0, dkv_own0 = grads_call(0, False, *common)
    dq, dkv_rem = grads_call(0, True, *common, dq_part=dq_part0)
    dq_part1, dkv_rem = grads_call(1, True, *common, dkv_alias=dkv_rem)
    returned = [shifted(dkv_rem[reach - hop], "seq", -hop) for hop in range(1, reach + 1)]
    dq, dkv_own1 = grads_call(1, False, *common, dq_part=dq_part1, dq_alias=dq)

    total = jnp.concatenate([dkv_own0[0], dkv_own1[0]], axis=1)
    for r in returned:
        total = total + r.astype(jnp.float32)
    total = total.reshape(tok, kvh, 2, HD)
    key_total = total[:, :, 0, :].reshape(tok, kvh * HD)
    value_total = total[:, :, 1, :].reshape(tok, kvh * HD)
    return (
        dq,
        (key_total * scale).astype(jnp.bfloat16),
        value_total.astype(jnp.bfloat16),
    )


def solution(mesh):
    in_specs = (
        P(("parts", "seq"), None),
        P(("parts", "seq"), None),
        P(("parts", "seq"), None),
        P(("parts", "seq"), None),
        P(("parts", "seq"), None),
        P(None, ("parts", "seq")),
        P("parts"),
    )
    out_specs = (P(("parts", "seq"), None), P(("parts", "seq"), None), P(("parts", "seq"), None))
    return jax.shard_map(
        per_device, mesh=mesh, in_specs=in_specs, out_specs=out_specs, check_vma=False
    )
```

time: 72.6 us -> 67.6 us (0.931)
  the two profiles are of different devices: /device:TPU:10 before, /device:TPU:22 now
where the time goes in v3:
time: 67.6 us; the launch traced here: 67.2 us
  Pallas kernels  33.8 us (50%)
  starting transfers between devices  17.1 us (25%)
  local copies, waits for them, and re-layouts  7.13 us (11%)
  other arithmetic  5.05 us (7%)
  waiting for transfers between devices  3.29 us (5%)
  between operations  0.86 us (1%)
    pallas_call x4, Pallas kernels, grads_call(): pl.pallas_call(kernel, grid_spec=grid_spec, out_shape=[dq_shape, dkv_shap...  33.8 us
    ppermute x4, starting transfers between devices, shifted(): return lax.ppermute(block, axis, route)  17.1 us
    ppermute x4, waiting for transfers between devices, shifted(): return lax.ppermute(block, axis, route)  3.29 us
    unnamed x14, local copies, waits for them, and re-layouts  2.57 us
  transfers between devices with their start and end apart: 4, of which 1 were waited for; matrix products, arithmetic and copies ran while one was open for 5% of the time, Pallas kernels for 23%

profile of v3, /device:TPU:22, one launch (start us, length us, event | category | flops | bytes accessed | tf_op | source)
XLA Modules:
  0.0 67.2 jit_solution(9642996224888982781)
XLA Ops:
  0.6 1.3 %reshape.86 = bf16[256,2,1,128]{3,2,1,0:T(2,128)(2,1)S(1)} reshape(bf16[256,256]{1,0:T(8,128)(2,1)} %param.8) | data formatting | bytes 262144 | tf_op jit(solution)/shard_map/reshape | solution.py:215
  1.9 1.3 %reshape.87 = bf16[256,2,1,128]{3,2,1,0:T(2,128)(2,1)S(1)} reshape(bf16[256,256]{1,0:T(8,128)(2,1)} %param.9) | data formatting | bytes 262144 | tf_op jit(solution)/shard_map/reshape | solution.py:215
  3.2 0.6 pad_maximum_fusion
  3.8 0.1 reshape.84.rest_0_
  3.9 1.9 %collective-permute-start.1 = (bf16[256,512]{1,0:T(8,128)(2,1)S(1)}, bf16[256,512]{1,0:T(8,128)(2,1)S(1)}, u32[]{:S(2)}, u32[]{:S(2)}) collective-permute-start(bf16[256,512]{1,0:T(8,128)(2,1)S(1)} %reshape.84.rest_0_), channel_id=1, source_target_pairs={{0,1},{1,2},{2,3},{3,4},{4,5},{5,6},{6,7},{7,8},{8,9},{9,10},{10,1... | collective-permute-start | bytes 786440 | tf_op jit(solution)/shard_map/ppermute | solution.py:20
  5.8 3.4 %collective-permute-start = (bf16[256,512]{1,0:T(8,128)(2,1)S(1)}, bf16[256,512]{1,0:T(8,128)(2,1)S(1)}, u32[]{:S(2)}, u32[]{:S(2)}) collective-permute-start(bf16[256,512]{1,0:T(8,128)(2,1)S(1)} %reshape.84.rest_0_), channel_id=1, source_target_pairs={{0,2},{1,3},{2,4},{3,5},{4,6},{5,7},{6,8},{7,9},{8,10},{9,11},{10,... | collective-permute-start | bytes 786440 | tf_op jit(solution)/shard_map/ppermute | solution.py:20
  9.3 0.1 copy.22
  9.4 0.6 convert_reduce_fusion.2
  10.1 0.2 convert_reduce_fusion.3
  10.2 0.1 convert_reduce_fusion
  10.3 1.2 %and_convert_fusion.flags_ref = s32[6]{0:T(128)} fusion(s32[6]{0:T(128)S(1)} %convert_reduce_fusion.3, s32[]{:T(128)} %get-tuple-element.25, s32[]{:T(128)S(6)} %mul.23), kind=kLoop, calls=%fused_computation.13 | loop fusion | flops 48 | bytes 56 | tf_op jit(solution)/shard_map/convert_element_type | solution.py:212
  11.5 0.1 convert_reduce_fusion.1
  11.6 1.2 %and_select_fusion.bias_ref = f32[768,256]{1,0:T(8,128)} fusion(s32[256]{0:T(256)S(1)} %iota_add_fusion.1, s32[256]{0:T(256)S(1)} %convert_reduce_fusion.1, s32[768]{0:T(1024)S(1)} %iota_add_fusion, s32[768]{0:T(1024)S(1)} %compare_select_fusion), kind=kLoop, calls=%fused_computation | loop fusion | flops 786432 | bytes 794624 | tf_op jit(solution)/shard_map/jit(_where)/select_n | solution.py:207
  12.8 7.6 %shard_map.94 = (f32[256,2048]{1,0:T(8,128)}, f32[1,256,256]{2,1,0:T(8,128)}) custom-call(s32[6]{0:T(128)} %and_convert_fusion.flags_ref, bf16[256,4096]{1,0:T(8,128)(2,1)} %q_ref.7, bf16[256,4096]{1,0:T(8,128)(2,1)} %do_ref.7, bf16[256,4096]{1,0:T(8,128)(2,1)} %o_ref.7, f32[32,256]{1,0:T(8,128)} %lse_ref.7, f32[768,256]{1,0:T(8,128)} %and_select_fusion.bias_ref, ...), custom_call_target="tpu_custom_call" | custom-call | tf_op jit(solution)/shard_map/pallas_call | solution.py:180
  20.3 0.0 collective-permute-done.1.rest_1_
  20.4 0.7 copy-done.1
  21.0 0.1 copy-done.2
  21.2 9.3 %shard_map.95 = (bf16[256,4096]{1,0:T(8,128)(2,1)}, bf16[2,256,512]{2,1,0:T(8,128)(2,1)}) custom-call(s32[6]{0:T(128)} %and_convert_fusion.flags_ref, bf16[256,4096]{1,0:T(8,128)(2,1)} %q_ref.7, bf16[256,4096]{1,0:T(8,128)(2,1)} %do_ref.7, bf16[256,4096]{1,0:T(8,128)(2,1)} %o_ref.7, f32[32,256]{1,0:T(8,128)} %lse_ref.7, f32[768,256]{1,0:T(8,128)} %and_select_fusion.bias_ref, ...), custom_call_target="tpu_custom_call" | custom-call | tf_op jit(solution)/shard_map/pallas_call | solution.py:180
  30.4 9.1 %shard_map.96 = (f32[256,2048]{1,0:T(8,128)}, bf16[2,256,512]{2,1,0:T(8,128)(2,1)}) custom-call(s32[6]{0:T(128)} %and_convert_fusion.flags_ref, bf16[256,4096]{1,0:T(8,128)(2,1)} %q_ref.7, bf16[256,4096]{1,0:T(8,128)(2,1)} %do_ref.7, bf16[256,4096]{1,0:T(8,128)(2,1)} %o_ref.7, f32[32,256]{1,0:T(8,128)} %lse_ref.7, ...), custom_call_target="tpu_custom_call", output_to_operand_aliasing={{1}: (8, {})} | custom-call | tf_op jit(solution)/shard_map/pallas_call | solution.py:180
  39.5 1.1 %slice_bitcast_fusion.1 = (bf16[256,512]{1,0:T(8,128)(2,1)S(1)}, bf16[256,512]{1,0:T(8,128)(2,1)S(1)}) fusion(bf16[2,256,512]{2,1,0:T(8,128)(2,1)} %get-tuple-element.18), kind=kLoop, calls=%fused_computation.6 | loop fusion | bytes 1048576 | tf_op jit(solution)/shard_map/squeeze | solution.py:223
  40.6 3.4 %collective-permute-start.2 = (bf16[256,512]{1,0:T(8,128)(2,1)S(1)}, bf16[256,512]{1,0:T(8,128)(2,1)S(1)}, u32[]{:S(2)}, u32[]{:S(2)}) collective-permute-start(bf16[256,512]{1,0:T(8,128)(2,1)S(1)} %get-tuple-element.27), channel_id=1, source_target_pairs={{1,0},{2,1},{3,2},{4,3},{5,4},{6,5},{7,6},{8,7},{9,8},{10,9},{11,1... | collective-permute-start | bytes 786440 | tf_op jit(solution)/shard_map/ppermute | solution.py:20
  43.9 8.4 %collective-permute-start.3 = (bf16[256,512]{1,0:T(8,128)(2,1)S(1)}, bf16[256,512]{1,0:T(8,128)(2,1)S(1)}, u32[]{:S(2)}, u32[]{:S(2)}) collective-permute-start(bf16[256,512]{1,0:T(8,128)(2,1)S(1)} %get-tuple-element.28), channel_id=1, source_target_pairs={{2,0},{3,1},{4,2},{5,3},{6,4},{7,5},{8,6},{9,7},{10,8},{11,9},{12,... | collective-permute-start | bytes 786440 | tf_op jit(solution)/shard_map/ppermute | solution.py:20
  52.4 7.9 %shard_map.97 = (bf16[256,4096]{1,0:T(8,128)(2,1)}, f32[1,256,256]{2,1,0:T(8,128)}) custom-call(s32[6]{0:T(128)} %and_convert_fusion.flags_ref, bf16[256,4096]{1,0:T(8,128)(2,1)} %q_ref.7, bf16[256,4096]{1,0:T(8,128)(2,1)} %do_ref.7, bf16[256,4096]{1,0:T(8,128)(2,1)} %o_ref.7, f32[32,256]{1,0:T(8,128)} %lse_ref.7, ...), custom_call_target="tpu_custom_call", output_to_operand_aliasing={{0}: (8, {})} | custom-call | tf_op jit(solution)/shard_map/pallas_call | solution.py:180
  60.3 3.3 %collective-permute-done.3 = bf16[256,512]{1,0:T(8,128)(2,1)S(1)} collective-permute-done((bf16[256,512]{1,0:T(8,128)(2,1)S(1)}, bf16[256,512]{1,0:T(8,128)(2,1)S(1)}, u32[]{:S(2)}, u32[]{:S(2)}) %collective-permute-start.3) | collective-permute-done | bytes 262176 | tf_op jit(solution)/shard_map/ppermute | solution.py:20
  63.6 1.0 %fusion = f32[256,512]{1,0:T(8,128)S(1)} fusion(f32[256,256]{1,0:T(8,128)} %bitcast.12, f32[256,256]{1,0:T(8,128)S(1)} %bitcast.11, bf16[256,512]{1,0:T(8,128)(2,1)S(1)} %collective-permute-done.3, bf16[256,512]{1,0:T(8,128)(2,1)S(1)} %collective-permute-done.2), kind=kLoop, calls=%fused_computation.2 | loop fusion | flops 655360 | bytes 1572864 | tf_op jit(solution)/shard_map/add | solution.py:228
  64.6 0.3 reshape.85
  64.9 0.2 slice.17
  65.1 0.3 slice.18
  65.4 0.1 copy.30
  65.5 0.8 %copy.28 = bf16[256,256]{1,0:T(8,128)(2,1)} copy(bf16[256,256]{0,1:T(8,128)(2,1)S(1)} %bitcast.9) | data formatting | bytes 262144
  66.3 0.1 copy.29
  66.5 0.8 %copy.27 = bf16[256,256]{1,0:T(8,128)(2,1)} copy(bf16[256,256]{0,1:T(8,128)(2,1)S(1)} %bitcast.10) | data formatting | bytes 262144
  (16 shorter events, 0.1 us)
Async XLA Ops:
  0.6 8.7 %copy-start.4 = (s32[16]{0:T(128)S(1)}, s32[16]{0:T(128)}, u32[]{:S(2)}) copy-start(s32[16]{0:T(128)} %param.13) | copy-start | bytes 196
  3.9 8.9 %copy-start = (bf16[256,512]{1,0:T(8,128)(2,1)}, bf16[256,512]{1,0:T(8,128)(2,1)S(1)}, u32[]{:S(2)}) copy-start(bf16[256,512]{1,0:T(8,128)(2,1)S(1)} %reshape.84.rest_0_) | copy-start | bytes 786436
  3.9 16.5 %collective-permute-start.1 = (bf16[256,512]{1,0:T(8,128)(2,1)S(1)}, bf16[256,512]{1,0:T(8,128)(2,1)S(1)}, u32[]{:S(2)}, u32[]{:S(2)}) collective-permute-start(bf16[256,512]{1,0:T(8,128)(2,1)S(1)} %reshape.84.rest_0_), channel_id=1, source_target_pairs={{0,1},{1,2},{2,3},{3,4},{4,5},{5,6},{6,7},{7,8},{8,9},{9,10},{10,1... | collective-permute-start | bytes 786440 | tf_op jit(solution)/shard_map/ppermute | solution.py:20
  5.8 14.5 %collective-permute-start = (bf16[256,512]{1,0:T(8,128)(2,1)S(1)}, bf16[256,512]{1,0:T(8,128)(2,1)S(1)}, u32[]{:S(2)}, u32[]{:S(2)}) collective-permute-start(bf16[256,512]{1,0:T(8,128)(2,1)S(1)} %reshape.84.rest_0_), channel_id=1, source_target_pairs={{0,2},{1,3},{2,4},{3,5},{4,6},{5,7},{6,8},{7,9},{8,10},{9,11},{10,... | collective-permute-start | bytes 786440 | tf_op jit(solution)/shard_map/ppermute | solution.py:20
  20.4 0.7 %copy-start.1 = (bf16[256,512]{1,0:T(8,128)(2,1)}, bf16[256,512]{1,0:T(8,128)(2,1)S(1)}, u32[]{:S(2)}) copy-start(bf16[256,512]{1,0:T(8,128)(2,1)S(1)} %collective-permute-done.1.rest_1_) | copy-start | bytes 786436
  20.4 0.8 %copy-start.2 = (bf16[256,512]{1,0:T(8,128)(2,1)}, bf16[256,512]{1,0:T(8,128)(2,1)S(1)}, u32[]{:S(2)}) copy-start(bf16[256,512]{1,0:T(8,128)(2,1)S(1)} %collective-permute-done.rest_0_) | copy-start | bytes 786436
  40.6 19.7 %collective-permute-start.2 = (bf16[256,512]{1,0:T(8,128)(2,1)S(1)}, bf16[256,512]{1,0:T(8,128)(2,1)S(1)}, u32[]{:S(2)}, u32[]{:S(2)}) collective-permute-start(bf16[256,512]{1,0:T(8,128)(2,1)S(1)} %get-tuple-element.27), channel_id=1, source_target_pairs={{1,0},{2,1},{3,2},{4,3},{5,4},{6,5},{7,6},{8,7},{9,8},{10,9},{11,1... | collective-permute-start | bytes 786440 | tf_op jit(solution)/shard_map/ppermute | solution.py:20
  43.9 19.6 %collective-permute-start.3 = (bf16[256,512]{1,0:T(8,128)(2,1)S(1)}, bf16[256,512]{1,0:T(8,128)(2,1)S(1)}, u32[]{:S(2)}, u32[]{:S(2)}) collective-permute-start(bf16[256,512]{1,0:T(8,128)(2,1)S(1)} %get-tuple-element.28), channel_id=1, source_target_pairs={{2,0},{3,1},{4,2},{5,3},{6,4},{7,5},{8,6},{9,7},{10,8},{11,9},{12,... | collective-permute-start | bytes 786440 | tf_op jit(solution)/shard_map/ppermute | solution.py:20
  52.4 11.2 %copy-start.3 = (f32[1,256,256]{2,1,0:T(8,128)S(1)}, f32[1,256,256]{2,1,0:T(8,128)}, u32[]{:S(2)}) copy-start(f32[1,256,256]{2,1,0:T(8,128)} %get-tuple-element.16) | copy-start | bytes 786436

commit v4 on v3

--- a/solution.py
+++ b/solution.py
@@ -24,7 +24,6 @@
     hb = HEADS_PER_STEP
     pieces = list(range(reach)) if remote else [reach]
     tiles_per_piece = tok // KEY_TILE
-    n_rows = len(pieces) * tok
     scale = 1.0 / math.sqrt(HD)
 
     def kernel(flags_ref, q_ref, do_ref, o_ref, lse_ref, bias_ref, *rest):
@@ -34,7 +33,7 @@
         rest = rest[n_alias:]
         dq_ref = rest.pop(0)
         dkv_ref = rest.pop(0)
-        qs_scr, dos_scr, dqt_scr, kt_scr, acc_scr = rest[-5:]
+        qs_scr, dos_scr, dl_scr, ds_scr, dq_scr, kt_scr, acc_scr = rest[-7:]
         b = pl.program_id(0)
         nb = pl.num_programs(0)
 
@@ -45,49 +44,56 @@
                 kt_scr[:, n * tok:(n + 1) * tok] = (
                     kv[:, :HD].astype(jnp.float32).T.astype(jnp.bfloat16))
 
-        delta_rows = []
         for i in range(hb):
             cols = slice(i * HD, (i + 1) * HD)
             qs_scr[i * tok:(i + 1) * tok, :] = q_ref[:, cols]
             dos_scr[i * tok:(i + 1) * tok, :] = do_ref[:, cols]
             prod = do_ref[:, cols].astype(jnp.float32) * o_ref[:, cols].astype(jnp.float32)
-            delta_rows.append(jnp.sum(prod.T, axis=0, keepdims=True))
-        dl_row = jnp.concatenate(delta_rows, axis=1)
-        lse_row = jnp.concatenate([lse_ref[i:i + 1, :] for i in range(hb)], axis=1)
-        dqt_scr[...] = jnp.zeros_like(dqt_scr)
-
-        for n, piece in enumerate(pieces):
-            kv = kv_refs[n]
-            for t in range(tiles_per_piece):
-                j = piece * tiles_per_piece + t
-                rows = slice(t * KEY_TILE, (t + 1) * KEY_TILE)
-                loc_rows = slice(n * tok + t * KEY_TILE, n * tok + (t + 1) * KEY_TILE)
-
-                def tile(kv=kv, rows=rows, loc_rows=loc_rows, n=n):
-                    k = kv[rows, :HD]
-                    v = kv[rows, HD:]
-                    qs = qs_scr[...]
-                    dos = dos_scr[...]
-                    st = lax.dot_general(k, qs, NT_DIMS, preferred_element_type=jnp.float32)
-                    bias = bias_ref[loc_rows, :]
-                    p = jnp.exp(st * scale - lse_row + jnp.concatenate([bias] * hb, axis=1))
-                    dv = jnp.dot(p.astype(jnp.bfloat16), dos, preferred_element_type=jnp.float32)
-                    dpt = lax.dot_general(v, dos, NT_DIMS, preferred_element_type=jnp.float32)
-                    ds = (p * (dpt - dl_row)).astype(jnp.bfloat16)
-                    dk = jnp.dot(ds, qs, preferred_element_type=jnp.float32)
-                    acc_scr[n, rows, :HD] += dk
-                    acc_scr[n, rows, HD:] += dv
-                    dqt_scr[...] += jnp.dot(
-                        kt_scr[:, loc_rows], ds, preferred_element_type=jnp.float32)
-
-                if remote:
-                    pl.when(flags_ref[j] != 0)(tile)
-                else:
-                    tile()
+            dl_scr[i:i + 1, :] = jnp.sum(prod.T, axis=0, keepdims=True)
+
+        def head(i, carry):
+            r0 = pl.multiple_of(i * tok, tok)
+            q = qs_scr[pl.ds(r0, tok), :]
+            do = dos_scr[pl.ds(r0, tok), :]
+            lse = lse_ref[pl.ds(i, 1), :]
+            dl = dl_scr[pl.ds(i, 1), :]
+            for n, piece in enumerate(pieces):
+                kv = kv_refs[n]
+                for t in range(tiles_per_piece):
+                    j = piece * tiles_per_piece + t
+                    rows = slice(t * KEY_TILE, (t + 1) * KEY_TILE)
+                    loc_rows = slice(n * tok + t * KEY_TILE, n * tok + (t + 1) * KEY_TILE)
+
+                    def tile(kv=kv, rows=rows, loc_rows=loc_rows, n=n):
+                        k = kv[rows, :HD]
+                        v = kv[rows, HD:]
+                        st = lax.dot_general(k, q, NT_DIMS, preferred_element_type=jnp.float32)
+                        p = jnp.exp(st * scale - lse + bias_ref[loc_rows, :])
+                        acc_scr[n, rows, HD:] += jnp.dot(
+                            p.astype(jnp.bfloat16), do, preferred_element_type=jnp.float32)
+                        dpt = lax.dot_general(v, do, NT_DIMS, preferred_element_type=jnp.float32)
+                        ds = (p * (dpt - dl)).astype(jnp.bfloat16)
+                        acc_scr[n, rows, :HD] += jnp.dot(
+                            ds, q, preferred_element_type=jnp.float32)
+                        ds_scr[loc_rows, :] = ds
+
+                    def skip(loc_rows=loc_rows):
+                        ds_scr[loc_rows, :] = jnp.zeros((KEY_TILE, tok), jnp.bfloat16)
+
+                    if remote:
+                        pl.when(flags_ref[j] != 0)(tile)
+                        pl.when(flags_ref[j] == 0)(skip)
+                    else:
+                        tile()
+            dqt = jnp.dot(kt_scr[...], ds_scr[...], preferred_element_type=jnp.float32)
+            dq_scr[pl.ds(r0, tok), :] = dqt.T
+            return carry
+
+        lax.fori_loop(0, hb, head, 0)
 
         for i in range(hb):
             cols = slice(i * HD, (i + 1) * HD)
-            part = dqt_scr[:, i * tok:(i + 1) * tok].T
+            part = dq_scr[i * tok:(i + 1) * tok, :]
             if dq_in:
                 part = part + dqp_ref[:, cols]
             if dq_final:
@@ -172,7 +178,9 @@
         scratch_shapes=[
             pltpu.VMEM((hb * tok, HD), jnp.bfloat16),
             pltpu.VMEM((hb * tok, HD), jnp.bfloat16),
-            pltpu.VMEM((HD, hb * tok), jnp.float32),
+            pltpu.VMEM((hb, tok), jnp.float32),
+            pltpu.VMEM((n_pieces * tok, tok), jnp.bfloat16),
+            pltpu.VMEM((hb * tok, HD), jnp.float32),
             pltpu.VMEM((HD, n_pieces * tok), jnp.bfloat16),
             pltpu.VMEM((n_pieces, tok, 2 * HD), jnp.float32),
         ],

time: 67.6 us -> 135 us (2.00)
  the two profiles are of different devices: /device:TPU:22 before, /device:TPU:12 now
where the time goes in v4:
time: 135 us; the launch traced here: 132 us
  Pallas kernels  66 us (49%)
  starting transfers between devices  53.3 us (39%)
  local copies, waits for them, and re-layouts  7.13 us (5%)
  other arithmetic  5.06 us (4%)
    pallas_call x4, Pallas kernels, grads_call(): pl.pallas_call(kernel, grid_spec=grid_spec, out_shape=[dq_shape, dkv_shap...  66 us
    ppermute x4, starting transfers between devices, shifted(): return lax.ppermute(block, axis, route)  53.3 us
  transfers between devices with their start and end apart: 4, of which 0 were waited for; matrix products, arithmetic and copies ran while one was open for 3% of the time, Pallas kernels for 23%

profile of v4, /device:TPU:12, one launch (start us, length us, event | category | flops | bytes accessed | tf_op | source)
XLA Modules:
  0.0 132.4 jit_solution(3460232197496797949)
XLA Ops:
  0.6 1.3 reshape.86
  1.9 1.3 reshape.87
  3.2 0.6 pad_maximum_fusion
  3.8 0.1 reshape.84.rest_0_
  3.9 1.9 %collective-permute-start.1 = (bf16[256,512]{1,0:T(8,128)(2,1)S(1)}, bf16[256,512]{1,0:T(8,128)(2,1)S(1)}, u32[]{:S(2)}, u32[]{:S(2)}) collective-permute-start(bf16[256,512]{1,0:T(8,128)(2,1)S(1)} %reshape.84.rest_0_), channel_id=1, source_target_pairs={{0,1},{1,2},{2,3},{3,4},{4,5},{5,6},{6,7},{7,8},{8,9},{9,10},{10,1... | collective-permute-start | bytes 786440 | tf_op jit(solution)/shard_map/ppermute | solution.py:20
  5.8 3.4 %collective-permute-start = (bf16[256,512]{1,0:T(8,128)(2,1)S(1)}, bf16[256,512]{1,0:T(8,128)(2,1)S(1)}, u32[]{:S(2)}, u32[]{:S(2)}) collective-permute-start(bf16[256,512]{1,0:T(8,128)(2,1)S(1)} %reshape.84.rest_0_), channel_id=1, source_target_pairs={{0,2},{1,3},{2,4},{3,5},{4,6},{5,7},{6,8},{7,9},{8,10},{9,11},{10,... | collective-permute-start | bytes 786440 | tf_op jit(solution)/shard_map/ppermute | solution.py:20
  9.3 0.1 copy.22
  9.4 0.6 convert_reduce_fusion.2
  10.1 0.2 convert_reduce_fusion.3
  10.2 0.1 convert_reduce_fusion
  10.3 1.2 and_convert_fusion.flags_ref
  11.5 0.1 convert_reduce_fusion.1
  11.6 1.2 and_select_fusion.bias_ref
  12.8 15.1 %shard_map.94 = (f32[256,2048]{1,0:T(8,128)}, f32[1,256,256]{2,1,0:T(8,128)}) custom-call(s32[6]{0:T(128)} %and_convert_fusion.flags_ref, bf16[256,4096]{1,0:T(8,128)(2,1)} %q_ref.7, bf16[256,4096]{1,0:T(8,128)(2,1)} %do_ref.7, bf16[256,4096]{1,0:T(8,128)(2,1)} %o_ref.7, f32[32,256]{1,0:T(8,128)} %lse_ref.7, f32[768,256]{1,0:T(8,128)} %and_select_fusion.bias_ref, ...), custom_call_target="tpu_custom_call" | custom-call | tf_op jit(solution)/shard_map/pallas_call | solution.py:188
  27.9 0.0 collective-permute-done.rest_0_
  27.9 0.7 copy-done.1
  28.6 0.1 copy-done.2
  28.7 17.8 %shard_map.95 = (bf16[256,4096]{1,0:T(8,128)(2,1)}, bf16[2,256,512]{2,1,0:T(8,128)(2,1)}) custom-call(s32[6]{0:T(128)} %and_convert_fusion.flags_ref, bf16[256,4096]{1,0:T(8,128)(2,1)} %q_ref.7, bf16[256,4096]{1,0:T(8,128)(2,1)} %do_ref.7, bf16[256,4096]{1,0:T(8,128)(2,1)} %o_ref.7, f32[32,256]{1,0:T(8,128)} %lse_ref.7, f32[768,256]{1,0:T(8,128)} %and_select_fusion.bias_ref, ...), custom_call_target="tpu_custom_call" | custom-call | tf_op jit(solution)/shard_map/pallas_call | solution.py:188
  46.5 17.6 %shard_map.96 = (f32[256,2048]{1,0:T(8,128)}, bf16[2,256,512]{2,1,0:T(8,128)(2,1)}) custom-call(s32[6]{0:T(128)} %and_convert_fusion.flags_ref, bf16[256,4096]{1,0:T(8,128)(2,1)} %q_ref.7, bf16[256,4096]{1,0:T(8,128)(2,1)} %do_ref.7, bf16[256,4096]{1,0:T(8,128)(2,1)} %o_ref.7, f32[32,256]{1,0:T(8,128)} %lse_ref.7, ...), custom_call_target="tpu_custom_call", output_to_operand_aliasing={{1}: (8, {})} | custom-call | tf_op jit(solution)/shard_map/pallas_call | solution.py:188
  64.1 1.1 slice_bitcast_fusion.1
  65.2 17.9 %collective-permute-start.2 = (bf16[256,512]{1,0:T(8,128)(2,1)S(1)}, bf16[256,512]{1,0:T(8,128)(2,1)S(1)}, u32[]{:S(2)}, u32[]{:S(2)}) collective-permute-start(bf16[256,512]{1,0:T(8,128)(2,1)S(1)} %get-tuple-element.27), channel_id=1, source_target_pairs={{1,0},{2,1},{3,2},{4,3},{5,4},{6,5},{7,6},{8,7},{9,8},{10,9},{11,1... | collective-permute-start | bytes 786440 | tf_op jit(solution)/shard_map/ppermute | solution.py:20
  83.1 30.1 %collective-permute-start.3 = (bf16[256,512]{1,0:T(8,128)(2,1)S(1)}, bf16[256,512]{1,0:T(8,128)(2,1)S(1)}, u32[]{:S(2)}, u32[]{:S(2)}) collective-permute-start(bf16[256,512]{1,0:T(8,128)(2,1)S(1)} %get-tuple-element.28), channel_id=1, source_target_pairs={{2,0},{3,1},{4,2},{5,3},{6,4},{7,5},{8,6},{9,7},{10,8},{11,9},{12,... | collective-permute-start | bytes 786440 | tf_op jit(solution)/shard_map/ppermute | solution.py:20
  113.2 15.5 %shard_map.97 = (bf16[256,4096]{1,0:T(8,128)(2,1)}, f32[1,256,256]{2,1,0:T(8,128)}) custom-call(s32[6]{0:T(128)} %and_convert_fusion.flags_ref, bf16[256,4096]{1,0:T(8,128)(2,1)} %q_ref.7, bf16[256,4096]{1,0:T(8,128)(2,1)} %do_ref.7, bf16[256,4096]{1,0:T(8,128)(2,1)} %o_ref.7, f32[32,256]{1,0:T(8,128)} %lse_ref.7, ...), custom_call_target="tpu_custom_call", output_to_operand_aliasing={{0}: (8, {})} | custom-call | tf_op jit(solution)/shard_map/pallas_call | solution.py:188
  128.6 0.0 collective-permute-done.2
  128.7 1.0 fusion
  129.7 0.3 reshape.85
  130.1 0.2 slice.17
  130.2 0.3 slice.18
  130.5 0.1 copy.30
  130.7 0.8 copy.28
  131.4 0.1 copy.29
  131.6 0.8 copy.27
  (16 shorter events, 0.1 us)
Async XLA Ops:
  0.6 8.7 %copy-start.4 = (s32[16]{0:T(128)S(1)}, s32[16]{0:T(128)}, u32[]{:S(2)}) copy-start(s32[16]{0:T(128)} %param.13) | copy-start | bytes 196
  3.9 8.9 %copy-start = (bf16[256,512]{1,0:T(8,128)(2,1)}, bf16[256,512]{1,0:T(8,128)(2,1)S(1)}, u32[]{:S(2)}) copy-start(bf16[256,512]{1,0:T(8,128)(2,1)S(1)} %reshape.84.rest_0_) | copy-start | bytes 786436
  3.9 24.0 %collective-permute-start.1 = (bf16[256,512]{1,0:T(8,128)(2,1)S(1)}, bf16[256,512]{1,0:T(8,128)(2,1)S(1)}, u32[]{:S(2)}, u32[]{:S(2)}) collective-permute-start(bf16[256,512]{1,0:T(8,128)(2,1)S(1)} %reshape.84.rest_0_), channel_id=1, source_target_pairs={{0,1},{1,2},{2,3},{3,4},{4,5},{5,6},{6,7},{7,8},{8,9},{9,10},{10,1... | collective-permute-start | bytes 786440 | tf_op jit(solution)/shard_map/ppermute | solution.py:20
  5.8 22.1 %collective-permute-start = (bf16[256,512]{1,0:T(8,128)(2,1)S(1)}, bf16[256,512]{1,0:T(8,128)(2,1)S(1)}, u32[]{:S(2)}, u32[]{:S(2)}) collective-permute-start(bf16[256,512]{1,0:T(8,128)(2,1)S(1)} %reshape.84.rest_0_), channel_id=1, source_target_pairs={{0,2},{1,3},{2,4},{3,5},{4,6},{5,7},{6,8},{7,9},{8,10},{9,11},{10,... | collective-permute-start | bytes 786440 | tf_op jit(solution)/shard_map/ppermute | solution.py:20
  27.9 0.7 copy-start.1
  27.9 0.8 copy-start.2
  65.2 63.5 %collective-permute-start.2 = (bf16[256,512]{1,0:T(8,128)(2,1)S(1)}, bf16[256,512]{1,0:T(8,128)(2,1)S(1)}, u32[]{:S(2)}, u32[]{:S(2)}) collective-permute-start(bf16[256,512]{1,0:T(8,128)(2,1)S(1)} %get-tuple-element.27), channel_id=1, source_target_pairs={{1,0},{2,1},{3,2},{4,3},{5,4},{6,5},{7,6},{8,7},{9,8},{10,9},{11,1... | collective-permute-start | bytes 786440 | tf_op jit(solution)/shard_map/ppermute | solution.py:20
  83.1 45.6 %collective-permute-start.3 = (bf16[256,512]{1,0:T(8,128)(2,1)S(1)}, bf16[256,512]{1,0:T(8,128)(2,1)S(1)}, u32[]{:S(2)}, u32[]{:S(2)}) collective-permute-start(bf16[256,512]{1,0:T(8,128)(2,1)S(1)} %get-tuple-element.28), channel_id=1, source_target_pairs={{2,0},{3,1},{4,2},{5,3},{6,4},{7,5},{8,6},{9,7},{10,8},{11,9},{12,... | collective-permute-start | bytes 786440 | tf_op jit(solution)/shard_map/ppermute | solution.py:20
  113.1 15.5 %copy-start.3 = (f32[1,256,256]{2,1,0:T(8,128)S(1)}, f32[1,256,256]{2,1,0:T(8,128)}, u32[]{:S(2)}) copy-start(f32[1,256,256]{2,1,0:T(8,128)} %get-tuple-element.16) | copy-start | bytes 786436

commit v5 on v3

--- a/solution.py
+++ b/solution.py
@@ -24,7 +24,7 @@
     hb = HEADS_PER_STEP
     pieces = list(range(reach)) if remote else [reach]
     tiles_per_piece = tok // KEY_TILE
-    n_rows = len(pieces) * tok
+    sentinel = (reach + 1) * tiles_per_piece
     scale = 1.0 / math.sqrt(HD)
 
     def kernel(flags_ref, q_ref, do_ref, o_ref, lse_ref, bias_ref, *rest):
@@ -34,9 +34,10 @@
         rest = rest[n_alias:]
         dq_ref = rest.pop(0)
         dkv_ref = rest.pop(0)
-        qs_scr, dos_scr, dqt_scr, kt_scr, acc_scr = rest[-5:]
+        qs_scr, dos_scr, dl_scr, p_scr, ds_scr, kt_scr, acc_scr = rest[-7:]
         b = pl.program_id(0)
         nb = pl.num_programs(0)
+        always = flags_ref[sentinel] != 0
 
         @pl.when(b == 0)
         def _():
@@ -45,16 +46,12 @@
                 kt_scr[:, n * tok:(n + 1) * tok] = (
                     kv[:, :HD].astype(jnp.float32).T.astype(jnp.bfloat16))
 
-        delta_rows = []
         for i in range(hb):
             cols = slice(i * HD, (i + 1) * HD)
             qs_scr[i * tok:(i + 1) * tok, :] = q_ref[:, cols]
             dos_scr[i * tok:(i + 1) * tok, :] = do_ref[:, cols]
             prod = do_ref[:, cols].astype(jnp.float32) * o_ref[:, cols].astype(jnp.float32)
-            delta_rows.append(jnp.sum(prod.T, axis=0, keepdims=True))
-        dl_row = jnp.concatenate(delta_rows, axis=1)
-        lse_row = jnp.concatenate([lse_ref[i:i + 1, :] for i in range(hb)], axis=1)
-        dqt_scr[...] = jnp.zeros_like(dqt_scr)
+            dl_scr[i:i + 1, :] = jnp.sum(prod.T, axis=0, keepdims=True)
 
         for n, piece in enumerate(pieces):
             kv = kv_refs[n]
@@ -66,34 +63,45 @@
                 def tile(kv=kv, rows=rows, loc_rows=loc_rows, n=n):
                     k = kv[rows, :HD]
                     v = kv[rows, HD:]
-                    qs = qs_scr[...]
-                    dos = dos_scr[...]
-                    st = lax.dot_general(k, qs, NT_DIMS, preferred_element_type=jnp.float32)
-                    bias = bias_ref[loc_rows, :]
-                    p = jnp.exp(st * scale - lse_row + jnp.concatenate([bias] * hb, axis=1))
-                    dv = jnp.dot(p.astype(jnp.bfloat16), dos, preferred_element_type=jnp.float32)
-                    dpt = lax.dot_general(v, dos, NT_DIMS, preferred_element_type=jnp.float32)
-                    ds = (p * (dpt - dl_row)).astype(jnp.bfloat16)
-                    dk = jnp.dot(ds, qs, preferred_element_type=jnp.float32)
-                    acc_scr[n, rows, :HD] += dk
-                    acc_scr[n, rows, HD:] += dv
-                    dqt_scr[...] += jnp.dot(
-                        kt_scr[:, loc_rows], ds, preferred_element_type=jnp.float32)
-
+                    for i in range(hb):
+                        cols = slice(i * HD, (i + 1) * HD)
+                        qcols = slice(i * tok, (i + 1) * tok)
+                        st = lax.dot_general(
+                            k, q_ref[:, cols], NT_DIMS, preferred_element_type=jnp.float32)
+                        p = jnp.exp(st * scale - lse_ref[i:i + 1, :] + bias_ref[loc_rows, :])
+                        p_scr[:, qcols] = p.astype(jnp.bfloat16)
+                        dpt = lax.dot_general(
+                            v, do_ref[:, cols], NT_DIMS, preferred_element_type=jnp.float32)
+                        ds_scr[loc_rows, qcols] = (
+                            p * (dpt - dl_scr[i:i + 1, :])).astype(jnp.bfloat16)
+
+                    @pl.when(always)
+                    def _():
+                        acc_scr[n, rows, HD:] += jnp.dot(
+                            p_scr[...], dos_scr[...], preferred_element_type=jnp.float32)
+                        acc_scr[n, rows, :HD] += jnp.dot(
+                            ds_scr[loc_rows, :], qs_scr[...], preferred_element_type=jnp.float32)
+
+                def skip(loc_rows=loc_rows):
+                    ds_scr[loc_rows, :] = jnp.zeros((KEY_TILE, hb * tok), jnp.bfloat16)
+
+                pl.when(flags_ref[j] != 0)(tile)
                 if remote:
-                    pl.when(flags_ref[j] != 0)(tile)
+                    pl.when(flags_ref[j] == 0)(skip)
+
+        @pl.when(always)
+        def _():
+            for i in range(hb):
+                cols = slice(i * HD, (i + 1) * HD)
+                dqt = jnp.dot(kt_scr[...], ds_scr[:, i * tok:(i + 1) * tok],
+                              preferred_element_type=jnp.float32)
+                part = dqt.T
+                if dq_in:
+                    part = part + dqp_ref[:, cols]
+                if dq_final:
+                    dq_ref[:, cols] = (part * scale).astype(dq_ref.dtype)
                 else:
-                    tile()
-
-        for i in range(hb):
-            cols = slice(i * HD, (i + 1) * HD)
-            part = dqt_scr[:, i * tok:(i + 1) * tok].T
-            if dq_in:
-                part = part + dqp_ref[:, cols]
-            if dq_final:
-                dq_ref[:, cols] = (part * scale).astype(dq_ref.dtype)
-            else:
-                dq_ref[:, cols] = part
+                    dq_ref[:, cols] = part
 
         @pl.when(b == nb - 1)
         def _():
@@ -172,7 +180,9 @@
         scratch_shapes=[
             pltpu.VMEM((hb * tok, HD), jnp.bfloat16),
             pltpu.VMEM((hb * tok, HD), jnp.bfloat16),
-            pltpu.VMEM((HD, hb * tok), jnp.float32),
+            pltpu.VMEM((hb, tok), jnp.float32),
+            pltpu.VMEM((KEY_TILE, hb * tok), jnp.bfloat16),
+            pltpu.VMEM((n_pieces * tok, hb * tok), jnp.bfloat16),
             pltpu.VMEM((HD, n_pieces * tok), jnp.bfloat16),
             pltpu.VMEM((n_pieces, tok, 2 * HD), jnp.float32),
         ],
@@ -209,7 +219,10 @@
     last_places = (position - reach) * tok + KEY_TILE * jnp.arange(
         1, n_tiles + 1, dtype=jnp.int32) - 1
     first_doc = doc_of(position[None] * tok)
-    flags = ((doc_of(last_places) == first_doc) & (last_places >= 0)).astype(jnp.int32)
+    flags = jnp.concatenate([
+        ((doc_of(last_places) == first_doc) & (last_places >= 0))
+        | (jnp.arange(n_tiles) >= reach * tok // KEY_TILE),
+        jnp.ones((1,), jnp.bool_)]).astype(jnp.int32)
 
     kv = jnp.concatenate(
         [keys.reshape(tok, kvh, 1, HD), values.reshape(tok, kvh, 1, HD)], axis=2

time: 67.6 us -> 70.7 us (1.046)
  the two profiles are of different devices: /device:TPU:22 before, /device:TPU:12 now
where the time goes in v5:
time: 70.7 us; the launch traced here: 70.4 us
  Pallas kernels  41.7 us (59%)
  starting transfers between devices  15.5 us (22%)
  local copies, waits for them, and re-layouts  7.13 us (10%)
  other arithmetic  5.13 us (7%)
  between operations  0.88 us (1%)
    pallas_call x4, Pallas kernels, grads_call(): pl.pallas_call(kernel, grid_spec=grid_spec, out_shape=[dq_shape, dkv_shap...  41.7 us
    ppermute x4, starting transfers between devices, shifted(): return lax.ppermute(block, axis, route)  15.5 us
    unnamed x14, local copies, waits for them, and re-layouts  2.57 us
  transfers between devices with their start and end apart: 4, of which 0 were waited for; matrix products, arithmetic and copies ran while one was open for 5% of the time, Pallas kernels for 26%

profile of v5, /device:TPU:12, one launch (start us, length us, event | category | flops | bytes accessed | tf_op | source)
XLA Modules:
  0.0 70.4 jit_solution(6651036269400329360)
XLA Ops:
  0.6 1.3 %reshape.86 = bf16[256,2,1,128]{3,2,1,0:T(2,128)(2,1)S(1)} reshape(bf16[256,256]{1,0:T(8,128)(2,1)} %param.8) | data formatting | bytes 262144 | tf_op jit(solution)/shard_map/reshape | solution.py:228
  1.9 1.3 %reshape.87 = bf16[256,2,1,128]{3,2,1,0:T(2,128)(2,1)S(1)} reshape(bf16[256,256]{1,0:T(8,128)(2,1)} %param.9) | data formatting | bytes 262144 | tf_op jit(solution)/shard_map/reshape | solution.py:228
  3.2 0.6 pad_maximum_fusion
  3.8 0.1 reshape.84.rest_0_
  3.9 1.9 %collective-permute-start.1 = (bf16[256,512]{1,0:T(8,128)(2,1)S(1)}, bf16[256,512]{1,0:T(8,128)(2,1)S(1)}, u32[]{:S(2)}, u32[]{:S(2)}) collective-permute-start(bf16[256,512]{1,0:T(8,128)(2,1)S(1)} %reshape.84.rest_0_), channel_id=1, source_target_pairs={{0,1},{1,2},{2,3},{3,4},{4,5},{5,6},{6,7},{7,8},{8,9},{9,10},{10,1... | collective-permute-start | bytes 786440 | tf_op jit(solution)/shard_map/ppermute | solution.py:20
  5.8 3.4 %collective-permute-start = (bf16[256,512]{1,0:T(8,128)(2,1)S(1)}, bf16[256,512]{1,0:T(8,128)(2,1)S(1)}, u32[]{:S(2)}, u32[]{:S(2)}) collective-permute-start(bf16[256,512]{1,0:T(8,128)(2,1)S(1)} %reshape.84.rest_0_), channel_id=1, source_target_pairs={{0,2},{1,3},{2,4},{3,5},{4,6},{5,7},{6,8},{7,9},{8,10},{9,11},{10,... | collective-permute-start | bytes 786440 | tf_op jit(solution)/shard_map/ppermute | solution.py:20
  9.3 0.1 copy.22
  9.4 0.6 convert_reduce_fusion.2
  10.1 0.2 convert_reduce_fusion.3
  10.2 0.1 convert_reduce_fusion.1
  10.3 0.1 convert_reduce_fusion
  10.4 0.7 compare_or_fusion
  11.1 0.6 add_convert_fusion.flags_ref
  11.7 1.2 %and_select_fusion.bias_ref = f32[768,256]{1,0:T(8,128)} fusion(s32[256]{0:T(256)S(1)} %iota_add_fusion.1, s32[256]{0:T(256)S(1)} %convert_reduce_fusion.1, s32[768]{0:T(1024)S(1)} %iota_add_fusion, s32[768]{0:T(1024)S(1)} %compare_select_fusion), kind=kLoop, calls=%fused_computation | loop fusion | flops 786432 | bytes 794624 | tf_op jit(solution)/shard_map/jit(_where)/select_n | solution.py:217
  12.9 9.1 %shard_map.94 = (f32[256,2048]{1,0:T(8,128)}, f32[1,256,256]{2,1,0:T(8,128)}) custom-call(s32[7]{0:T(128)} %add_convert_fusion.flags_ref, bf16[256,4096]{1,0:T(8,128)(2,1)} %q_ref.7, bf16[256,4096]{1,0:T(8,128)(2,1)} %do_ref.7, bf16[256,4096]{1,0:T(8,128)(2,1)} %o_ref.7, f32[32,256]{1,0:T(8,128)} %lse_ref.7, f32[768,256]{1,0:T(8,128)} %and_select_fusion.bias_ref, ...), custom_call_target="tpu_custom_call" | custom-call | tf_op jit(solution)/shard_map/pallas_call | solution.py:190
  22.0 0.0 collective-permute-done.1.rest_1_
  22.0 0.7 copy-done.1
  22.7 0.1 copy-done.2
  22.8 11.5 %shard_map.95 = (bf16[256,4096]{1,0:T(8,128)(2,1)}, bf16[2,256,512]{2,1,0:T(8,128)(2,1)}) custom-call(s32[7]{0:T(128)} %add_convert_fusion.flags_ref, bf16[256,4096]{1,0:T(8,128)(2,1)} %q_ref.7, bf16[256,4096]{1,0:T(8,128)(2,1)} %do_ref.7, bf16[256,4096]{1,0:T(8,128)(2,1)} %o_ref.7, f32[32,256]{1,0:T(8,128)} %lse_ref.7, f32[768,256]{1,0:T(8,128)} %and_select_fusion.bias_ref, ...), custom_call_target="tpu_custom_call" | custom-call | tf_op jit(solution)/shard_map/pallas_call | solution.py:190
  34.3 11.5 %shard_map.96 = (f32[256,2048]{1,0:T(8,128)}, bf16[2,256,512]{2,1,0:T(8,128)(2,1)}) custom-call(s32[7]{0:T(128)} %add_convert_fusion.flags_ref, bf16[256,4096]{1,0:T(8,128)(2,1)} %q_ref.7, bf16[256,4096]{1,0:T(8,128)(2,1)} %do_ref.7, bf16[256,4096]{1,0:T(8,128)(2,1)} %o_ref.7, f32[32,256]{1,0:T(8,128)} %lse_ref.7, ...), custom_call_target="tpu_custom_call", output_to_operand_aliasing={{1}: (8, {})} | custom-call | tf_op jit(solution)/shard_map/pallas_call | solution.py:190
  45.9 1.1 %slice_bitcast_fusion.1 = (bf16[256,512]{1,0:T(8,128)(2,1)S(1)}, bf16[256,512]{1,0:T(8,128)(2,1)S(1)}) fusion(bf16[2,256,512]{2,1,0:T(8,128)(2,1)} %get-tuple-element.18), kind=kLoop, calls=%fused_computation.6 | loop fusion | bytes 1048576 | tf_op jit(solution)/shard_map/squeeze | solution.py:236
  46.9 1.9 %collective-permute-start.2 = (bf16[256,512]{1,0:T(8,128)(2,1)S(1)}, bf16[256,512]{1,0:T(8,128)(2,1)S(1)}, u32[]{:S(2)}, u32[]{:S(2)}) collective-permute-start(bf16[256,512]{1,0:T(8,128)(2,1)S(1)} %get-tuple-element.27), channel_id=1, source_target_pairs={{1,0},{2,1},{3,2},{4,3},{5,4},{6,5},{7,6},{8,7},{9,8},{10,9},{11,1... | collective-permute-start | bytes 786440 | tf_op jit(solution)/shard_map/ppermute | solution.py:20
  48.9 8.3 %collective-permute-start.3 = (bf16[256,512]{1,0:T(8,128)(2,1)S(1)}, bf16[256,512]{1,0:T(8,128)(2,1)S(1)}, u32[]{:S(2)}, u32[]{:S(2)}) collective-permute-start(bf16[256,512]{1,0:T(8,128)(2,1)S(1)} %get-tuple-element.28), channel_id=1, source_target_pairs={{2,0},{3,1},{4,2},{5,3},{6,4},{7,5},{8,6},{9,7},{10,8},{11,9},{12,... | collective-permute-start | bytes 786440 | tf_op jit(solution)/shard_map/ppermute | solution.py:20
  57.2 9.5 %shard_map.97 = (bf16[256,4096]{1,0:T(8,128)(2,1)}, f32[1,256,256]{2,1,0:T(8,128)}) custom-call(s32[7]{0:T(128)} %add_convert_fusion.flags_ref, bf16[256,4096]{1,0:T(8,128)(2,1)} %q_ref.7, bf16[256,4096]{1,0:T(8,128)(2,1)} %do_ref.7, bf16[256,4096]{1,0:T(8,128)(2,1)} %o_ref.7, f32[32,256]{1,0:T(8,128)} %lse_ref.7, ...), custom_call_target="tpu_custom_call", output_to_operand_aliasing={{0}: (8, {})} | custom-call | tf_op jit(solution)/shard_map/pallas_call | solution.py:190
  66.7 1.0 %fusion = f32[256,512]{1,0:T(8,128)S(1)} fusion(f32[256,256]{1,0:T(8,128)} %bitcast.12, f32[256,256]{1,0:T(8,128)S(1)} %bitcast.11, bf16[256,512]{1,0:T(8,128)(2,1)S(1)} %collective-permute-done.3, bf16[256,512]{1,0:T(8,128)(2,1)S(1)} %collective-permute-done.2), kind=kLoop, calls=%fused_computation.2 | loop fusion | flops 655360 | bytes 1572864 | tf_op jit(solution)/shard_map/add | solution.py:241
  67.7 0.3 reshape.85
  68.1 0.2 slice.17
  68.2 0.3 slice.18
  68.5 0.1 copy.30
  68.7 0.8 %copy.28 = bf16[256,256]{1,0:T(8,128)(2,1)} copy(bf16[256,256]{0,1:T(8,128)(2,1)S(1)} %bitcast.9) | data formatting | bytes 262144
  69.4 0.1 copy.29
  69.6 0.8 %copy.27 = bf16[256,256]{1,0:T(8,128)(2,1)} copy(bf16[256,256]{0,1:T(8,128)(2,1)S(1)} %bitcast.10) | data formatting | bytes 262144
  (17 shorter events, 0.1 us)
Async XLA Ops:
  0.6 8.7 %copy-start.4 = (s32[16]{0:T(128)S(1)}, s32[16]{0:T(128)}, u32[]{:S(2)}) copy-start(s32[16]{0:T(128)} %param.13) | copy-start | bytes 196
  3.9 9.0 %copy-start = (bf16[256,512]{1,0:T(8,128)(2,1)}, bf16[256,512]{1,0:T(8,128)(2,1)S(1)}, u32[]{:S(2)}) copy-start(bf16[256,512]{1,0:T(8,128)(2,1)S(1)} %reshape.84.rest_0_) | copy-start | bytes 786436
  3.9 18.1 %collective-permute-start.1 = (bf16[256,512]{1,0:T(8,128)(2,1)S(1)}, bf16[256,512]{1,0:T(8,128)(2,1)S(1)}, u32[]{:S(2)}, u32[]{:S(2)}) collective-permute-start(bf16[256,512]{1,0:T(8,128)(2,1)S(1)} %reshape.84.rest_0_), channel_id=1, source_target_pairs={{0,1},{1,2},{2,3},{3,4},{4,5},{5,6},{6,7},{7,8},{8,9},{9,10},{10,1... | collective-permute-start | bytes 786440 | tf_op jit(solution)/shard_map/ppermute | solution.py:20
  5.8 16.2 %collective-permute-start = (bf16[256,512]{1,0:T(8,128)(2,1)S(1)}, bf16[256,512]{1,0:T(8,128)(2,1)S(1)}, u32[]{:S(2)}, u32[]{:S(2)}) collective-permute-start(bf16[256,512]{1,0:T(8,128)(2,1)S(1)} %reshape.84.rest_0_), channel_id=1, source_target_pairs={{0,2},{1,3},{2,4},{3,5},{4,6},{5,7},{6,8},{7,9},{8,10},{9,11},{10,... | collective-permute-start | bytes 786440 | tf_op jit(solution)/shard_map/ppermute | solution.py:20
  22.0 0.7 copy-start.1
  22.0 0.8 %copy-start.2 = (bf16[256,512]{1,0:T(8,128)(2,1)}, bf16[256,512]{1,0:T(8,128)(2,1)S(1)}, u32[]{:S(2)}) copy-start(bf16[256,512]{1,0:T(8,128)(2,1)S(1)} %collective-permute-done.rest_0_) | copy-start | bytes 786436
  46.9 19.7 %collective-permute-start.2 = (bf16[256,512]{1,0:T(8,128)(2,1)S(1)}, bf16[256,512]{1,0:T(8,128)(2,1)S(1)}, u32[]{:S(2)}, u32[]{:S(2)}) collective-permute-start(bf16[256,512]{1,0:T(8,128)(2,1)S(1)} %get-tuple-element.27), channel_id=1, source_target_pairs={{1,0},{2,1},{3,2},{4,3},{5,4},{6,5},{7,6},{8,7},{9,8},{10,9},{11,1... | collective-permute-start | bytes 786440 | tf_op jit(solution)/shard_map/ppermute | solution.py:20
  48.9 17.8 %collective-permute-start.3 = (bf16[256,512]{1,0:T(8,128)(2,1)S(1)}, bf16[256,512]{1,0:T(8,128)(2,1)S(1)}, u32[]{:S(2)}, u32[]{:S(2)}) collective-permute-start(bf16[256,512]{1,0:T(8,128)(2,1)S(1)} %get-tuple-element.28), channel_id=1, source_target_pairs={{2,0},{3,1},{4,2},{5,3},{6,4},{7,5},{8,6},{9,7},{10,8},{11,9},{12,... | collective-permute-start | bytes 786440 | tf_op jit(solution)/shard_map/ppermute | solution.py:20
  57.1 9.5 %copy-start.3 = (f32[1,256,256]{2,1,0:T(8,128)S(1)}, f32[1,256,256]{2,1,0:T(8,128)}, u32[]{:S(2)}) copy-start(f32[1,256,256]{2,1,0:T(8,128)} %get-tuple-element.16) | copy-start | bytes 786436

commit v6 on v3

--- a/solution.py
+++ b/solution.py
@@ -212,8 +212,8 @@
     flags = ((doc_of(last_places) == first_doc) & (last_places >= 0)).astype(jnp.int32)
 
     kv = jnp.concatenate(
-        [keys.reshape(tok, kvh, 1, HD), values.reshape(tok, kvh, 1, HD)], axis=2
-    ).reshape(tok, kvh * 2 * HD)
+        [part for g in range(kvh)
+         for part in (keys[:, g * HD:(g + 1) * HD], values[:, g * HD:(g + 1) * HD])], axis=1)
     kv_pieces = [kv] + [shifted(kv, "seq", hop) for hop in range(1, reach + 1)]
     common = (flags, queries, out_grad, outputs, logsumexp, bias, kv_pieces, reach)
 
@@ -226,9 +226,10 @@
     total = jnp.concatenate([dkv_own0[0], dkv_own1[0]], axis=1)
     for r in returned:
         total = total + r.astype(jnp.float32)
-    total = total.reshape(tok, kvh, 2, HD)
-    key_total = total[:, :, 0, :].reshape(tok, kvh * HD)
-    value_total = total[:, :, 1, :].reshape(tok, kvh * HD)
+    key_total = jnp.concatenate(
+        [total[:, (2 * g) * HD:(2 * g + 1) * HD] for g in range(kvh)], axis=1)
+    value_total = jnp.concatenate(
+        [total[:, (2 * g + 1) * HD:(2 * g + 2) * HD] for g in range(kvh)], axis=1)
     return (
         dq,
         (key_total * scale).astype(jnp.bfloat16),

time: 67.6 us -> 63.7 us (0.942)
  the two profiles are of different devices: /device:TPU:22 before, /device:TPU:12 now
where the time goes in v6:
time: 63.7 us; the launch traced here: 63.4 us
  Pallas kernels  37.5 us (59%)
  starting transfers between devices  15.7 us (25%)
  other arithmetic  5.84 us (9%)
  local copies, waits for them, and re-layouts  3.57 us (6%)
  between operations  0.81 us (1%)
    pallas_call x4, Pallas kernels, grads_call(): pl.pallas_call(kernel, grid_spec=grid_spec, out_shape=[dq_shape, dkv_shap...  37.5 us
    ppermute x4, starting transfers between devices, shifted(): return lax.ppermute(block, axis, route)  15.7 us
  transfers between devices with their start and end apart: 4, of which 0 were waited for; matrix products, arithmetic and copies ran while one was open for 7% of the time, Pallas kernels for 24%

profile of v6, /device:TPU:12, one launch (start us, length us, event | category | flops | bytes accessed | tf_op | source)
XLA Modules:
  0.0 63.4 jit_solution(6290562672806310821)
XLA Ops:
  0.6 1.0 %fusion.6 = (bf16[256,128]{1,0:T(8,128)(2,1)S(1)}, bf16[256,128]{1,0:T(8,128)(2,1)S(1)}, bf16[256,128]{1,0:T(8,128)(2,1)S(1)}, bf16[256,128]{1,0:T(8,128)(2,1)S(1)}) fusion(bf16[256,256]{1,0:T(8,128)(2,1)} %param.8, bf16[256,256]{1,0:T(8,128)(2,1)} %param.9), kind=kLoop, calls=%fused_computation.21 | loop fusion | bytes 524288 | tf_op jit(solution)/shard_map/slice | solution.py:216
  1.6 0.0 copy-start
  1.6 1.9 %collective-permute-start.1 = (bf16[256,512]{1,0:T(8,128)(2,1)S(1)}, bf16[256,512]{1,0:T(8,128)(2,1)S(1)}, u32[]{:S(2)}, u32[]{:S(2)}) collective-permute-start(bf16[256,512]{1,0:T(8,128)(2,1)S(1)} %pad_maximum_fusion.rest_0_), channel_id=1, source_target_pairs={{0,1},{1,2},{2,3},{3,4},{4,5},{5,6},{6,7},{7,8},{8,9},{9,10},{10,1... | collective-permute-start | bytes 786440 | tf_op jit(solution)/shard_map/ppermute | solution.py:20
  3.6 3.4 %collective-permute-start = (bf16[256,512]{1,0:T(8,128)(2,1)S(1)}, bf16[256,512]{1,0:T(8,128)(2,1)S(1)}, u32[]{:S(2)}, u32[]{:S(2)}) collective-permute-start(bf16[256,512]{1,0:T(8,128)(2,1)S(1)} %pad_maximum_fusion.rest_0_), channel_id=1, source_target_pairs={{0,2},{1,3},{2,4},{3,5},{4,6},{5,7},{6,8},{7,9},{8,10},{9,11},{10,... | collective-permute-start | bytes 786440 | tf_op jit(solution)/shard_map/ppermute | solution.py:20
  7.0 0.7 %copy.14 = s32[16,1]{1,0:T(8,128)S(1)} copy(s32[16,1]{0,1:T(1,128)} %bitcast.9) | data formatting | bytes 128 | tf_op jit(solution)/shard_map/reshape
  7.8 0.6 %convert_reduce_fusion.2 = (s32[]{:T(128)}, s32[16]{0:T(128)S(1)}) fusion(s32[16,1]{1,0:T(8,128)S(1)} %reduce-window.4, s32[]{:T(128)S(6)} %mul.24), kind=kLoop, calls=%fused_computation.11 | loop fusion | flops 47 | bytes 136 | tf_op jit(solution)/shard_map/reduce_sum | solution.py:199
  8.5 0.2 convert_reduce_fusion.3
  8.6 0.1 convert_reduce_fusion
  8.7 1.2 %and_convert_fusion.flags_ref = s32[6]{0:T(128)} fusion(s32[6]{0:T(128)S(1)} %convert_reduce_fusion.3, s32[]{:T(128)} %get-tuple-element.19, s32[]{:T(128)S(6)} %mul.22), kind=kLoop, calls=%fused_computation.15 | loop fusion | flops 48 | bytes 56 | tf_op jit(solution)/shard_map/convert_element_type | solution.py:212
  9.9 0.1 convert_reduce_fusion.1
  10.0 1.2 %and_select_fusion.bias_ref = f32[768,256]{1,0:T(8,128)} fusion(s32[256]{0:T(256)S(1)} %iota_add_fusion.1, s32[256]{0:T(256)S(1)} %convert_reduce_fusion.1, s32[768]{0:T(1024)S(1)} %iota_add_fusion, s32[768]{0:T(1024)S(1)} %compare_select_fusion), kind=kLoop, calls=%fused_computation | loop fusion | flops 786432 | bytes 794624 | tf_op jit(solution)/shard_map/jit(_where)/select_n | solution.py:207
  11.2 0.0 copy-done
  11.2 7.6 %shard_map.94 = (f32[256,2048]{1,0:T(8,128)}, f32[1,256,256]{2,1,0:T(8,128)}) custom-call(s32[6]{0:T(128)} %and_convert_fusion.flags_ref, bf16[256,4096]{1,0:T(8,128)(2,1)} %q_ref.7, bf16[256,4096]{1,0:T(8,128)(2,1)} %do_ref.7, bf16[256,4096]{1,0:T(8,128)(2,1)} %o_ref.7, f32[32,256]{1,0:T(8,128)} %lse_ref.7, f32[768,256]{1,0:T(8,128)} %and_select_fusion.bias_ref, ...), custom_call_target="tpu_custom_call" | custom-call | tf_op jit(solution)/shard_map/pallas_call | solution.py:180
  18.8 0.0 collective-permute-done.1.rest_1_
  18.8 0.0 copy-start.1
  18.8 0.0 collective-permute-done.rest_0_
  18.8 0.0 copy-start.2
  18.8 0.7 %copy-done.1 = bf16[256,512]{1,0:T(8,128)(2,1)} copy-done((bf16[256,512]{1,0:T(8,128)(2,1)}, bf16[256,512]{1,0:T(8,128)(2,1)S(1)}, u32[]{:S(2)}) %copy-start.1) | copy-done | bytes 262168
  19.5 0.1 copy-done.2
  19.6 11.0 %shard_map.95 = (bf16[256,4096]{1,0:T(8,128)(2,1)}, bf16[2,256,512]{2,1,0:T(8,128)(2,1)}) custom-call(s32[6]{0:T(128)} %and_convert_fusion.flags_ref, bf16[256,4096]{1,0:T(8,128)(2,1)} %q_ref.7, bf16[256,4096]{1,0:T(8,128)(2,1)} %do_ref.7, bf16[256,4096]{1,0:T(8,128)(2,1)} %o_ref.7, f32[32,256]{1,0:T(8,128)} %lse_ref.7, f32[768,256]{1,0:T(8,128)} %and_select_fusion.bias_ref, ...), custom_call_target="tpu_custom_call" | custom-call | tf_op jit(solution)/shard_map/pallas_call | solution.py:180
  30.6 10.9 %shard_map.96 = (f32[256,2048]{1,0:T(8,128)}, bf16[2,256,512]{2,1,0:T(8,128)(2,1)}) custom-call(s32[6]{0:T(128)} %and_convert_fusion.flags_ref, bf16[256,4096]{1,0:T(8,128)(2,1)} %q_ref.7, bf16[256,4096]{1,0:T(8,128)(2,1)} %do_ref.7, bf16[256,4096]{1,0:T(8,128)(2,1)} %o_ref.7, f32[32,256]{1,0:T(8,128)} %lse_ref.7, ...), custom_call_target="tpu_custom_call", output_to_operand_aliasing={{1}: (8, {})} | custom-call | tf_op jit(solution)/shard_map/pallas_call | solution.py:180
  41.5 1.1 %slice_bitcast_fusion.1 = (bf16[256,512]{1,0:T(8,128)(2,1)S(1)}, bf16[256,512]{1,0:T(8,128)(2,1)S(1)}) fusion(bf16[2,256,512]{2,1,0:T(8,128)(2,1)} %get-tuple-element.18), kind=kLoop, calls=%fused_computation.7 | loop fusion | bytes 1048576 | tf_op jit(solution)/shard_map/squeeze | solution.py:223
  42.6 1.9 %collective-permute-start.2 = (bf16[256,512]{1,0:T(8,128)(2,1)S(1)}, bf16[256,512]{1,0:T(8,128)(2,1)S(1)}, u32[]{:S(2)}, u32[]{:S(2)}) collective-permute-start(bf16[256,512]{1,0:T(8,128)(2,1)S(1)} %get-tuple-element.25), channel_id=1, source_target_pairs={{1,0},{2,1},{3,2},{4,3},{5,4},{6,5},{7,6},{8,7},{9,8},{10,9},{11,1... | collective-permute-start | bytes 786440 | tf_op jit(solution)/shard_map/ppermute | solution.py:20
  44.5 8.4 %collective-permute-start.3 = (bf16[256,512]{1,0:T(8,128)(2,1)S(1)}, bf16[256,512]{1,0:T(8,128)(2,1)S(1)}, u32[]{:S(2)}, u32[]{:S(2)}) collective-permute-start(bf16[256,512]{1,0:T(8,128)(2,1)S(1)} %get-tuple-element.26), channel_id=1, source_target_pairs={{2,0},{3,1},{4,2},{5,3},{6,4},{7,5},{8,6},{9,7},{10,8},{11,9},{12,... | collective-permute-start | bytes 786440 | tf_op jit(solution)/shard_map/ppermute | solution.py:20
  53.0 0.0 copy-start.3
  53.0 7.9 %shard_map.97 = (bf16[256,4096]{1,0:T(8,128)(2,1)}, f32[1,256,256]{2,1,0:T(8,128)}) custom-call(s32[6]{0:T(128)} %and_convert_fusion.flags_ref, bf16[256,4096]{1,0:T(8,128)(2,1)} %q_ref.7, bf16[256,4096]{1,0:T(8,128)(2,1)} %do_ref.7, bf16[256,4096]{1,0:T(8,128)(2,1)} %o_ref.7, f32[32,256]{1,0:T(8,128)} %lse_ref.7, ...), custom_call_target="tpu_custom_call", output_to_operand_aliasing={{0}: (8, {})} | custom-call | tf_op jit(solution)/shard_map/pallas_call | solution.py:180
  60.9 0.0 collective-permute-done.2
  60.9 0.0 collective-permute-done.3
  60.9 0.0 copy-done.3
  60.9 1.0 %fusion.2 = (bf16[256,512]{1,0:T(8,128)(2,1)S(1)}, f32[256,512]{1,0:T(8,128)S(1)}) fusion(bf16[256,512]{1,0:T(8,128)(2,1)S(1)} %collective-permute-done.3, bf16[256,512]{1,0:T(8,128)(2,1)S(1)} %collective-permute-done.2, f32[256,256]{1,0:T(8,128)} %bitcast.8, f32[256,256]{1,0:T(8,128)S(1)} %bitcast.7), kind=kLoop, calls=%fused_computation.18 | loop fusion | flops 786432 | bytes 1835008 | tf_op jit(solution)/shard_map/convert.3
  62.0 0.7 %pad_maximum_fusion.1 = bf16[256,256]{1,0:T(8,128)(2,1)} fusion(bf16[256,128]{1,0:T(8,128)(2,1)S(1)} %get-tuple-element.28, bf16[256,128]{1,0:T(8,128)(2,1)S(1)} %get-tuple-element.27), kind=kLoop, calls=%fused_computation.8 | loop fusion | flops 262144 | bytes 262144 | tf_op jit(solution)/shard_map/concatenate | solution.py:231
  62.7 0.7 %fusion.1 = bf16[256,256]{1,0:T(8,128)(2,1)} fusion(f32[256,128]{1,0:T(8,128)S(1)} %get-tuple-element.24, f32[256,128]{1,0:T(8,128)S(1)} %get-tuple-element.23), kind=kLoop, calls=%fused_computation.5 | loop fusion | flops 196608 | bytes 393216 | tf_op jit(solution)/shard_map/convert_element_type | solution.py:235
  (8 shorter events, 0.1 us)
Async XLA Ops:
  1.6 9.6 %copy-start = (bf16[256,512]{1,0:T(8,128)(2,1)}, bf16[256,512]{1,0:T(8,128)(2,1)S(1)}, u32[]{:S(2)}) copy-start(bf16[256,512]{1,0:T(8,128)(2,1)S(1)} %pad_maximum_fusion.rest_0_) | copy-start | bytes 786436
  1.6 17.1 %collective-permute-start.1 = (bf16[256,512]{1,0:T(8,128)(2,1)S(1)}, bf16[256,512]{1,0:T(8,128)(2,1)S(1)}, u32[]{:S(2)}, u32[]{:S(2)}) collective-permute-start(bf16[256,512]{1,0:T(8,128)(2,1)S(1)} %pad_maximum_fusion.rest_0_), channel_id=1, source_target_pairs={{0,1},{1,2},{2,3},{3,4},{4,5},{5,6},{6,7},{7,8},{8,9},{9,10},{10,1... | collective-permute-start | bytes 786440 | tf_op jit(solution)/shard_map/ppermute | solution.py:20
  3.6 15.2 %collective-permute-start = (bf16[256,512]{1,0:T(8,128)(2,1)S(1)}, bf16[256,512]{1,0:T(8,128)(2,1)S(1)}, u32[]{:S(2)}, u32[]{:S(2)}) collective-permute-start(bf16[256,512]{1,0:T(8,128)(2,1)S(1)} %pad_maximum_fusion.rest_0_), channel_id=1, source_target_pairs={{0,2},{1,3},{2,4},{3,5},{4,6},{5,7},{6,8},{7,9},{8,10},{9,11},{10,... | collective-permute-start | bytes 786440 | tf_op jit(solution)/shard_map/ppermute | solution.py:20
  18.8 0.7 %copy-start.1 = (bf16[256,512]{1,0:T(8,128)(2,1)}, bf16[256,512]{1,0:T(8,128)(2,1)S(1)}, u32[]{:S(2)}) copy-start(bf16[256,512]{1,0:T(8,128)(2,1)S(1)} %collective-permute-done.1.rest_1_) | copy-start | bytes 786436
  18.8 0.8 %copy-start.2 = (bf16[256,512]{1,0:T(8,128)(2,1)}, bf16[256,512]{1,0:T(8,128)(2,1)S(1)}, u32[]{:S(2)}) copy-start(bf16[256,512]{1,0:T(8,128)(2,1)S(1)} %collective-permute-done.rest_0_) | copy-start | bytes 786436
  42.6 18.3 %collective-permute-start.2 = (bf16[256,512]{1,0:T(8,128)(2,1)S(1)}, bf16[256,512]{1,0:T(8,128)(2,1)S(1)}, u32[]{:S(2)}, u32[]{:S(2)}) collective-permute-start(bf16[256,512]{1,0:T(8,128)(2,1)S(1)} %get-tuple-element.25), channel_id=1, source_target_pairs={{1,0},{2,1},{3,2},{4,3},{5,4},{6,5},{7,6},{8,7},{9,8},{10,9},{11,1... | collective-permute-start | bytes 786440 | tf_op jit(solution)/shard_map/ppermute | solution.py:20
  44.5 16.4 %collective-permute-start.3 = (bf16[256,512]{1,0:T(8,128)(2,1)S(1)}, bf16[256,512]{1,0:T(8,128)(2,1)S(1)}, u32[]{:S(2)}, u32[]{:S(2)}) collective-permute-start(bf16[256,512]{1,0:T(8,128)(2,1)S(1)} %get-tuple-element.26), channel_id=1, source_target_pairs={{2,0},{3,1},{4,2},{5,3},{6,4},{7,5},{8,6},{9,7},{10,8},{11,9},{12,... | collective-permute-start | bytes 786440 | tf_op jit(solution)/shard_map/ppermute | solution.py:20
  53.0 8.0 %copy-start.3 = (f32[1,256,256]{2,1,0:T(8,128)S(1)}, f32[1,256,256]{2,1,0:T(8,128)}, u32[]{:S(2)}) copy-start(f32[1,256,256]{2,1,0:T(8,128)} %get-tuple-element.16) | copy-start | bytes 786436

commit v7 on v6

--- a/solution.py
+++ b/solution.py
@@ -10,6 +10,7 @@
 HD = 128
 MOST = 512
 KEY_TILE = 128
+QUERY_TILE = 128
 HEADS_PER_STEP = 8
 NT_DIMS = (((1,), (1,)), ((), ()))
 
@@ -24,7 +25,8 @@
     hb = HEADS_PER_STEP
     pieces = list(range(reach)) if remote else [reach]
     tiles_per_piece = tok // KEY_TILE
-    n_rows = len(pieces) * tok
+    n_halves = tok // QUERY_TILE
+    span = hb * QUERY_TILE
     scale = 1.0 / math.sqrt(HD)
 
     def kernel(flags_ref, q_ref, do_ref, o_ref, lse_ref, bias_ref, *rest):
@@ -48,12 +50,19 @@
         delta_rows = []
         for i in range(hb):
             cols = slice(i * HD, (i + 1) * HD)
-            qs_scr[i * tok:(i + 1) * tok, :] = q_ref[:, cols]
-            dos_scr[i * tok:(i + 1) * tok, :] = do_ref[:, cols]
+            for h in range(n_halves):
+                dst = slice(h * span + i * QUERY_TILE, h * span + (i + 1) * QUERY_TILE)
+                src = slice(h * QUERY_TILE, (h + 1) * QUERY_TILE)
+                qs_scr[dst, :] = q_ref[src, cols]
+                dos_scr[dst, :] = do_ref[src, cols]
             prod = do_ref[:, cols].astype(jnp.float32) * o_ref[:, cols].astype(jnp.float32)
             delta_rows.append(jnp.sum(prod.T, axis=0, keepdims=True))
-        dl_row = jnp.concatenate(delta_rows, axis=1)
-        lse_row = jnp.concatenate([lse_ref[i:i + 1, :] for i in range(hb)], axis=1)
+        dl_row = jnp.concatenate(
+            [delta_rows[i][:, h * QUERY_TILE:(h + 1) * QUERY_TILE]
+             for h in range(n_halves) for i in range(hb)], axis=1)
+        lse_row = jnp.concatenate(
+            [lse_ref[i:i + 1, h * QUERY_TILE:(h + 1) * QUERY_TILE]
+             for h in range(n_halves) for i in range(hb)], axis=1)
         dqt_scr[...] = jnp.zeros_like(dqt_scr)
 
         for n, piece in enumerate(pieces):
@@ -62,32 +71,35 @@
                 j = piece * tiles_per_piece + t
                 rows = slice(t * KEY_TILE, (t + 1) * KEY_TILE)
                 loc_rows = slice(n * tok + t * KEY_TILE, n * tok + (t + 1) * KEY_TILE)
-
-                def tile(kv=kv, rows=rows, loc_rows=loc_rows, n=n):
-                    k = kv[rows, :HD]
-                    v = kv[rows, HD:]
-                    qs = qs_scr[...]
-                    dos = dos_scr[...]
-                    st = lax.dot_general(k, qs, NT_DIMS, preferred_element_type=jnp.float32)
-                    bias = bias_ref[loc_rows, :]
-                    p = jnp.exp(st * scale - lse_row + jnp.concatenate([bias] * hb, axis=1))
-                    dv = jnp.dot(p.astype(jnp.bfloat16), dos, preferred_element_type=jnp.float32)
-                    dpt = lax.dot_general(v, dos, NT_DIMS, preferred_element_type=jnp.float32)
-                    ds = (p * (dpt - dl_row)).astype(jnp.bfloat16)
-                    dk = jnp.dot(ds, qs, preferred_element_type=jnp.float32)
-                    acc_scr[n, rows, :HD] += dk
-                    acc_scr[n, rows, HD:] += dv
-                    dqt_scr[...] += jnp.dot(
-                        kt_scr[:, loc_rows], ds, preferred_element_type=jnp.float32)
-
-                if remote:
-                    pl.when(flags_ref[j] != 0)(tile)
-                else:
-                    tile()
+                for h in range(n_halves):
+                    lanes = slice(h * span, (h + 1) * span)
+
+                    def block(kv=kv, rows=rows, loc_rows=loc_rows, n=n, h=h, lanes=lanes):
+                        k = kv[rows, :HD]
+                        v = kv[rows, HD:]
+                        qs = qs_scr[lanes, :]
+                        dos = dos_scr[lanes, :]
+                        st = lax.dot_general(k, qs, NT_DIMS, preferred_element_type=jnp.float32)
+                        bias = bias_ref[loc_rows, h * QUERY_TILE:(h + 1) * QUERY_TILE]
+                        p = jnp.exp(st * scale - lse_row[:, lanes]
+                                    + jnp.concatenate([bias] * hb, axis=1))
+                        dv = jnp.dot(p.astype(jnp.bfloat16), dos,
+                                     preferred_element_type=jnp.float32)
+                        dpt = lax.dot_general(v, dos, NT_DIMS, preferred_element_type=jnp.float32)
+                        ds = (p * (dpt - dl_row[:, lanes])).astype(jnp.bfloat16)
+                        dk = jnp.dot(ds, qs, preferred_element_type=jnp.float32)
+                        acc_scr[n, rows, :HD] += dk
+                        acc_scr[n, rows, HD:] += dv
+                        dqt_scr[:, lanes] += jnp.dot(
+                            kt_scr[:, loc_rows], ds, preferred_element_type=jnp.float32)
+
+                    pl.when(flags_ref[j * n_halves + h] != 0)(block)
 
         for i in range(hb):
             cols = slice(i * HD, (i + 1) * HD)
-            part = dqt_scr[:, i * tok:(i + 1) * tok].T
+            part = jnp.concatenate(
+                [dqt_scr[:, h * span + i * QUERY_TILE:h * span + (i + 1) * QUERY_TILE].T
+                 for h in range(n_halves)], axis=0)
             if dq_in:
                 part = part + dqp_ref[:, cols]
             if dq_final:
@@ -205,11 +217,13 @@
     visible = (key_ids[:, None] == query_ids[None, :]) & (
         key_places[:, None] <= query_places[None, :])
     bias = jnp.where(visible, 0.0, -jnp.inf).astype(jnp.float32)
-    n_tiles = win // KEY_TILE
-    last_places = (position - reach) * tok + KEY_TILE * jnp.arange(
-        1, n_tiles + 1, dtype=jnp.int32) - 1
-    first_doc = doc_of(position[None] * tok)
-    flags = ((doc_of(last_places) == first_doc) & (last_places >= 0)).astype(jnp.int32)
+    key_lo = (position - reach) * tok + KEY_TILE * jnp.arange(win // KEY_TILE, dtype=jnp.int32)
+    key_hi = key_lo + KEY_TILE - 1
+    query_lo = position * tok + QUERY_TILE * jnp.arange(tok // QUERY_TILE, dtype=jnp.int32)
+    query_hi = query_lo + QUERY_TILE - 1
+    same_doc = doc_of(key_hi)[:, None] == doc_of(query_lo)[None, :]
+    flags = ((key_lo[:, None] <= query_hi[None, :]) & (key_hi[:, None] >= 0)
+             & ((key_hi[:, None] >= query_lo[None, :]) | same_doc)).astype(jnp.int32).reshape(-1)
 
     kv = jnp.concatenate(
         [part for g in range(kvh)

time: 63.7 us -> 68.7 us (1.078)
  the two profiles are of different devices: /device:TPU:12 before, /device:TPU:24 now
where the time goes in v7:
time: 68.7 us; the launch traced here: 68.3 us
  Pallas kernels  41.4 us (60%)
  starting transfers between devices  17.5 us (25%)
  other arithmetic  4.41 us (6%)
  local copies, waits for them, and re-layouts  4.15 us (6%)
  between operations  0.83 us (1%)
    pallas_call x4, Pallas kernels, grads_call(): pl.pallas_call(kernel, grid_spec=grid_spec, out_shape=[dq_shape, dkv_shap...  41.4 us
    ppermute x4, starting transfers between devices, shifted(): return lax.ppermute(block, axis, route)  17.5 us
  transfers between devices with their start and end apart: 4, of which 0 were waited for; matrix products, arithmetic and copies ran while one was open for 5% of the time, Pallas kernels for 28%

profile of v7, /device:TPU:24, one launch (start us, length us, event | category | flops | bytes accessed | tf_op | source)
XLA Modules:
  0.0 68.3 jit_solution(10452412936112704703)
XLA Ops:
  0.6 1.0 %fusion.7 = (bf16[256,128]{1,0:T(8,128)(2,1)S(1)}, bf16[256,128]{1,0:T(8,128)(2,1)S(1)}, bf16[256,128]{1,0:T(8,128)(2,1)S(1)}, bf16[256,128]{1,0:T(8,128)(2,1)S(1)}) fusion(bf16[256,256]{1,0:T(8,128)(2,1)} %param.8, bf16[256,256]{1,0:T(8,128)(2,1)} %param.9), kind=kLoop, calls=%fused_computation.26 | loop fusion | bytes 524288 | tf_op jit(solution)/shard_map/slice | solution.py:230
  1.6 0.0 copy-start
  1.6 1.9 %collective-permute-start.1 = (bf16[256,512]{1,0:T(8,128)(2,1)S(1)}, bf16[256,512]{1,0:T(8,128)(2,1)S(1)}, u32[]{:S(2)}, u32[]{:S(2)}) collective-permute-start(bf16[256,512]{1,0:T(8,128)(2,1)S(1)} %pad_maximum_fusion.rest_0_), channel_id=1, source_target_pairs={{0,1},{1,2},{2,3},{3,4},{4,5},{5,6},{6,7},{7,8},{8,9},{9,10},{10,1... | collective-permute-start | bytes 786440 | tf_op jit(solution)/shard_map/ppermute | solution.py:21
  3.6 3.4 %collective-permute-start = (bf16[256,512]{1,0:T(8,128)(2,1)S(1)}, bf16[256,512]{1,0:T(8,128)(2,1)S(1)}, u32[]{:S(2)}, u32[]{:S(2)}) collective-permute-start(bf16[256,512]{1,0:T(8,128)(2,1)S(1)} %pad_maximum_fusion.rest_0_), channel_id=1, source_target_pairs={{0,2},{1,3},{2,4},{3,5},{4,6},{5,7},{6,8},{7,9},{8,10},{9,11},{10,... | collective-permute-start | bytes 786440 | tf_op jit(solution)/shard_map/ppermute | solution.py:21
  7.1 0.7 %copy.14 = s32[16,1]{1,0:T(8,128)S(1)} copy(s32[16,1]{0,1:T(1,128)} %bitcast.9) | data formatting | bytes 128 | tf_op jit(solution)/shard_map/reshape.73
  7.8 0.1 reduce
  8.0 0.2 fusion.2
  8.2 0.2 convert_reduce_fusion.2
  8.3 0.1 convert_reduce_fusion
  8.4 0.1 and_convert_fusion
  8.5 0.1 convert_reduce_fusion.1
  8.6 0.6 reshape.94.flags_ref
  9.2 1.2 %and_select_fusion.bias_ref = f32[768,256]{1,0:T(8,128)} fusion(s32[256]{0:T(256)S(1)} %iota_add_fusion.1, s32[256]{0:T(256)S(1)} %convert_reduce_fusion.1, s32[768]{0:T(1024)S(1)} %iota_add_fusion, s32[768]{0:T(1024)S(1)} %compare_select_fusion), kind=kLoop, calls=%fused_computation | loop fusion | flops 786432 | bytes 794624 | tf_op jit(solution)/shard_map/jit(_where)/select_n | solution.py:219
  10.4 0.0 copy-done
  10.4 9.4 %shard_map.94 = (f32[256,2048]{1,0:T(8,128)}, f32[1,256,256]{2,1,0:T(8,128)}) custom-call(s32[12]{0:T(128)} %reshape.94.flags_ref, bf16[256,4096]{1,0:T(8,128)(2,1)} %q_ref.7, bf16[256,4096]{1,0:T(8,128)(2,1)} %do_ref.7, bf16[256,4096]{1,0:T(8,128)(2,1)} %o_ref.7, f32[32,256]{1,0:T(8,128)} %lse_ref.7, f32[768,256]{1,0:T(8,128)} %and_select_fusion.bias_ref, ...), custom_call_target="tpu_custom_call" | custom-call | tf_op jit(solution)/shard_map/pallas_call | solution.py:192
  19.7 0.0 collective-permute-done.1.rest_1_
  19.7 0.0 copy-start.1
  19.8 0.0 collective-permute-done.rest_0_
  19.8 0.0 copy-start.2
  19.8 0.7 copy-done.1
  20.4 0.1 copy-done.2
  20.5 11.2 %shard_map.95 = (bf16[256,4096]{1,0:T(8,128)(2,1)}, bf16[2,256,512]{2,1,0:T(8,128)(2,1)}) custom-call(s32[12]{0:T(128)} %reshape.94.flags_ref, bf16[256,4096]{1,0:T(8,128)(2,1)} %q_ref.7, bf16[256,4096]{1,0:T(8,128)(2,1)} %do_ref.7, bf16[256,4096]{1,0:T(8,128)(2,1)} %o_ref.7, f32[32,256]{1,0:T(8,128)} %lse_ref.7, f32[768,256]{1,0:T(8,128)} %and_select_fusion.bias_ref, ...), custom_call_target="tpu_custom_call" | custom-call | tf_op jit(solution)/shard_map/pallas_call | solution.py:192
  31.7 11.2 %shard_map.96 = (f32[256,2048]{1,0:T(8,128)}, bf16[2,256,512]{2,1,0:T(8,128)(2,1)}) custom-call(s32[12]{0:T(128)} %reshape.94.flags_ref, bf16[256,4096]{1,0:T(8,128)(2,1)} %q_ref.7, bf16[256,4096]{1,0:T(8,128)(2,1)} %do_ref.7, bf16[256,4096]{1,0:T(8,128)(2,1)} %o_ref.7, f32[32,256]{1,0:T(8,128)} %lse_ref.7, ...), custom_call_target="tpu_custom_call", output_to_operand_aliasing={{1}: (8, {})} | custom-call | tf_op jit(solution)/shard_map/pallas_call | solution.py:192
  42.9 1.1 %slice_bitcast_fusion.1 = (bf16[256,512]{1,0:T(8,128)(2,1)S(1)}, bf16[256,512]{1,0:T(8,128)(2,1)S(1)}) fusion(bf16[2,256,512]{2,1,0:T(8,128)(2,1)} %get-tuple-element.18), kind=kLoop, calls=%fused_computation.7 | loop fusion | bytes 1048576 | tf_op jit(solution)/shard_map/squeeze | solution.py:237
  44.0 1.9 %collective-permute-start.2 = (bf16[256,512]{1,0:T(8,128)(2,1)S(1)}, bf16[256,512]{1,0:T(8,128)(2,1)S(1)}, u32[]{:S(2)}, u32[]{:S(2)}) collective-permute-start(bf16[256,512]{1,0:T(8,128)(2,1)S(1)} %get-tuple-element.23), channel_id=1, source_target_pairs={{1,0},{2,1},{3,2},{4,3},{5,4},{6,5},{7,6},{8,7},{9,8},{10,9},{11,1... | collective-permute-start | bytes 786440 | tf_op jit(solution)/shard_map/ppermute | solution.py:21
  45.9 10.2 %collective-permute-start.3 = (bf16[256,512]{1,0:T(8,128)(2,1)S(1)}, bf16[256,512]{1,0:T(8,128)(2,1)S(1)}, u32[]{:S(2)}, u32[]{:S(2)}) collective-permute-start(bf16[256,512]{1,0:T(8,128)(2,1)S(1)} %get-tuple-element.24), channel_id=1, source_target_pairs={{2,0},{3,1},{4,2},{5,3},{6,4},{7,5},{8,6},{9,7},{10,8},{11,9},{12,... | collective-permute-start | bytes 786440 | tf_op jit(solution)/shard_map/ppermute | solution.py:21
  56.1 9.7 %shard_map.97 = (bf16[256,4096]{1,0:T(8,128)(2,1)}, f32[1,256,256]{2,1,0:T(8,128)}) custom-call(s32[12]{0:T(128)} %reshape.94.flags_ref, bf16[256,4096]{1,0:T(8,128)(2,1)} %q_ref.7, bf16[256,4096]{1,0:T(8,128)(2,1)} %do_ref.7, bf16[256,4096]{1,0:T(8,128)(2,1)} %o_ref.7, f32[32,256]{1,0:T(8,128)} %lse_ref.7, ...), custom_call_target="tpu_custom_call", output_to_operand_aliasing={{0}: (8, {})} | custom-call | tf_op jit(solution)/shard_map/pallas_call | solution.py:192
  65.8 0.0 collective-permute-done.2
  65.8 0.0 collective-permute-done.3
  65.9 1.0 %fusion.3 = (bf16[256,512]{1,0:T(8,128)(2,1)S(1)}, f32[256,512]{1,0:T(8,128)S(1)}) fusion(bf16[256,512]{1,0:T(8,128)(2,1)S(1)} %collective-permute-done.3, bf16[256,512]{1,0:T(8,128)(2,1)S(1)} %collective-permute-done.2, f32[256,256]{1,0:T(8,128)} %bitcast.8, f32[256,256]{1,0:T(8,128)S(1)} %bitcast.7), kind=kLoop, calls=%fused_computation.23 | loop fusion | flops 786432 | bytes 1835008 | tf_op jit(solution)/shard_map/convert.4
  67.0 0.7 pad_maximum_fusion.1
  67.6 0.7 fusion.1
  (12 shorter events, 0.1 us)
Async XLA Ops:
  1.6 8.7 %copy-start = (bf16[256,512]{1,0:T(8,128)(2,1)}, bf16[256,512]{1,0:T(8,128)(2,1)S(1)}, u32[]{:S(2)}) copy-start(bf16[256,512]{1,0:T(8,128)(2,1)S(1)} %pad_maximum_fusion.rest_0_) | copy-start | bytes 786436
  1.6 18.1 %collective-permute-start.1 = (bf16[256,512]{1,0:T(8,128)(2,1)S(1)}, bf16[256,512]{1,0:T(8,128)(2,1)S(1)}, u32[]{:S(2)}, u32[]{:S(2)}) collective-permute-start(bf16[256,512]{1,0:T(8,128)(2,1)S(1)} %pad_maximum_fusion.rest_0_), channel_id=1, source_target_pairs={{0,1},{1,2},{2,3},{3,4},{4,5},{5,6},{6,7},{7,8},{8,9},{9,10},{10,1... | collective-permute-start | bytes 786440 | tf_op jit(solution)/shard_map/ppermute | solution.py:21
  3.6 16.2 %collective-permute-start = (bf16[256,512]{1,0:T(8,128)(2,1)S(1)}, bf16[256,512]{1,0:T(8,128)(2,1)S(1)}, u32[]{:S(2)}, u32[]{:S(2)}) collective-permute-start(bf16[256,512]{1,0:T(8,128)(2,1)S(1)} %pad_maximum_fusion.rest_0_), channel_id=1, source_target_pairs={{0,2},{1,3},{2,4},{3,5},{4,6},{5,7},{6,8},{7,9},{8,10},{9,11},{10,... | collective-permute-start | bytes 786440 | tf_op jit(solution)/shard_map/ppermute | solution.py:21
  19.7 0.7 %copy-start.1 = (bf16[256,512]{1,0:T(8,128)(2,1)}, bf16[256,512]{1,0:T(8,128)(2,1)S(1)}, u32[]{:S(2)}) copy-start(bf16[256,512]{1,0:T(8,128)(2,1)S(1)} %collective-permute-done.1.rest_1_) | copy-start | bytes 786436
  19.8 0.8 %copy-start.2 = (bf16[256,512]{1,0:T(8,128)(2,1)}, bf16[256,512]{1,0:T(8,128)(2,1)S(1)}, u32[]{:S(2)}) copy-start(bf16[256,512]{1,0:T(8,128)(2,1)S(1)} %collective-permute-done.rest_0_) | copy-start | bytes 786436
  44.0 21.9 %collective-permute-start.2 = (bf16[256,512]{1,0:T(8,128)(2,1)S(1)}, bf16[256,512]{1,0:T(8,128)(2,1)S(1)}, u32[]{:S(2)}, u32[]{:S(2)}) collective-permute-start(bf16[256,512]{1,0:T(8,128)(2,1)S(1)} %get-tuple-element.23), channel_id=1, source_target_pairs={{1,0},{2,1},{3,2},{4,3},{5,4},{6,5},{7,6},{8,7},{9,8},{10,9},{11,1... | collective-permute-start | bytes 786440 | tf_op jit(solution)/shard_map/ppermute | solution.py:21
  45.9 20.0 %collective-permute-start.3 = (bf16[256,512]{1,0:T(8,128)(2,1)S(1)}, bf16[256,512]{1,0:T(8,128)(2,1)S(1)}, u32[]{:S(2)}, u32[]{:S(2)}) collective-permute-start(bf16[256,512]{1,0:T(8,128)(2,1)S(1)} %get-tuple-element.24), channel_id=1, source_target_pairs={{2,0},{3,1},{4,2},{5,3},{6,4},{7,5},{8,6},{9,7},{10,8},{11,9},{12,... | collective-permute-start | bytes 786440 | tf_op jit(solution)/shard_map/ppermute | solution.py:21
  56.1 9.8 %copy-start.3 = (f32[1,256,256]{2,1,0:T(8,128)S(1)}, f32[1,256,256]{2,1,0:T(8,128)}, u32[]{:S(2)}) copy-start(f32[1,256,256]{2,1,0:T(8,128)} %get-tuple-element.16) | copy-start | bytes 786436

commit v8 on v6

--- a/solution.py
+++ b/solution.py
@@ -33,7 +33,7 @@
         dqp_ref = rest.pop(0) if dq_in else None
         rest = rest[n_alias:]
         dq_ref = rest.pop(0)
-        dkv_ref = rest.pop(0)
+        dkv_refs = [rest.pop(0) for _ in pieces]
         qs_scr, dos_scr, dqt_scr, kt_scr, acc_scr = rest[-5:]
         b = pl.program_id(0)
         nb = pl.num_programs(0)
@@ -97,7 +97,8 @@
 
         @pl.when(b == nb - 1)
         def _():
-            dkv_ref[...] = acc_scr[...].astype(dkv_ref.dtype)
+            for n, dkv_ref in enumerate(dkv_refs):
+                dkv_ref[...] = acc_scr[n].astype(dkv_ref.dtype)
 
     return kernel
 
@@ -124,7 +125,7 @@
         return (0, b)
 
     def bias_block(b, f):
-        return (0, 0) if remote else (reach, 0)
+        return (0, 0)
 
     def kv_block(b, f):
         return (0, group)
@@ -146,9 +147,10 @@
         in_specs.append(pl.BlockSpec(memory_space=pl.ANY))
         args.append(dq_alias)
     if dkv_alias is not None:
-        aliases[len(args) + 1] = 1
-        in_specs.append(pl.BlockSpec(memory_space=pl.ANY))
-        args.append(dkv_alias)
+        for n, piece_arr in enumerate(dkv_alias):
+            aliases[len(args) + 1] = 1 + n
+            in_specs.append(pl.BlockSpec(memory_space=pl.ANY))
+            args.append(piece_arr)
 
     kernel = make_kernel(tok, reach, remote, dq_part is not None, dq_final, len(aliases))
     if dq_final:
@@ -158,17 +160,17 @@
         dq_shape = jax.ShapeDtypeStruct((tok, heads_per_group * HD), jnp.float32)
         dq_spec = pl.BlockSpec((tok, hb * HD), local_block)
     if remote:
-        dkv_shape = jax.ShapeDtypeStruct((n_pieces, tok, kvh * 2 * HD), jnp.bfloat16)
-        dkv_spec = pl.BlockSpec((n_pieces, tok, 2 * HD), lambda b, f: (0, 0, group))
+        dkv_shape = jax.ShapeDtypeStruct((tok, kvh * 2 * HD), jnp.bfloat16)
+        dkv_spec = pl.BlockSpec((tok, 2 * HD), lambda b, f: (0, group))
     else:
-        dkv_shape = jax.ShapeDtypeStruct((n_pieces, tok, 2 * HD), jnp.float32)
-        dkv_spec = pl.BlockSpec((n_pieces, tok, 2 * HD), lambda b, f: (0, 0, 0))
+        dkv_shape = jax.ShapeDtypeStruct((tok, 2 * HD), jnp.float32)
+        dkv_spec = pl.BlockSpec((tok, 2 * HD), lambda b, f: (0, 0))
 
     grid_spec = pltpu.PrefetchScalarGridSpec(
         num_scalar_prefetch=1,
         grid=(nb,),
         in_specs=in_specs,
-        out_specs=[dq_spec, dkv_spec],
+        out_specs=[dq_spec] + [dkv_spec] * n_pieces,
         scratch_shapes=[
             pltpu.VMEM((hb * tok, HD), jnp.bfloat16),
             pltpu.VMEM((hb * tok, HD), jnp.bfloat16),
@@ -177,13 +179,14 @@
             pltpu.VMEM((n_pieces, tok, 2 * HD), jnp.float32),
         ],
     )
-    return pl.pallas_call(
+    outs = pl.pallas_call(
         kernel,
         grid_spec=grid_spec,
-        out_shape=[dq_shape, dkv_shape],
+        out_shape=[dq_shape] + [dkv_shape] * n_pieces,
         input_output_aliases=aliases,
         compiler_params=pltpu.CompilerParams(dimension_semantics=("arbitrary",)),
     )(flags, *args)
+    return outs[0], outs[1:]
 
 
 def per_device(queries, keys, values, outputs, out_grad, logsumexp, doc_lengths):
@@ -202,9 +205,12 @@
     query_ids = doc_of(query_places)
     key_places = (position - reach) * tok + jnp.arange(win, dtype=jnp.int32)
     key_ids = jnp.where(key_places >= 0, doc_of(key_places), -1)
-    visible = (key_ids[:, None] == query_ids[None, :]) & (
-        key_places[:, None] <= query_places[None, :])
-    bias = jnp.where(visible, 0.0, -jnp.inf).astype(jnp.float32)
+    own_visible = (query_ids[:, None] == query_ids[None, :]) & (
+        query_places[:, None] <= query_places[None, :])
+    bias_own = jnp.where(own_visible, 0.0, -jnp.inf).astype(jnp.float32)
+    remote_ids = key_ids[:reach * tok]
+    bias_rem = jnp.where(remote_ids[:, None] == query_ids[None, :], 0.0, -jnp.inf
+                         ).astype(jnp.float32)
     n_tiles = win // KEY_TILE
     last_places = (position - reach) * tok + KEY_TILE * jnp.arange(
         1, n_tiles + 1, dtype=jnp.int32) - 1
@@ -215,15 +221,17 @@
         [part for g in range(kvh)
          for part in (keys[:, g * HD:(g + 1) * HD], values[:, g * HD:(g + 1) * HD])], axis=1)
     kv_pieces = [kv] + [shifted(kv, "seq", hop) for hop in range(1, reach + 1)]
-    common = (flags, queries, out_grad, outputs, logsumexp, bias, kv_pieces, reach)
-
-    dq_part0, dkv_own0 = grads_call(0, False, *common)
-    dq, dkv_rem = grads_call(0, True, *common, dq_part=dq_part0)
-    dq_part1, dkv_rem = grads_call(1, True, *common, dkv_alias=dkv_rem)
+    no_flags = jnp.zeros((n_tiles,), jnp.int32)
+    own = (no_flags, queries, out_grad, outputs, logsumexp, bias_own, kv_pieces, reach)
+    rem = (flags, queries, out_grad, outputs, logsumexp, bias_rem, kv_pieces, reach)
+
+    dq_part0, (dkv_own0,) = grads_call(0, False, *own)
+    dq, dkv_rem = grads_call(0, True, *rem, dq_part=dq_part0)
+    dq_part1, dkv_rem = grads_call(1, True, *rem, dkv_alias=dkv_rem)
     returned = [shifted(dkv_rem[reach - hop], "seq", -hop) for hop in range(1, reach + 1)]
-    dq, dkv_own1 = grads_call(1, False, *common, dq_part=dq_part1, dq_alias=dq)
-
-    total = jnp.concatenate([dkv_own0[0], dkv_own1[0]], axis=1)
+    dq, (dkv_own1,) = grads_call(1, False, *own, dq_part=dq_part1, dq_alias=dq)
+
+    total = jnp.concatenate([dkv_own0, dkv_own1], axis=1)
     for r in returned:
         total = total + r.astype(jnp.float32)
     key_total = jnp.concatenate(

time: 63.7 us -> 65.1 us (1.022)
  the two profiles are of different devices: /device:TPU:12 before, /device:TPU:22 now
where the time goes in v8:
time: 65.1 us; the launch traced here: 64.8 us
  Pallas kernels  34 us (52%)
  waiting for transfers between devices  11.4 us (18%)
  starting transfers between devices  9.18 us (14%)
  other arithmetic  6.43 us (10%)
  local copies, waits for them, and re-layouts  3.02 us (5%)
  between operations  0.77 us (1%)
    pallas_call x4, Pallas kernels, grads_call(): pl.pallas_call(kernel, grid_spec=grid_spec, out_shape=[dq_shape] + [dkv_s...  34 us
    ppermute x4, waiting for transfers between devices, shifted(): return lax.ppermute(block, axis, route)  11.4 us
    ppermute x4, starting transfers between devices, shifted(): return lax.ppermute(block, axis, route)  9.18 us
  transfers between devices with their start and end apart: 4, of which 1 were waited for; matrix products, arithmetic and copies ran while one was open for 8% of the time, Pallas kernels for 24%

profile of v8, /device:TPU:22, one launch (start us, length us, event | category | flops | bytes accessed | tf_op | source)
XLA Modules:
  0.0 64.8 jit_solution(17570992051925275242)
XLA Ops:
  0.6 1.0 %fusion.6 = (bf16[256,128]{1,0:T(8,128)(2,1)S(1)}, bf16[256,128]{1,0:T(8,128)(2,1)S(1)}, bf16[256,128]{1,0:T(8,128)(2,1)S(1)}, bf16[256,128]{1,0:T(8,128)(2,1)S(1)}) fusion(bf16[256,256]{1,0:T(8,128)(2,1)} %param.8, bf16[256,256]{1,0:T(8,128)(2,1)} %param.9), kind=kLoop, calls=%fused_computation.20 | loop fusion | bytes 524288 | tf_op jit(solution)/shard_map/slice | solution.py:222
  1.6 0.0 copy-start
  1.6 1.9 %collective-permute-start.1 = (bf16[256,512]{1,0:T(8,128)(2,1)S(1)}, bf16[256,512]{1,0:T(8,128)(2,1)S(1)}, u32[]{:S(2)}, u32[]{:S(2)}) collective-permute-start(bf16[256,512]{1,0:T(8,128)(2,1)S(1)} %pad_maximum_fusion.rest_0_), channel_id=1, source_target_pairs={{0,1},{1,2},{2,3},{3,4},{4,5},{5,6},{6,7},{7,8},{8,9},{9,10},{10,1... | collective-permute-start | bytes 786440 | tf_op jit(solution)/shard_map/ppermute | solution.py:20
  3.6 3.4 %collective-permute-start = (bf16[256,512]{1,0:T(8,128)(2,1)S(1)}, bf16[256,512]{1,0:T(8,128)(2,1)S(1)}, u32[]{:S(2)}, u32[]{:S(2)}) collective-permute-start(bf16[256,512]{1,0:T(8,128)(2,1)S(1)} %pad_maximum_fusion.rest_0_), channel_id=1, source_target_pairs={{0,2},{1,3},{2,4},{3,5},{4,6},{5,7},{6,8},{7,9},{8,10},{9,11},{10,... | collective-permute-start | bytes 786440 | tf_op jit(solution)/shard_map/ppermute | solution.py:20
  7.0 0.7 %copy.15 = s32[16,1]{1,0:T(8,128)S(1)} copy(s32[16,1]{0,1:T(1,128)} %bitcast.1) | data formatting | bytes 128 | tf_op jit(solution)/shard_map/reshape
  7.8 0.6 convert_reduce_fusion.2
  8.5 0.1 convert_reduce_fusion
  8.6 0.2 convert_reduce_fusion.3
  8.7 0.1 convert_reduce_fusion.1
  8.8 0.9 %and_select_fusion.bias_ref = f32[256,256]{1,0:T(8,128)} fusion(s32[256]{0:T(256)S(1)} %iota_add_fusion.1, s32[256]{0:T(256)S(1)} %convert_reduce_fusion.1), kind=kLoop, calls=%fused_computation.6 | loop fusion | flops 262144 | bytes 264192 | tf_op jit(solution)/shard_map/jit(_where)/select_n | solution.py:210
  9.7 1.2 %and_convert_fusion.flags_ref = s32[6]{0:T(128)} fusion(s32[6]{0:T(128)S(1)} %convert_reduce_fusion.3, s32[]{:T(128)} %get-tuple-element.23, s32[]{:T(128)S(6)} %mul.23), kind=kLoop, calls=%fused_computation.14 | loop fusion | flops 48 | bytes 56 | tf_op jit(solution)/shard_map/convert_element_type | solution.py:218
  10.8 0.5 broadcast_3_flags_ref.2.flags_ref
  11.4 0.0 copy-done
  11.4 7.6 %shard_map.94 = (f32[256,2048]{1,0:T(8,128)}, f32[256,256]{1,0:T(8,128)}) custom-call(s32[6]{0:T(128)} %broadcast_3_flags_ref.2.flags_ref, bf16[256,4096]{1,0:T(8,128)(2,1)} %q_ref.7, bf16[256,4096]{1,0:T(8,128)(2,1)} %do_ref.7, bf16[256,4096]{1,0:T(8,128)(2,1)} %o_ref.7, f32[32,256]{1,0:T(8,128)} %lse_ref.7, f32[256,256]{1,0:T(8,128)} %and_select_fusion.bias_ref, ...), custom_call_target="tpu_custom_call" | custom-call | tf_op jit(solution)/shard_map/pallas_call | solution.py:182
  19.0 0.9 %compare_select_fusion.bias_ref = f32[512,256]{1,0:T(8,128)} fusion(s32[256]{0:T(256)S(1)} %convert_reduce_fusion.1, s32[512]{0:T(512)S(1)} %slice.33), kind=kLoop, calls=%fused_computation.2 | loop fusion | flops 262144 | bytes 527360 | tf_op jit(solution)/shard_map/jit(_where)/select_n | solution.py:212
  19.9 0.0 collective-permute-done.1.rest_1_
  19.9 0.0 collective-permute-done.rest_0_
  19.9 0.0 copy-start.2
  19.9 0.7 %copy-done.1 = bf16[256,512]{1,0:T(8,128)(2,1)} copy-done((bf16[256,512]{1,0:T(8,128)(2,1)}, bf16[256,512]{1,0:T(8,128)(2,1)S(1)}, u32[]{:S(2)}) %copy-start.1) | copy-done | bytes 262168
  20.6 0.1 copy-done.2
  20.7 9.2 %shard_map.95 = (bf16[256,4096]{1,0:T(8,128)(2,1)}, bf16[256,512]{1,0:T(8,128)(2,1)}, bf16[256,512]{1,0:T(8,128)(2,1)}) custom-call(s32[6]{0:T(128)} %and_convert_fusion.flags_ref, bf16[256,4096]{1,0:T(8,128)(2,1)} %q_ref.7, bf16[256,4096]{1,0:T(8,128)(2,1)} %do_ref.7, bf16[256,4096]{1,0:T(8,128)(2,1)} %o_ref.7, f32[32,256]{1,0:T(8,128)} %lse_ref.7, ...), custom_call_target="tpu_custom_call" | custom-call | tf_op jit(solution)/shard_map/pallas_call | solution.py:182
  30.0 9.2 %shard_map.96 = (f32[256,2048]{1,0:T(8,128)}, bf16[256,512]{1,0:T(8,128)(2,1)}, bf16[256,512]{1,0:T(8,128)(2,1)}) custom-call(s32[6]{0:T(128)} %and_convert_fusion.flags_ref, bf16[256,4096]{1,0:T(8,128)(2,1)} %q_ref.7, bf16[256,4096]{1,0:T(8,128)(2,1)} %do_ref.7, bf16[256,4096]{1,0:T(8,128)(2,1)} %o_ref.7, ...), custom_call_target="tpu_custom_call", output_to_operand_aliasing={{1}: (8, {}), {2}: (9, {})} | custom-call | tf_op jit(solution)/shard_map/pallas_call | solution.py:182
  39.1 1.9 %collective-permute-start.2 = (bf16[256,512]{1,0:T(8,128)(2,1)}, bf16[256,512]{1,0:T(8,128)(2,1)S(1)}, u32[]{:S(2)}, u32[]{:S(2)}) collective-permute-start(bf16[256,512]{1,0:T(8,128)(2,1)} %get-tuple-element.21), channel_id=1, source_target_pairs={{1,0},{2,1},{3,2},{4,3},{5,4},{6,5},{7,6},{8,7},{9,8},{10,9},{11,1... | collective-permute-start | bytes 786440 | tf_op jit(solution)/shard_map/ppermute | solution.py:20
  41.0 1.9 %collective-permute-start.3 = (bf16[256,512]{1,0:T(8,128)(2,1)}, bf16[256,512]{1,0:T(8,128)(2,1)S(1)}, u32[]{:S(2)}, u32[]{:S(2)}) collective-permute-start(bf16[256,512]{1,0:T(8,128)(2,1)} %get-tuple-element.22), channel_id=1, source_target_pairs={{2,0},{3,1},{4,2},{5,3},{6,4},{7,5},{8,6},{9,7},{10,8},{11,9},{12,... | collective-permute-start | bytes 786440 | tf_op jit(solution)/shard_map/ppermute | solution.py:20
  43.0 0.0 copy-start.3
  43.0 7.9 %shard_map.97 = (bf16[256,4096]{1,0:T(8,128)(2,1)}, f32[256,256]{1,0:T(8,128)}) custom-call(s32[6]{0:T(128)} %broadcast_3_flags_ref.2.flags_ref, bf16[256,4096]{1,0:T(8,128)(2,1)} %q_ref.7, bf16[256,4096]{1,0:T(8,128)(2,1)} %do_ref.7, bf16[256,4096]{1,0:T(8,128)(2,1)} %o_ref.7, f32[32,256]{1,0:T(8,128)} %lse_ref.7, ...), custom_call_target="tpu_custom_call", output_to_operand_aliasing={{0}: (8, {})} | custom-call | tf_op jit(solution)/shard_map/pallas_call | solution.py:182
  50.9 0.0 collective-permute-done.2
  50.9 11.4 %collective-permute-done.3 = bf16[256,512]{1,0:T(8,128)(2,1)S(1)} collective-permute-done((bf16[256,512]{1,0:T(8,128)(2,1)}, bf16[256,512]{1,0:T(8,128)(2,1)S(1)}, u32[]{:S(2)}, u32[]{:S(2)}) %collective-permute-start.3) | collective-permute-done | bytes 262176 | tf_op jit(solution)/shard_map/ppermute | solution.py:20
  62.3 0.0 copy-done.3
  62.3 1.0 %fusion.2 = (bf16[256,512]{1,0:T(8,128)(2,1)S(1)}, f32[256,512]{1,0:T(8,128)S(1)}) fusion(bf16[256,512]{1,0:T(8,128)(2,1)S(1)} %collective-permute-done.3, bf16[256,512]{1,0:T(8,128)(2,1)S(1)} %collective-permute-done.2, f32[256,256]{1,0:T(8,128)} %get-tuple-element.20, f32[256,256]{1,0:T(8,128)S(1)} %copy-done.3), kind=kLoop, calls=%fused_computation.17 | loop fusion | flops 786432 | bytes 1835008 | tf_op jit(solution)/shard_map/convert.3
  63.4 0.7 %pad_maximum_fusion.1 = bf16[256,256]{1,0:T(8,128)(2,1)} fusion(bf16[256,128]{1,0:T(8,128)(2,1)S(1)} %get-tuple-element.30, bf16[256,128]{1,0:T(8,128)(2,1)S(1)} %get-tuple-element.29), kind=kLoop, calls=%fused_computation.7 | loop fusion | flops 262144 | bytes 262144 | tf_op jit(solution)/shard_map/concatenate | solution.py:239
  64.1 0.7 %fusion.1 = bf16[256,256]{1,0:T(8,128)(2,1)} fusion(f32[256,128]{1,0:T(8,128)S(1)} %get-tuple-element.28, f32[256,128]{1,0:T(8,128)S(1)} %get-tuple-element.27), kind=kLoop, calls=%fused_computation.5 | loop fusion | flops 196608 | bytes 393216 | tf_op jit(solution)/shard_map/convert_element_type | solution.py:243
  (10 shorter events, 0.1 us)
Async XLA Ops:
  1.6 9.7 %copy-start = (bf16[256,512]{1,0:T(8,128)(2,1)}, bf16[256,512]{1,0:T(8,128)(2,1)S(1)}, u32[]{:S(2)}) copy-start(bf16[256,512]{1,0:T(8,128)(2,1)S(1)} %pad_maximum_fusion.rest_0_) | copy-start | bytes 786436
  1.6 18.3 %collective-permute-start.1 = (bf16[256,512]{1,0:T(8,128)(2,1)S(1)}, bf16[256,512]{1,0:T(8,128)(2,1)S(1)}, u32[]{:S(2)}, u32[]{:S(2)}) collective-permute-start(bf16[256,512]{1,0:T(8,128)(2,1)S(1)} %pad_maximum_fusion.rest_0_), channel_id=1, source_target_pairs={{0,1},{1,2},{2,3},{3,4},{4,5},{5,6},{6,7},{7,8},{8,9},{9,10},{10,1... | collective-permute-start | bytes 786440 | tf_op jit(solution)/shard_map/ppermute | solution.py:20
  3.6 16.4 %collective-permute-start = (bf16[256,512]{1,0:T(8,128)(2,1)S(1)}, bf16[256,512]{1,0:T(8,128)(2,1)S(1)}, u32[]{:S(2)}, u32[]{:S(2)}) collective-permute-start(bf16[256,512]{1,0:T(8,128)(2,1)S(1)} %pad_maximum_fusion.rest_0_), channel_id=1, source_target_pairs={{0,2},{1,3},{2,4},{3,5},{4,6},{5,7},{6,8},{7,9},{8,10},{9,11},{10,... | collective-permute-start | bytes 786440 | tf_op jit(solution)/shard_map/ppermute | solution.py:20
  19.9 0.7 %copy-start.1 = (bf16[256,512]{1,0:T(8,128)(2,1)}, bf16[256,512]{1,0:T(8,128)(2,1)S(1)}, u32[]{:S(2)}) copy-start(bf16[256,512]{1,0:T(8,128)(2,1)S(1)} %collective-permute-done.1.rest_1_) | copy-start | bytes 786436
  19.9 0.8 %copy-start.2 = (bf16[256,512]{1,0:T(8,128)(2,1)}, bf16[256,512]{1,0:T(8,128)(2,1)S(1)}, u32[]{:S(2)}) copy-start(bf16[256,512]{1,0:T(8,128)(2,1)S(1)} %collective-permute-done.rest_0_) | copy-start | bytes 786436
  39.1 11.8 %collective-permute-start.2 = (bf16[256,512]{1,0:T(8,128)(2,1)}, bf16[256,512]{1,0:T(8,128)(2,1)S(1)}, u32[]{:S(2)}, u32[]{:S(2)}) collective-permute-start(bf16[256,512]{1,0:T(8,128)(2,1)} %get-tuple-element.21), channel_id=1, source_target_pairs={{1,0},{2,1},{3,2},{4,3},{5,4},{6,5},{7,6},{8,7},{9,8},{10,9},{11,1... | collective-permute-start | bytes 786440 | tf_op jit(solution)/shard_map/ppermute | solution.py:20
  41.0 21.3 %collective-permute-start.3 = (bf16[256,512]{1,0:T(8,128)(2,1)}, bf16[256,512]{1,0:T(8,128)(2,1)S(1)}, u32[]{:S(2)}, u32[]{:S(2)}) collective-permute-start(bf16[256,512]{1,0:T(8,128)(2,1)} %get-tuple-element.22), channel_id=1, source_target_pairs={{2,0},{3,1},{4,2},{5,3},{6,4},{7,5},{8,6},{9,7},{10,8},{11,9},{12,... | collective-permute-start | bytes 786440 | tf_op jit(solution)/shard_map/ppermute | solution.py:20
  43.0 19.3 %copy-start.3 = (f32[256,256]{1,0:T(8,128)S(1)}, f32[256,256]{1,0:T(8,128)}, u32[]{:S(2)}) copy-start(f32[256,256]{1,0:T(8,128)} %get-tuple-element.19) | copy-start | bytes 786436

commit v9 on v8

--- a/solution.py
+++ b/solution.py
@@ -9,7 +9,7 @@
 
 HD = 128
 MOST = 512
-KEY_TILE = 128
+KEY_TILE = 256
 HEADS_PER_STEP = 8
 NT_DIMS = (((1,), (1,)), ((), ()))
 

time: 65.1 us -> 62.5 us (0.960)
  the two profiles are of different devices: /device:TPU:22 before, /device:TPU:12 now
where the time goes in v9:
time: 62.5 us; the launch traced here: 62.1 us
  Pallas kernels  32.2 us (52%)
  starting transfers between devices  15.8 us (25%)
  other arithmetic  6.43 us (10%)
  waiting for transfers between devices  3.91 us (6%)
  local copies, waits for them, and re-layouts  3.02 us (5%)
  between operations  0.77 us (1%)
    pallas_call x4, Pallas kernels, grads_call(): pl.pallas_call(kernel, grid_spec=grid_spec, out_shape=[dq_shape] + [dkv_s...  32.2 us
    ppermute x4, starting transfers between devices, shifted(): return lax.ppermute(block, axis, route)  15.8 us
    ppermute x4, waiting for transfers between devices, shifted(): return lax.ppermute(block, axis, route)  3.91 us
  transfers between devices with their start and end apart: 4, of which 1 were waited for; matrix products, arithmetic and copies ran while one was open for 8% of the time, Pallas kernels for 24%

profile of v9, /device:TPU:12, one launch (start us, length us, event | category | flops | bytes accessed | tf_op | source)
XLA Modules:
  0.0 62.1 jit_solution(9044303953368282611)
XLA Ops:
  0.6 1.0 %fusion.6 = (bf16[256,128]{1,0:T(8,128)(2,1)S(1)}, bf16[256,128]{1,0:T(8,128)(2,1)S(1)}, bf16[256,128]{1,0:T(8,128)(2,1)S(1)}, bf16[256,128]{1,0:T(8,128)(2,1)S(1)}) fusion(bf16[256,256]{1,0:T(8,128)(2,1)} %param.8, bf16[256,256]{1,0:T(8,128)(2,1)} %param.9), kind=kLoop, calls=%fused_computation.20 | loop fusion | bytes 524288 | tf_op jit(solution)/shard_map/slice | solution.py:222
  1.6 0.0 copy-start
  1.6 1.9 %collective-permute-start.1 = (bf16[256,512]{1,0:T(8,128)(2,1)S(1)}, bf16[256,512]{1,0:T(8,128)(2,1)S(1)}, u32[]{:S(2)}, u32[]{:S(2)}) collective-permute-start(bf16[256,512]{1,0:T(8,128)(2,1)S(1)} %pad_maximum_fusion.rest_0_), channel_id=1, source_target_pairs={{0,1},{1,2},{2,3},{3,4},{4,5},{5,6},{6,7},{7,8},{8,9},{9,10},{10,1... | collective-permute-start | bytes 786440 | tf_op jit(solution)/shard_map/ppermute | solution.py:20
  3.6 3.4 %collective-permute-start = (bf16[256,512]{1,0:T(8,128)(2,1)S(1)}, bf16[256,512]{1,0:T(8,128)(2,1)S(1)}, u32[]{:S(2)}, u32[]{:S(2)}) collective-permute-start(bf16[256,512]{1,0:T(8,128)(2,1)S(1)} %pad_maximum_fusion.rest_0_), channel_id=1, source_target_pairs={{0,2},{1,3},{2,4},{3,5},{4,6},{5,7},{6,8},{7,9},{8,10},{9,11},{10,... | collective-permute-start | bytes 786440 | tf_op jit(solution)/shard_map/ppermute | solution.py:20
  7.0 0.7 %copy.15 = s32[16,1]{1,0:T(8,128)S(1)} copy(s32[16,1]{0,1:T(1,128)} %bitcast.1) | data formatting | bytes 128 | tf_op jit(solution)/shard_map/reshape
  7.8 0.6 %convert_reduce_fusion.2 = (s32[]{:T(128)}, s32[16]{0:T(128)S(1)}) fusion(s32[16,1]{1,0:T(8,128)S(1)} %reduce-window.4, s32[]{:T(128)S(6)} %mul.22), kind=kLoop, calls=%fused_computation.10 | loop fusion | flops 47 | bytes 136 | tf_op jit(solution)/shard_map/reduce_sum | solution.py:202
  8.5 0.1 convert_reduce_fusion
  8.6 0.2 convert_reduce_fusion.3
  8.7 0.1 convert_reduce_fusion.1
  8.8 0.9 %and_select_fusion.bias_ref = f32[256,256]{1,0:T(8,128)} fusion(s32[256]{0:T(256)S(1)} %iota_add_fusion.1, s32[256]{0:T(256)S(1)} %convert_reduce_fusion.1), kind=kLoop, calls=%fused_computation.6 | loop fusion | flops 262144 | bytes 264192 | tf_op jit(solution)/shard_map/jit(_where)/select_n | solution.py:210
  9.7 1.2 %and_convert_fusion.flags_ref = s32[3]{0:T(128)} fusion(s32[3]{0:T(128)S(1)} %convert_reduce_fusion.3, s32[]{:T(128)} %get-tuple-element.23, s32[]{:T(128)S(6)} %mul.23), kind=kLoop, calls=%fused_computation.14 | loop fusion | flops 24 | bytes 32 | tf_op jit(solution)/shard_map/convert_element_type | solution.py:218
  10.8 0.5 broadcast_3_flags_ref.2.flags_ref
  11.4 0.0 copy-done
  11.4 7.4 %shard_map.94 = (f32[256,2048]{1,0:T(8,128)}, f32[256,256]{1,0:T(8,128)}) custom-call(s32[3]{0:T(128)} %broadcast_3_flags_ref.2.flags_ref, bf16[256,4096]{1,0:T(8,128)(2,1)} %q_ref.7, bf16[256,4096]{1,0:T(8,128)(2,1)} %do_ref.7, bf16[256,4096]{1,0:T(8,128)(2,1)} %o_ref.7, f32[32,256]{1,0:T(8,128)} %lse_ref.7, f32[256,256]{1,0:T(8,128)} %and_select_fusion.bias_ref, ...), custom_call_target="tpu_custom_call" | custom-call | tf_op jit(solution)/shard_map/pallas_call | solution.py:182
  18.7 0.9 %compare_select_fusion.bias_ref = f32[512,256]{1,0:T(8,128)} fusion(s32[256]{0:T(256)S(1)} %convert_reduce_fusion.1, s32[512]{0:T(512)S(1)} %slice.33), kind=kLoop, calls=%fused_computation.2 | loop fusion | flops 262144 | bytes 527360 | tf_op jit(solution)/shard_map/jit(_where)/select_n | solution.py:212
  19.7 0.0 collective-permute-done.1.rest_1_
  19.7 0.0 collective-permute-done.rest_0_
  19.7 0.0 copy-start.2
  19.7 0.7 %copy-done.1 = bf16[256,512]{1,0:T(8,128)(2,1)} copy-done((bf16[256,512]{1,0:T(8,128)(2,1)}, bf16[256,512]{1,0:T(8,128)(2,1)S(1)}, u32[]{:S(2)}) %copy-start.1) | copy-done | bytes 262168
  20.4 0.1 copy-done.2
  20.5 8.6 %shard_map.95 = (bf16[256,4096]{1,0:T(8,128)(2,1)}, bf16[256,512]{1,0:T(8,128)(2,1)}, bf16[256,512]{1,0:T(8,128)(2,1)}) custom-call(s32[3]{0:T(128)} %and_convert_fusion.flags_ref, bf16[256,4096]{1,0:T(8,128)(2,1)} %q_ref.7, bf16[256,4096]{1,0:T(8,128)(2,1)} %do_ref.7, bf16[256,4096]{1,0:T(8,128)(2,1)} %o_ref.7, f32[32,256]{1,0:T(8,128)} %lse_ref.7, ...), custom_call_target="tpu_custom_call" | custom-call | tf_op jit(solution)/shard_map/pallas_call | solution.py:182
  29.1 8.5 %shard_map.96 = (f32[256,2048]{1,0:T(8,128)}, bf16[256,512]{1,0:T(8,128)(2,1)}, bf16[256,512]{1,0:T(8,128)(2,1)}) custom-call(s32[3]{0:T(128)} %and_convert_fusion.flags_ref, bf16[256,4096]{1,0:T(8,128)(2,1)} %q_ref.7, bf16[256,4096]{1,0:T(8,128)(2,1)} %do_ref.7, bf16[256,4096]{1,0:T(8,128)(2,1)} %o_ref.7, ...), custom_call_target="tpu_custom_call", output_to_operand_aliasing={{1}: (8, {}), {2}: (9, {})} | custom-call | tf_op jit(solution)/shard_map/pallas_call | solution.py:182
  37.6 3.4 %collective-permute-start.2 = (bf16[256,512]{1,0:T(8,128)(2,1)}, bf16[256,512]{1,0:T(8,128)(2,1)S(1)}, u32[]{:S(2)}, u32[]{:S(2)}) collective-permute-start(bf16[256,512]{1,0:T(8,128)(2,1)} %get-tuple-element.21), channel_id=1, source_target_pairs={{1,0},{2,1},{3,2},{4,3},{5,4},{6,5},{7,6},{8,7},{9,8},{10,9},{11,1... | collective-permute-start | bytes 786440 | tf_op jit(solution)/shard_map/ppermute | solution.py:20
  41.0 7.1 %collective-permute-start.3 = (bf16[256,512]{1,0:T(8,128)(2,1)}, bf16[256,512]{1,0:T(8,128)(2,1)S(1)}, u32[]{:S(2)}, u32[]{:S(2)}) collective-permute-start(bf16[256,512]{1,0:T(8,128)(2,1)} %get-tuple-element.22), channel_id=1, source_target_pairs={{2,0},{3,1},{4,2},{5,3},{6,4},{7,5},{8,6},{9,7},{10,8},{11,9},{12,... | collective-permute-start | bytes 786440 | tf_op jit(solution)/shard_map/ppermute | solution.py:20
  48.1 0.0 copy-start.3
  48.1 7.7 %shard_map.97 = (bf16[256,4096]{1,0:T(8,128)(2,1)}, f32[256,256]{1,0:T(8,128)}) custom-call(s32[3]{0:T(128)} %broadcast_3_flags_ref.2.flags_ref, bf16[256,4096]{1,0:T(8,128)(2,1)} %q_ref.7, bf16[256,4096]{1,0:T(8,128)(2,1)} %do_ref.7, bf16[256,4096]{1,0:T(8,128)(2,1)} %o_ref.7, f32[32,256]{1,0:T(8,128)} %lse_ref.7, ...), custom_call_target="tpu_custom_call", output_to_operand_aliasing={{0}: (8, {})} | custom-call | tf_op jit(solution)/shard_map/pallas_call | solution.py:182
  55.7 0.0 collective-permute-done.2
  55.8 3.9 %collective-permute-done.3 = bf16[256,512]{1,0:T(8,128)(2,1)S(1)} collective-permute-done((bf16[256,512]{1,0:T(8,128)(2,1)}, bf16[256,512]{1,0:T(8,128)(2,1)S(1)}, u32[]{:S(2)}, u32[]{:S(2)}) %collective-permute-start.3) | collective-permute-done | bytes 262176 | tf_op jit(solution)/shard_map/ppermute | solution.py:20
  59.7 0.0 copy-done.3
  59.7 1.0 %fusion.2 = (bf16[256,512]{1,0:T(8,128)(2,1)S(1)}, f32[256,512]{1,0:T(8,128)S(1)}) fusion(bf16[256,512]{1,0:T(8,128)(2,1)S(1)} %collective-permute-done.3, bf16[256,512]{1,0:T(8,128)(2,1)S(1)} %collective-permute-done.2, f32[256,256]{1,0:T(8,128)} %get-tuple-element.20, f32[256,256]{1,0:T(8,128)S(1)} %copy-done.3), kind=kLoop, calls=%fused_computation.17 | loop fusion | flops 786432 | bytes 1835008 | tf_op jit(solution)/shard_map/convert.3
  60.8 0.7 %pad_maximum_fusion.1 = bf16[256,256]{1,0:T(8,128)(2,1)} fusion(bf16[256,128]{1,0:T(8,128)(2,1)S(1)} %get-tuple-element.30, bf16[256,128]{1,0:T(8,128)(2,1)S(1)} %get-tuple-element.29), kind=kLoop, calls=%fused_computation.7 | loop fusion | flops 262144 | bytes 262144 | tf_op jit(solution)/shard_map/concatenate | solution.py:239
  61.4 0.7 %fusion.1 = bf16[256,256]{1,0:T(8,128)(2,1)} fusion(f32[256,128]{1,0:T(8,128)S(1)} %get-tuple-element.28, f32[256,128]{1,0:T(8,128)S(1)} %get-tuple-element.27), kind=kLoop, calls=%fused_computation.5 | loop fusion | flops 196608 | bytes 393216 | tf_op jit(solution)/shard_map/convert_element_type | solution.py:243
  (10 shorter events, 0.1 us)
Async XLA Ops:
  1.6 9.7 %copy-start = (bf16[256,512]{1,0:T(8,128)(2,1)}, bf16[256,512]{1,0:T(8,128)(2,1)S(1)}, u32[]{:S(2)}) copy-start(bf16[256,512]{1,0:T(8,128)(2,1)S(1)} %pad_maximum_fusion.rest_0_) | copy-start | bytes 786436
  1.6 18.0 %collective-permute-start.1 = (bf16[256,512]{1,0:T(8,128)(2,1)S(1)}, bf16[256,512]{1,0:T(8,128)(2,1)S(1)}, u32[]{:S(2)}, u32[]{:S(2)}) collective-permute-start(bf16[256,512]{1,0:T(8,128)(2,1)S(1)} %pad_maximum_fusion.rest_0_), channel_id=1, source_target_pairs={{0,1},{1,2},{2,3},{3,4},{4,5},{5,6},{6,7},{7,8},{8,9},{9,10},{10,1... | collective-permute-start | bytes 786440 | tf_op jit(solution)/shard_map/ppermute | solution.py:20
  3.6 16.1 %collective-permute-start = (bf16[256,512]{1,0:T(8,128)(2,1)S(1)}, bf16[256,512]{1,0:T(8,128)(2,1)S(1)}, u32[]{:S(2)}, u32[]{:S(2)}) collective-permute-start(bf16[256,512]{1,0:T(8,128)(2,1)S(1)} %pad_maximum_fusion.rest_0_), channel_id=1, source_target_pairs={{0,2},{1,3},{2,4},{3,5},{4,6},{5,7},{6,8},{7,9},{8,10},{9,11},{10,... | collective-permute-start | bytes 786440 | tf_op jit(solution)/shard_map/ppermute | solution.py:20
  19.7 0.7 %copy-start.1 = (bf16[256,512]{1,0:T(8,128)(2,1)}, bf16[256,512]{1,0:T(8,128)(2,1)S(1)}, u32[]{:S(2)}) copy-start(bf16[256,512]{1,0:T(8,128)(2,1)S(1)} %collective-permute-done.1.rest_1_) | copy-start | bytes 786436
  19.7 0.8 %copy-start.2 = (bf16[256,512]{1,0:T(8,128)(2,1)}, bf16[256,512]{1,0:T(8,128)(2,1)S(1)}, u32[]{:S(2)}) copy-start(bf16[256,512]{1,0:T(8,128)(2,1)S(1)} %collective-permute-done.rest_0_) | copy-start | bytes 786436
  37.6 18.1 %collective-permute-start.2 = (bf16[256,512]{1,0:T(8,128)(2,1)}, bf16[256,512]{1,0:T(8,128)(2,1)S(1)}, u32[]{:S(2)}, u32[]{:S(2)}) collective-permute-start(bf16[256,512]{1,0:T(8,128)(2,1)} %get-tuple-element.21), channel_id=1, source_target_pairs={{1,0},{2,1},{3,2},{4,3},{5,4},{6,5},{7,6},{8,7},{9,8},{10,9},{11,1... | collective-permute-start | bytes 786440 | tf_op jit(solution)/shard_map/ppermute | solution.py:20
  41.0 18.7 %collective-permute-start.3 = (bf16[256,512]{1,0:T(8,128)(2,1)}, bf16[256,512]{1,0:T(8,128)(2,1)S(1)}, u32[]{:S(2)}, u32[]{:S(2)}) collective-permute-start(bf16[256,512]{1,0:T(8,128)(2,1)} %get-tuple-element.22), channel_id=1, source_target_pairs={{2,0},{3,1},{4,2},{5,3},{6,4},{7,5},{8,6},{9,7},{10,8},{11,9},{12,... | collective-permute-start | bytes 786440 | tf_op jit(solution)/shard_map/ppermute | solution.py:20
  48.1 11.6 %copy-start.3 = (f32[256,256]{1,0:T(8,128)S(1)}, f32[256,256]{1,0:T(8,128)}, u32[]{:S(2)}) copy-start(f32[256,256]{1,0:T(8,128)} %get-tuple-element.19) | copy-start | bytes 786436
